TPU v7x, 512 devices: a whole 4x4x16 slice. The times are simulated.
512 devices in a mesh: guide: 2 (over core), seq: 64 (over x, z), tp: 4 (over y).
Axes of the slice: x: 4, y: 4, z: 16, core: 2. Of those that a mesh axis runs over, the one named last changes fastest.
Arguments:
- hidden: bfloat16 [2, 32, 2048], P('guide'), may hold values from -6 to 6
- attn_gain: float32 [2048], replicated, may hold values from 0.25 to 1.75
- final_gain: float32 [2048], replicated, may hold values from 0.25 to 1.75
- query_gain: float32 [64], replicated, may hold values from 0.5 to 6
- new_key_gain: float32 [64], replicated, may hold values from 0.5 to 3
- query_weight: bfloat16 [2048, 1280], P('seq', 'tp'), may hold values from -1 to 1
- key_value_weight: bfloat16 [2048, 640], P('seq'), may hold values from -0.125 to 0.125
- output_weight: bfloat16 [1280, 2048], P('tp'), may hold values from -0.15625 to 0.15625
- head_weight: bfloat16 [2048, 32000], P('seq', 'tp'), may hold values from -0.125 to 0.125
- page_cache: bfloat16 [2, 768, 128, 640], P('guide', 'seq'), may hold values from -12 to 12
- cache_length: int32 [2, 32], P('guide'), may hold values from 1 to 16384, as said below
- page_table: int32 [2, 32, 128], P('guide'), may hold values from -1 to 767, as said below
Outputs:
- guided: float32 [32, 32000], P('guide', 'tp')
Inputs may be any that keep to these rules, and one draw needn't show every extreme that they name: `cache_length`: in each group one request holds exactly 16384 tokens. page_table[g, i, p] is the slot of page_cache[g] (seq index times 12 plus local slot) that holds tokens p * 128 to p * 128 + 127 of request i, for p below ceil(cache_length[g, i] / 128); it is -1 beyond. A slot holds at most one page; many slots are empty.
All inputs are finite; a program needn't handle non-finite values.
Results may differ from a plain program's by a relative error of at most 0.0093.
Values sent between devices are 32-bit elements; how exact they have to be, the bound alone decides.
No kernel may reach another device: no remote copies, remote signals or barrier semaphores. Data moves between devices by JAX's collectives and lax.ppermute only.
A program may use at most 64 MiB of HBM per device.

v0:
```python
import jax
import jax.numpy as jnp
from jax import lax
from jax.sharding import PartitionSpec as P

QUERY_HEADS = 20
KEY_VALUE_HEADS = 5
HEAD_SIZE = 64


GUIDE_WEIGHT = 2.5
NORM_EPS = 1e-06
NEG_FILL = -1e30


def from_partner(value, axis, stride):
    mask = 2**stride
    pairs = [(source, source ^ mask) for source in range(lax.axis_size(axis))]
    return lax.ppermute(value, axis, pairs)


def norm_rows(token_rows, scale_gain):
    mean_square = jnp.mean(token_rows * token_rows, axis=-1, keepdims=True)
    return (token_rows * lax.rsqrt(mean_square + NORM_EPS) * scale_gain).astype(jnp.bfloat16)


def per_head_norm(vectors, head_gain):
    mean_square = jnp.mean(vectors * vectors, axis=-1, keepdims=True)
    return vectors * lax.rsqrt(mean_square + NORM_EPS) * head_gain


def rotate(vectors, positions):
    half_dim = vectors.shape[-1] // 2
    frequency = 10000.0 ** (-jnp.arange(half_dim).astype(jnp.float32) / half_dim)
    angles = positions.astype(jnp.float32)[:, None] * frequency[None, :]
    cosine = jnp.cos(angles)[:, None, :]
    sine_part = jnp.sin(angles)[:, None, :]
    first_half = vectors[..., :half_dim]
    second_half = vectors[..., half_dim:]
    return jnp.concatenate(
        [
            first_half * cosine - second_half * sine_part,
            second_half * cosine + first_half * sine_part,
        ],
        axis=-1,
    )


def shards(
    hidden,
    attn_gain,
    final_gain,
    query_gain,
    new_key_gain,
    query_weight,
    key_value_weight,
    output_weight,
    head_weight,
    page_cache,
    cache_length,
    page_table,
):
    token_rows = hidden[0].astype(jnp.float32)
    lengths = cache_length[0]
    page_map = page_table[0]
    nearby_cache = page_cache[0]
    request_number = token_rows.shape[0]
    half_rows = request_number // 2
    part_width = query_weight.shape[0]
    nearby_heads = query_weight.shape[1] // HEAD_SIZE
    scale = 1.0 / HEAD_SIZE**0.5
    shard_index = lax.axis_index("seq")
    normed = norm_rows(token_rows, attn_gain)
    normed_part = lax.dynamic_slice_in_dim(normed, shard_index * part_width, part_width, 1)
    query_sum, key_value_sum = lax.psum(
        (
            jnp.dot(normed_part, query_weight, preferred_element_type=jnp.float32),
            jnp.dot(normed_part, key_value_weight, preferred_element_type=jnp.float32),
        ),
        "seq",
    )
    head_mapping = (lax.axis_index("tp") * nearby_heads + jnp.arange(nearby_heads)) // (
        QUERY_HEADS // KEY_VALUE_HEADS
    )
    query_normed = per_head_norm(
        query_sum.reshape(request_number, nearby_heads, HEAD_SIZE), query_gain
    )
    normalized_key = per_head_norm(
        key_value_sum[:, : KEY_VALUE_HEADS * HEAD_SIZE].reshape(
            request_number, KEY_VALUE_HEADS, HEAD_SIZE
        ),
        new_key_gain,
    )
    query_rot = rotate(query_normed, lengths).astype(jnp.bfloat16)
    key_all = rotate(normalized_key, lengths)
    value_complete = key_value_sum[:, KEY_VALUE_HEADS * HEAD_SIZE :].reshape(
        request_number, KEY_VALUE_HEADS, HEAD_SIZE
    )
    key_new = jnp.take(key_all, head_mapping, axis=1).astype(jnp.bfloat16)
    fresh_value = jnp.take(value_complete, head_mapping, axis=1).astype(jnp.bfloat16)
    slot_number = nearby_cache.shape[0]
    page_token_count = nearby_cache.shape[1]
    global_slot = shard_index * slot_number + jnp.arange(slot_number)
    matches = page_map[:, :, None] == global_slot[None, None, :]
    owner_mask = jnp.any(matches, axis=1)
    page_number = jnp.sum(
        jnp.where(matches, jnp.arange(page_map.shape[1])[None, :, None], 0), axis=(0, 1)
    )
    owner_req = jnp.sum(jnp.where(owner_mask, jnp.arange(request_number)[:, None], 0), axis=0)
    slot_live = jnp.any(owner_mask, axis=0)
    owner_length = jnp.take(lengths, owner_req)
    positions = page_number[:, None] * page_token_count + jnp.arange(page_token_count)[None, :]
    is_valid = slot_live[:, None] & (positions < owner_length[:, None])
    key_tile = nearby_cache[:, :, : KEY_VALUE_HEADS * HEAD_SIZE].reshape(
        slot_number, page_token_count, KEY_VALUE_HEADS, HEAD_SIZE
    )
    value_tile = nearby_cache[:, :, KEY_VALUE_HEADS * HEAD_SIZE :].reshape(
        slot_number, page_token_count, KEY_VALUE_HEADS, HEAD_SIZE
    )
    key_heads = jnp.take(key_tile, head_mapping, axis=2)
    value_heads = jnp.take(value_tile, head_mapping, axis=2)
    slot_query = jnp.take(query_rot, owner_req, axis=0)
    scores = (
        jnp.einsum("shd,skhd->shk", slot_query, key_heads, preferred_element_type=jnp.float32)
        * scale
    )
    scores = jnp.where(is_valid[:, None, :], scores, NEG_FILL)
    slot_max = jnp.max(scores, axis=2)
    request_max = jnp.max(jnp.where(owner_mask[:, :, None], slot_max[None, :, :], NEG_FILL), axis=1)
    owner_max = jnp.take(request_max, owner_req, axis=0)
    weights = jnp.where(is_valid[:, None, :], jnp.exp(scores - owner_max[:, :, None]), 0.0).astype(
        jnp.bfloat16
    )
    slot_total = jnp.sum(weights.astype(jnp.float32), axis=2)
    slot_weighted = jnp.einsum(
        "shk,skhd->shd", weights, value_heads, preferred_element_type=jnp.float32
    )
    owner_float = owner_mask.astype(jnp.float32)
    request_total = jnp.dot(owner_float, slot_total, precision=lax.Precision.HIGHEST)
    request_weighted = jnp.einsum(
        "rs,shd->rhd", owner_float, slot_weighted, precision=lax.Precision.HIGHEST
    )
    merged_max = lax.pmax(request_max, "seq")
    rescale = jnp.exp(request_max - merged_max)
    merged_total, merged_weighted = lax.psum(
        (request_total * rescale, request_weighted * rescale[:, :, None]), "seq"
    )
    self_score = (
        jnp.sum(query_rot.astype(jnp.float32) * key_new.astype(jnp.float32), axis=2) * scale
    )
    row_max = jnp.maximum(merged_max, self_score)
    old_scale = jnp.exp(merged_max - row_max)
    self_weight = jnp.exp(self_score - row_max)
    denominator = merged_total * old_scale + self_weight
    weighted = merged_weighted * old_scale[:, :, None] + self_weight[
        :, :, None
    ] * fresh_value.astype(jnp.float32)
    attended = (
        (weighted / denominator[:, :, None])
        .astype(jnp.bfloat16)
        .reshape(request_number, nearby_heads * HEAD_SIZE)
    )
    output_part = jnp.dot(attended, output_weight, preferred_element_type=jnp.float32)
    output_sum = lax.psum(output_part, "tp")
    residual = token_rows + output_sum
    final_rows = norm_rows(residual, final_gain)
    final_part = lax.dynamic_slice_in_dim(final_rows, shard_index * part_width, part_width, 1)
    logit_part = jnp.dot(final_part, head_weight, preferred_element_type=jnp.float32)
    guide_index = lax.axis_index("guide")
    logits = lax.psum(logit_part, "seq")
    outgoing = lax.dynamic_slice_in_dim(logits, (1 - guide_index) * half_rows, half_rows, 0)
    paired = from_partner(outgoing, "guide", 0)
    own_rows = lax.dynamic_slice_in_dim(logits, guide_index * half_rows, half_rows, 0)
    conditional = jnp.where(guide_index == 0, own_rows, paired)
    unconditional = jnp.where(guide_index == 0, paired, own_rows)
    guided = unconditional + GUIDE_WEIGHT * (conditional - unconditional)
    return guided


def solution(mesh):
    in_specs = (
        P("guide", None, None),
        P(),
        P(),
        P(),
        P(),
        P("seq", "tp"),
        P("seq", None),
        P("tp", None),
        P("seq", "tp"),
        P("guide", "seq", None, None),
        P("guide", None),
        P("guide", None, None),
    )
    out_specs = P("guide", "tp")
    return jax.shard_map(shards, mesh=mesh, in_specs=in_specs, out_specs=out_specs, check_vma=False)
```

profile of v0, /device:TPU:6, one launch (start us, length us, event | category | flops | bytes accessed | tf_op | source)
XLA Modules:
  0.0 1082.3 jit_solution(4798824411742732155)
XLA Ops:
  6.5 1.0 bitcast_convert_fusion.1
  7.6 1.0 multiply_reduce_fusion.1
  8.6 0.8 dynamic-slice
  9.4 1.6 fusion.28
  12.2 1.8 compare_reduce_fusion
  14.0 1.7 fusion.4
  15.7 4.0 copy.37
  19.6 2.6 fusion.32
  23.0 1.9 gather_fusion.4
  25.5 1.6 fusion.26
  27.0 0.9 reshape.223
  27.9 260.2 %psum.42 = f32[32,5,64]{2,1,0:T(8,128)S(1)} all-reduce(f32[32,5,64]{2,1,0:T(8,128)S(1)} %reshape.223), channel_id=1, replica_groups=mesh['guide'=2,'seq'=64,'tp'=4] {'seq'}, use_global_device_ids=true, to_apply=%region_5.6 | all-reduce | flops 10240 | bytes 81920 | tf_op jit(solution)/shard_map/psum | solution.py:75
  288.8 1.4 multiply_cosine_fusion
  291.6 1.2 broadcast_select_fusion.1
  292.8 2.2 select_bitcast_fusion.1
  295.0 0.8 subtract_convert_fusion
  295.9 0.8 slice.50
  297.6 0.8 multiply_subtract_fusion
  299.2 1.1 multiply_reduce_fusion.2
  302.2 138.9 %pmax.7 = f32[32,5]{0,1:T(8,128)S(1)} all-reduce(f32[32,5]{0,1:T(8,128)S(1)} %select_reduce_fusion), channel_id=1, replica_groups=mesh['guide'=2,'seq'=64,'tp'=4] {'seq'}, use_global_device_ids=true, to_apply=%region_9.11 | all-reduce | flops 160 | bytes 1280 | tf_op jit(solution)/shard_map/pmax | solution.py:143
  443.6 0.9 slice.53
  445.2 275.0 %all-reduce = (f32[32,5,64]{2,0,1:T(8,128)S(1)}, f32[32,5]{0,1:T(8,128)S(1)}) all-reduce(f32[32,5,64]{2,0,1:T(8,128)S(1)} %convolution_multiply_fusion, f32[32,5]{0,1:T(8,128)S(1)} %convolution_multiply_fusion.1), channel_id=1, replica_groups=mesh['guide'=2,'seq'=64,'tp'=4] {'seq'}, use_global_device_ids=true, to_apply=%region_10.12 | all-reduce | flops 10400 | bytes 83200 | tf_op jit(solution)/shard_map/psum | solution.py:145
  720.5 1.0 fusion.33
  721.7 0.8 dynamic-slice.1
  722.4 70.6 %all-reduce.7.cloned.1.call-done = f32[32,2048]{1,0:T(8,128)} async-done(((f32[32,2048]{1,0:T(8,128)}), f32[32,2048]{1,0:T(8,128)}) %all-reduce.7.cloned.1.call-update) | async-done | bytes 262160 | tf_op jit(solution)/shard_map/psum | solution.py:164
  793.1 1.1 multiply_reduce_fusion
  794.2 1.4 fusion.15
  795.6 273.4 %all-reduce.9.cloned.1.call-done = f32[32,8000]{1,0:T(8,128)} async-done(((f32[32,8000]{1,0:T(8,128)}), f32[32,8000]{1,0:T(8,128)}) %all-reduce.9.cloned.1.call-update) | async-done | bytes 1024016 | tf_op jit(solution)/shard_map/psum | solution.py:170
  1069.0 1.1 constant_dynamic-slice_fusion
  1070.0 1.9 collective-permute-start
  1072.0 1.9 collective-permute-done
  1073.8 1.9 multiply_add_fusion
  (77 shorter events, 11.7 us)
Async XLA Ops:
  6.5 714.0 %copy-start = (bf16[320,2048]{1,0:T(8,128)(2,1)S(1)}, bf16[320,2048]{1,0:T(8,128)(2,1)}, u32[]{:S(2)}) copy-start(bf16[320,2048]{1,0:T(8,128)(2,1)} %param.23) | copy-start | bytes 3932164
  6.5 289.3 %all-reduce.5.cloned.1.call-start = ((), (), s32[]{:S(2)}) async-start(), calls=%async_computation | async-start | bytes 163840 | tf_op jit(solution)/shard_map/psum | solution.py:75
  9.4 2.8 copy-start.9
  11.0 782.0 %all-reduce.7.cloned.1.call-start = ((), (), s32[]{:S(2)}) async-start(), calls=%async_computation.1 | async-start | bytes 524288 | tf_op jit(solution)/shard_map/psum | solution.py:164
  23.0 2.0 copy-start.1
  288.3 0.5 copy-start.11
  292.8 2.2 copy-start.6
  292.8 2.2 copy-start.7
  292.8 3.0 copy-start.10
  295.0 6.5 copy-start.4
  295.0 147.6 %copy-start.3 = (bf16[12,128,5,64]{1,3,0,2:T(8,128)(2,1)S(1)}, bf16[12,128,5,64]{1,3,0,2:T(8,128)(2,1)}, u32[]{:S(2)}) copy-start(bf16[12,128,5,64]{1,3,0,2:T(8,128)(2,1)} %get-tuple-element.31) | copy-start | bytes 2949124
  298.5 421.8 %copy-start.8 = (pred[5]{0:T(512)(128)(4,1)S(1)}, pred[5]{0:T(512)(128)(4,1)}, u32[]{:S(2)}) copy-start(pred[5]{0:T(512)(128)(4,1)} %compare_and_fusion) | copy-start | bytes 19
  442.6 350.5 %copy-start.2 = (bf16[1,32,2048]{2,1,0:T(8,128)(2,1)S(1)}, bf16[1,32,2048]{2,1,0:T(8,128)(2,1)}, u32[]{:S(2)}) copy-start(bf16[1,32,2048]{2,1,0:T(8,128)(2,1)} %param.16) | copy-start | bytes 393220
  443.2 351.0 %copy-start.5 = (bf16[32,8000]{1,0:T(8,128)(2,1)S(1)}, bf16[32,8000]{1,0:T(8,128)(2,1)}, u32[]{:S(2)}) copy-start(bf16[32,8000]{1,0:T(8,128)(2,1)} %param.24) | copy-start | bytes 1536004
  721.6 347.3 %all-reduce.9.cloned.1.call-start = ((), (), s32[]{:S(2)}) async-start(), calls=%async_computation.2 | async-start | bytes 2064384 | tf_op jit(solution)/shard_map/psum | solution.py:170
  1070.0 3.8 collective-permute-start
Sparse Core Ops, SparseCore 0:
  11.2 263.0 all-reduce.4
  721.7 71.2 all-reduce.6
  796.8 272.0 all-reduce.8
where the time goes:
time: 1090 us; the launch traced here: 1080 us
  blocking collectives  674 us (62%)
  waiting for transfers between devices  346 us (32%)
  other arithmetic  21.5 us (2%)
  local copies, waits for them, and re-layouts  18.4 us (2%)
  between operations  13.4 us (1%)
    psum x1, blocking collectives, shards(): lax.psum((request_total * rescale, request_weighted * rescale[:, :, None]...  275 us
    psum x1, waiting for transfers between devices, shards(): logits = lax.psum(logit_part, 'seq')  273 us
    psum x1, blocking collectives, shards(): lax.psum((jnp.dot(normed_part, query_weight, preferred_element_type=jnp.f...  260 us
    pmax x1, blocking collectives, shards(): merged_max = lax.pmax(request_max, 'seq')  139 us
    psum x1, waiting for transfers between devices, shards(): output_sum = lax.psum(output_part, 'tp')  70.6 us
  transfers between devices with their start and end apart: 4, of which 3 were waited for; matrix products, arithmetic and copies ran while one was open for 2% of the time, Pallas kernels for 0%

commit v1 on v0

--- a/solution.py
+++ b/solution.py
@@ -44,6 +44,51 @@
         ],
         axis=-1,
     )
+
+
+def all_reduce(value, axis):
+    count = lax.axis_size(axis)
+    flat = value.reshape(-1)
+    chunk = -(-flat.size // count)
+    chunk = -(-chunk // 128) * 128
+    flat = jnp.pad(flat, (0, count * chunk - flat.size))
+    parts = lax.all_to_all(flat.reshape(count, chunk), axis, 0, 0, tiled=True)
+    total = jnp.sum(parts, axis=0, keepdims=True)
+    whole = lax.all_to_all(jnp.broadcast_to(total, (count, chunk)), axis, 0, 0, tiled=True)
+    return whole.reshape(-1)[: value.size].reshape(value.shape)
+
+
+def spread_units(units, count, fill):
+    per = -(-units.shape[0] // count)
+    padding = [(0, count * per - units.shape[0])] + [(0, 0)] * (units.ndim - 1)
+    return jnp.pad(units, padding, constant_values=fill).reshape((count, per) + units.shape[1:])
+
+
+def merge_attention(local_max, local_total, local_weighted, self_score, fresh_value, axis):
+    count = lax.axis_size(axis)
+    me = lax.axis_index(axis)
+    unit_count = local_max.shape[0]
+    stats = jnp.concatenate([local_max[:, None], local_total[:, None], local_weighted], axis=1)
+    spread = spread_units(stats, count, 0.0)
+    spread = spread.at[:, :, 0].set(spread_units(local_max, count, NEG_FILL))
+    parts = lax.all_to_all(spread, axis, 0, 0, tiled=True)
+    part_max = parts[:, :, 0]
+    merged_max = jnp.max(part_max, axis=0)
+    rescale = jnp.exp(part_max - merged_max[None, :])
+    merged_total = jnp.sum(rescale * parts[:, :, 1], axis=0)
+    merged_weighted = jnp.sum(rescale[:, :, None] * parts[:, :, 2:], axis=0)
+    own_score = lax.dynamic_index_in_dim(spread_units(self_score, count, 0.0), me, 0, keepdims=False)
+    own_value = lax.dynamic_index_in_dim(spread_units(fresh_value, count, 0.0), me, 0, keepdims=False)
+    row_max = jnp.maximum(merged_max, own_score)
+    old_scale = jnp.exp(merged_max - row_max)
+    self_weight = jnp.exp(own_score - row_max)
+    denominator = merged_total * old_scale + self_weight
+    weighted = merged_weighted * old_scale[:, None] + self_weight[:, None] * own_value
+    fraction = jnp.concatenate([weighted, denominator[:, None]], axis=1)
+    gathered = lax.all_to_all(
+        jnp.broadcast_to(fraction[None], (count,) + fraction.shape), axis, 0, 0, tiled=True
+    ).reshape(-1, fraction.shape[-1])[:unit_count]
+    return (gathered[:, :-1] / gathered[:, -1:]).astype(jnp.bfloat16)
 
 
 def shards(
@@ -68,17 +113,23 @@
     half_rows = request_number // 2
     part_width = query_weight.shape[0]
     nearby_heads = query_weight.shape[1] // HEAD_SIZE
+    query_width = query_weight.shape[1]
     scale = 1.0 / HEAD_SIZE**0.5
     shard_index = lax.axis_index("seq")
     normed = norm_rows(token_rows, attn_gain)
     normed_part = lax.dynamic_slice_in_dim(normed, shard_index * part_width, part_width, 1)
-    query_sum, key_value_sum = lax.psum(
-        (
-            jnp.dot(normed_part, query_weight, preferred_element_type=jnp.float32),
-            jnp.dot(normed_part, key_value_weight, preferred_element_type=jnp.float32),
+    projected = all_reduce(
+        jnp.concatenate(
+            [
+                jnp.dot(normed_part, query_weight, preferred_element_type=jnp.float32),
+                jnp.dot(normed_part, key_value_weight, preferred_element_type=jnp.float32),
+            ],
+            axis=1,
         ),
         "seq",
     )
+    query_sum = projected[:, :query_width]
+    key_value_sum = projected[:, query_width:]
     head_mapping = (lax.axis_index("tp") * nearby_heads + jnp.arange(nearby_heads)) // (
         QUERY_HEADS // KEY_VALUE_HEADS
     )
@@ -140,41 +191,40 @@
     request_weighted = jnp.einsum(
         "rs,shd->rhd", owner_float, slot_weighted, precision=lax.Precision.HIGHEST
     )
-    merged_max = lax.pmax(request_max, "seq")
-    rescale = jnp.exp(request_max - merged_max)
-    merged_total, merged_weighted = lax.psum(
-        (request_total * rescale, request_weighted * rescale[:, :, None]), "seq"
-    )
     self_score = (
         jnp.sum(query_rot.astype(jnp.float32) * key_new.astype(jnp.float32), axis=2) * scale
     )
-    row_max = jnp.maximum(merged_max, self_score)
-    old_scale = jnp.exp(merged_max - row_max)
-    self_weight = jnp.exp(self_score - row_max)
-    denominator = merged_total * old_scale + self_weight
-    weighted = merged_weighted * old_scale[:, :, None] + self_weight[
-        :, :, None
-    ] * fresh_value.astype(jnp.float32)
-    attended = (
-        (weighted / denominator[:, :, None])
-        .astype(jnp.bfloat16)
-        .reshape(request_number, nearby_heads * HEAD_SIZE)
-    )
+    unit_count = request_number * nearby_heads
+    attended = merge_attention(
+        request_max.reshape(unit_count),
+        request_total.reshape(unit_count),
+        request_weighted.reshape(unit_count, HEAD_SIZE),
+        self_score.reshape(unit_count),
+        fresh_value.astype(jnp.float32).reshape(unit_count, HEAD_SIZE),
+        "seq",
+    ).reshape(request_number, nearby_heads * HEAD_SIZE)
     output_part = jnp.dot(attended, output_weight, preferred_element_type=jnp.float32)
     output_sum = lax.psum(output_part, "tp")
     residual = token_rows + output_sum
-    final_rows = norm_rows(residual, final_gain)
-    final_part = lax.dynamic_slice_in_dim(final_rows, shard_index * part_width, part_width, 1)
-    logit_part = jnp.dot(final_part, head_weight, preferred_element_type=jnp.float32)
+    mean_square = jnp.mean(residual * residual, axis=-1, keepdims=True)
+    row_scale = lax.rsqrt(mean_square + NORM_EPS)
+    gain_part = lax.dynamic_slice_in_dim(final_gain, shard_index * part_width, part_width, 0)
+    residual_part = lax.dynamic_slice_in_dim(residual, shard_index * part_width, part_width, 1)
+    scaled_part = jnp.concatenate([residual_part, row_scale], axis=1)
     guide_index = lax.axis_index("guide")
-    logits = lax.psum(logit_part, "seq")
-    outgoing = lax.dynamic_slice_in_dim(logits, (1 - guide_index) * half_rows, half_rows, 0)
-    paired = from_partner(outgoing, "guide", 0)
-    own_rows = lax.dynamic_slice_in_dim(logits, guide_index * half_rows, half_rows, 0)
+    outgoing = lax.dynamic_slice_in_dim(scaled_part, (1 - guide_index) * half_rows, half_rows, 0)
+    incoming = from_partner(outgoing, "guide", 0)
+    own = lax.dynamic_slice_in_dim(scaled_part, guide_index * half_rows, half_rows, 0)
+    paired = (incoming[:, :-1] * incoming[:, -1:] * gain_part).astype(jnp.bfloat16)
+    own_rows = (own[:, :-1] * own[:, -1:] * gain_part).astype(jnp.bfloat16)
     conditional = jnp.where(guide_index == 0, own_rows, paired)
     unconditional = jnp.where(guide_index == 0, paired, own_rows)
-    guided = unconditional + GUIDE_WEIGHT * (conditional - unconditional)
-    return guided
+    both = jnp.concatenate([conditional, unconditional], axis=0)
+    logit_part = jnp.dot(both, head_weight, preferred_element_type=jnp.float32)
+    conditional_part = logit_part[:half_rows]
+    unconditional_part = logit_part[half_rows:]
+    guided_part = unconditional_part + GUIDE_WEIGHT * (conditional_part - unconditional_part)
+    return all_reduce(guided_part, "seq")
 
 
 def solution(mesh):

time: 1090 us -> 282 us (0.26)
  blocking collectives: 674 us -> 104 us
  waiting for transfers between devices: 346 us -> 75.6 us
  starting transfers between devices: 2.01 us -> 40.3 us
    psum x2 -> x0, blocking collectives: 535 us -> none  [the longest x1 275 us: shards(): lax.psum((request_total * rescale, request_weighted * rescale[:, :, None]...]
    psum x2 -> x0, waiting for transfers between devices: 273 us -> none  [the longest x1 273 us: shards(): logits = lax.psum(logit_part, 'seq')]
    pmax x1 -> x0, blocking collectives: 139 us -> none  [shards(): merged_max = lax.pmax(request_max, 'seq')]
    all_to_all x0 -> x3, blocking collectives: none -> 104 us  [the longest x1 47.7 us: all_reduce(): parts = lax.all_to_all(flat.reshape(count, chunk), axis, 0, 0, tiled=True)]
    all_to_all x0 -> x3, starting transfers between devices: none -> 38.3 us  [the longest x1 18.8 us: all_reduce(): parts = lax.all_to_all(flat.reshape(count, chunk), axis, 0, 0, tiled=True)]
    all_to_all x0 -> x3, waiting for transfers between devices: none -> 26.3 us  [the longest x1 12.7 us: all_reduce(): lax.all_to_all(jnp.broadcast_to(total, (count, chunk)), axis, 0, 0, tiled...]
    psum x1, waiting for transfers between devices: 70.6 us -> 48.4 us  [shards(): output_sum = lax.psum(output_part, 'tp')]
  transfers between devices with their start and end apart: 4 -> 5, of which waited for: 3 -> 5; matrix products, arithmetic and copies ran while one was open for 2% -> 6% of each run, Pallas kernels for 0% -> 0%
where the time goes in v1:
time: 282 us; the launch traced here: 281 us
  blocking collectives  104 us (37%)
  waiting for transfers between devices  75.6 us (27%)
  starting transfers between devices  40.3 us (14%)
  local copies, waits for them, and re-layouts  24.6 us (9%)
  other arithmetic  17.8 us (6%)
  between operations  14.1 us (5%)
  matrix products  4.63 us (2%)
    psum x1, waiting for transfers between devices, shards(): output_sum = lax.psum(output_part, 'tp')  48.4 us
    all_to_all x1, blocking collectives, all_reduce(): parts = lax.all_to_all(flat.reshape(count, chunk), axis, 0, 0, tiled=True)  47.7 us
    all_to_all x1, blocking collectives, all_reduce(): lax.all_to_all(jnp.broadcast_to(total, (count, chunk)), axis, 0, 0, tiled...  37.2 us
    all_to_all x1, blocking collectives, merge_attention(): lax.all_to_all(jnp.broadcast_to(fraction[None], (count,) + fraction.shape...  19.1 us
    all_to_all x1, starting transfers between devices, all_reduce(): parts = lax.all_to_all(flat.reshape(count, chunk), axis, 0, 0, tiled=True)  18.8 us
    all_to_all x1, starting transfers between devices, all_reduce(): lax.all_to_all(jnp.broadcast_to(total, (count, chunk)), axis, 0, 0, tiled...  13 us
    all_to_all x1, waiting for transfers between devices, all_reduce(): lax.all_to_all(jnp.broadcast_to(total, (count, chunk)), axis, 0, 0, tiled...  12.7 us
    all_to_all x1, waiting for transfers between devices, merge_attention(): parts = lax.all_to_all(spread, axis, 0, 0, tiled=True)  11.5 us
  transfers between devices with their start and end apart: 5, of which 5 were waited for; matrix products, arithmetic and copies ran while one was open for 6% of the time, Pallas kernels for 0%

profile of v1, /device:TPU:6, one launch (start us, length us, event | category | flops | bytes accessed | tf_op | source)
XLA Modules:
  0.0 281.0 jit_solution(5311557495256595641)
XLA Ops:
  6.5 1.0 bitcast_convert_fusion.1
  7.6 1.0 multiply_reduce_fusion.1
  9.4 1.0 fusion.47
  10.4 0.9 fusion.45
  12.2 18.8 %all-to-all-start = ((f32[64,1,512]{2,1,0:T(1,128)}), f32[64,1,512]{2,1,0:T(1,128)S(1)}, u32[]{:S(2)}, u32[]{:S(2)}) async-start(f32[64,1,512]{2,1,0:T(1,128)} %bitcast.6), calls=%async_computation | async-start | bytes 262144 | tf_op jit(solution)/shard_map/all_to_all | solution.py:55
  31.0 1.3 compare_reduce_fusion
  32.3 1.1 fusion.6
  33.4 4.0 %copy.129 = bf16[1,12,128,640]{2,3,1,0:T(8,128)(2,1)} copy(bf16[1,12,128,640]{3,2,1,0:T(8,128)(2,1)} %param.27) | data formatting | bytes 3932160 | tf_op args[9]
  37.4 2.6 fusion.49
  40.8 1.9 gather_fusion.4
  44.3 2.1 all-to-all-done
  47.3 13.0 %all-to-all-start.1 = ((f32[64,1,512]{2,1,0:T(1,128)}), f32[64,1,512]{2,1,0:T(1,128)S(1)}, u32[]{:S(2)}, u32[]{:S(2)}) async-start(f32[64,1,512]{2,1,0:T(1,128)} %broadcast_in_dim.161), calls=%async_computation.1 | async-start | bytes 262144 | tf_op jit(solution)/shard_map/all_to_all | solution.py:57
  61.0 1.5 select_bitcast_fusion.1
  62.5 12.7 %all-to-all-done.1 = f32[64,1,512]{2,1,0:T(1,128)S(1)} async-done(((f32[64,1,512]{2,1,0:T(1,128)}), f32[64,1,512]{2,1,0:T(1,128)S(1)}, u32[]{:S(2)}, u32[]{:S(2)}) %all-to-all-start.1) | async-done | bytes 131104 | tf_op jit(solution)/shard_map/all_to_all | solution.py:57
  76.8 1.2 gather_fusion.5
  78.0 0.9 reshape.399
  79.8 0.8 subtract_convert_fusion
  80.6 1.0 multiply_reduce_fusion.2
  88.4 0.8 reshape.499
  89.2 6.5 %all-to-all-start.2 = ((f32[64,1,198]{2,1,0:T(1,128)}), f32[64,1,198]{2,1,0:T(1,128)S(1)}, u32[]{:S(2)}, u32[]{:S(2)}) async-start(f32[64,1,198]{2,1,0:T(1,128)} %reshape.499), calls=%async_computation.2 | async-start | bytes 131072 | tf_op jit(solution)/shard_map/all_to_all | solution.py:74
  97.1 11.5 %all-to-all-done.2 = f32[64,1,198]{2,1,0:T(1,128)S(1)} async-done(((f32[64,1,198]{2,1,0:T(1,128)}), f32[64,1,198]{2,1,0:T(1,128)S(1)}, u32[]{:S(2)}, u32[]{:S(2)}) %all-to-all-start.2) | async-done | bytes 50720 | tf_op jit(solution)/shard_map/all_to_all | solution.py:74
  109.1 0.8 reduce.14
  111.6 19.1 %all_to_all.40 = f32[64,1,195]{2,1,0:T(1,128)S(1)} all-to-all(f32[64,1,195]{2,1,0:T(1,128)S(1)} %reshape.501), channel_id=1, replica_groups=mesh['guide'=2,'seq'=64,'tp'=4] {'seq'}, dimensions={0} | all-to-all | bytes 99840 | tf_op jit(solution)/shard_map/all_to_all | solution.py:88
  130.7 0.8 reduce.15
  132.1 1.0 fusion.52
  133.9 48.4 %all-reduce.8.cloned.1.call-done = f32[32,2048]{1,0:T(8,128)} async-done(((f32[32,2048]{1,0:T(8,128)}), f32[32,2048]{1,0:T(8,128)}) %all-reduce.8.cloned.1.call-update) | async-done | bytes 262160 | tf_op jit(solution)/shard_map/psum | solution.py:207
  182.3 1.1 multiply_reduce_fusion
  183.6 1.9 collective-permute-start
  185.8 1.0 collective-permute-done
  187.6 47.7 %all_to_all.41 = f32[64,1,2048]{2,1,0:T(1,128)S(1)} all-to-all(f32[64,1,2048]{2,1,0:T(1,128)S(1)} %bitcast.90), channel_id=1, replica_groups=mesh['guide'=2,'seq'=64,'tp'=4] {'seq'}, dimensions={0} | all-to-all | bytes 1048576 | tf_op jit(solution)/shard_map/all_to_all | solution.py:55
  235.9 37.2 %all_to_all.42 = f32[64,1,2048]{2,1,0:T(1,128)S(1)} all-to-all(f32[64,1,2048]{2,1,0:T(1,128)S(1)} %broadcast_in_dim.170), channel_id=1, replica_groups=mesh['guide'=2,'seq'=64,'tp'=4] {'seq'}, dimensions={0} | all-to-all | bytes 1048576 | tf_op jit(solution)/shard_map/all_to_all | solution.py:57
  273.2 1.0 reshape.416
  (141 shorter events, 21.3 us)
Async XLA Ops:
  6.5 125.5 %copy-start = (bf16[320,2048]{1,0:T(8,128)(2,1)S(1)}, bf16[320,2048]{1,0:T(8,128)(2,1)}, u32[]{:S(2)}) copy-start(bf16[320,2048]{1,0:T(8,128)(2,1)} %param.25) | copy-start | bytes 3932164
  12.2 34.3 %all-to-all-start = ((f32[64,1,512]{2,1,0:T(1,128)}), f32[64,1,512]{2,1,0:T(1,128)S(1)}, u32[]{:S(2)}, u32[]{:S(2)}) async-start(f32[64,1,512]{2,1,0:T(1,128)} %bitcast.6), calls=%async_computation | async-start | bytes 262144 | tf_op jit(solution)/shard_map/all_to_all | solution.py:55
  31.0 30.0 %copy-start.12 = (pred[5]{0:T(512)(128)(4,1)}, pred[5]{0:T(512)(128)(4,1)S(1)}, u32[]{:S(2)}) copy-start(pred[5]{0:T(512)(128)(4,1)S(1)} %compare_and_fusion) | copy-start | bytes 19
  32.3 10.4 %copy-start.7 = (pred[32,12]{0,1:T(8,128)(4,1)}, pred[32,12]{0,1:T(8,128)(4,1)S(1)}, u32[]{:S(2)}) copy-start(pred[32,12]{0,1:T(8,128)(4,1)S(1)} %get-tuple-element.20) | copy-start | bytes 1156
  40.0 36.8 %copy-start.10 = (s32[1024]{0:T(1024)}, s32[1024]{0:T(1024)S(1)}, u32[]{:S(2)}) copy-start(s32[1024]{0:T(1024)S(1)} %pad_clamp_fusion) | copy-start | bytes 12292
  40.8 2.0 copy-start.1
  42.9 0.7 copy-start.11
  44.3 32.3 %copy-start.6 = (f32[32,32]{1,0:T(8,128)}, f32[32,32]{1,0:T(8,128)S(1)}, u32[]{:S(2)}) copy-start(f32[32,32]{1,0:T(8,128)S(1)} %get-tuple-element.47) | copy-start | bytes 12292
  47.3 27.9 %all-to-all-start.1 = ((f32[64,1,512]{2,1,0:T(1,128)}), f32[64,1,512]{2,1,0:T(1,128)S(1)}, u32[]{:S(2)}, u32[]{:S(2)}) async-start(f32[64,1,512]{2,1,0:T(1,128)} %broadcast_in_dim.161), calls=%async_computation.1 | async-start | bytes 262144 | tf_op jit(solution)/shard_map/all_to_all | solution.py:57
  61.0 15.5 %copy-start.15 = (f32[64]{0:T(128)S(1)}, f32[64]{0:T(128)}, u32[]{:S(2)}) copy-start(f32[64]{0:T(128)} %param.22) | copy-start | bytes 772
  62.5 20.5 %copy-start.4 = (bf16[12,128,5,64]{1,3,0,2:T(8,128)(2,1)S(1)}, bf16[12,128,5,64]{1,3,0,2:T(8,128)(2,1)}, u32[]{:S(2)}) copy-start(bf16[12,128,5,64]{1,3,0,2:T(8,128)(2,1)} %get-tuple-element.48) | copy-start | bytes 2949124
  76.6 9.7 %copy-start.3 = (bf16[12,128,5,64]{1,3,0,2:T(8,128)(2,1)S(1)}, bf16[12,128,5,64]{1,3,0,2:T(8,128)(2,1)}, u32[]{:S(2)}) copy-start(bf16[12,128,5,64]{1,3,0,2:T(8,128)(2,1)} %get-tuple-element.49) | copy-start | bytes 2949124
  79.8 6.2 %copy-start.14 = (pred[12]{0:T(512)(128)(4,1)S(1)}, pred[12]{0:T(512)(128)(4,1)}, u32[]{:S(2)}) copy-start(pred[12]{0:T(512)(128)(4,1)} %get-tuple-element.26) | copy-start | bytes 40
  79.8 6.3 %copy-start.9 = (pred[12,128]{1,0:T(8,128)(4,1)S(1)}, pred[12,128]{1,0:T(8,128)(4,1)}, u32[]{:S(2)}) copy-start(pred[12,128]{1,0:T(8,128)(4,1)} %fusion.28) | copy-start | bytes 4612
  79.8 7.1 %copy-start.8 = (pred[32,12]{0,1:T(8,128)(4,1)S(1)}, pred[32,12]{0,1:T(8,128)(4,1)}, u32[]{:S(2)}) copy-start(pred[32,12]{0,1:T(8,128)(4,1)} %copy-done.7) | copy-start | bytes 1156
  83.4 13.2 %copy-start.13 = (pred[5]{0:T(512)(128)(4,1)S(1)}, pred[5]{0:T(512)(128)(4,1)}, u32[]{:S(2)}) copy-start(pred[5]{0:T(512)(128)(4,1)} %copy-done.12) | copy-start | bytes 19
  89.2 19.4 %all-to-all-start.2 = ((f32[64,1,198]{2,1,0:T(1,128)}), f32[64,1,198]{2,1,0:T(1,128)S(1)}, u32[]{:S(2)}, u32[]{:S(2)}) async-start(f32[64,1,198]{2,1,0:T(1,128)} %reshape.499), calls=%async_computation.2 | async-start | bytes 131072 | tf_op jit(solution)/shard_map/all_to_all | solution.py:74
  95.8 86.5 %all-reduce.8.cloned.1.call-start = ((), (), s32[]{:S(2)}) async-start(), calls=%async_computation.6 | async-start | bytes 524288 | tf_op jit(solution)/shard_map/psum | solution.py:207
  110.2 72.1 %copy-start.2 = (bf16[1,32,2048]{2,1,0:T(8,128)(2,1)S(1)}, bf16[1,32,2048]{2,1,0:T(8,128)(2,1)}, u32[]{:S(2)}) copy-start(bf16[1,32,2048]{2,1,0:T(8,128)(2,1)} %param.18) | copy-start | bytes 393220
  111.4 75.5 %copy-start.5 = (bf16[32,8000]{1,0:T(8,128)(2,1)S(1)}, bf16[32,8000]{1,0:T(8,128)(2,1)}, u32[]{:S(2)}) copy-start(bf16[32,8000]{1,0:T(8,128)(2,1)} %param.26) | copy-start | bytes 1536004
  183.6 3.1 %collective-permute-start = (f32[16,33]{1,0:T(8,128)S(1)}, f32[16,33]{1,0:T(8,128)S(1)}, u32[]{:S(2)}, u32[]{:S(2)}) collective-permute-start(f32[16,33]{1,0:T(8,128)S(1)} %get-tuple-element.42), channel_id=1, source_target_pairs={{0,256},{256,0},{1,257},{257,1},{2,258},{258,2},{3,259},{259,3},{4... | collective-permute-start | bytes 6344 | tf_op jit(solution)/shard_map/ppermute | solution.py:19
Sparse Core Ops, SparseCore 0:
  133.3 48.9 all-reduce.7

commit v2 on v1

--- a/solution.py
+++ b/solution.py
@@ -11,12 +11,6 @@
 GUIDE_WEIGHT = 2.5
 NORM_EPS = 1e-06
 NEG_FILL = -1e30
-
-
-def from_partner(value, axis, stride):
-    mask = 2**stride
-    pairs = [(source, source ^ mask) for source in range(lax.axis_size(axis))]
-    return lax.ppermute(value, axis, pairs)
 
 
 def norm_rows(token_rows, scale_gain):
@@ -204,22 +198,18 @@
         "seq",
     ).reshape(request_number, nearby_heads * HEAD_SIZE)
     output_part = jnp.dot(attended, output_weight, preferred_element_type=jnp.float32)
-    output_sum = lax.psum(output_part, "tp")
-    residual = token_rows + output_sum
-    mean_square = jnp.mean(residual * residual, axis=-1, keepdims=True)
-    row_scale = lax.rsqrt(mean_square + NORM_EPS)
-    gain_part = lax.dynamic_slice_in_dim(final_gain, shard_index * part_width, part_width, 0)
-    residual_part = lax.dynamic_slice_in_dim(residual, shard_index * part_width, part_width, 1)
-    scaled_part = jnp.concatenate([residual_part, row_scale], axis=1)
-    guide_index = lax.axis_index("guide")
-    outgoing = lax.dynamic_slice_in_dim(scaled_part, (1 - guide_index) * half_rows, half_rows, 0)
-    incoming = from_partner(outgoing, "guide", 0)
-    own = lax.dynamic_slice_in_dim(scaled_part, guide_index * half_rows, half_rows, 0)
-    paired = (incoming[:, :-1] * incoming[:, -1:] * gain_part).astype(jnp.bfloat16)
-    own_rows = (own[:, :-1] * own[:, -1:] * gain_part).astype(jnp.bfloat16)
-    conditional = jnp.where(guide_index == 0, own_rows, paired)
-    unconditional = jnp.where(guide_index == 0, paired, own_rows)
-    both = jnp.concatenate([conditional, unconditional], axis=0)
+    output_part = output_part + jnp.where(lax.axis_index("tp") == 0, token_rows, 0.0)
+    guide_count = lax.axis_size("guide")
+    tp_count = lax.axis_size("tp")
+    outgoing = jnp.broadcast_to(
+        output_part.reshape(guide_count, 1, half_rows, -1),
+        (guide_count, tp_count, half_rows, output_part.shape[1]),
+    ).reshape(guide_count * tp_count, half_rows, -1)
+    incoming = lax.all_to_all(outgoing, ("guide", "tp"), 0, 0, tiled=True)
+    residual = jnp.sum(incoming.reshape(guide_count, tp_count, half_rows, -1), axis=1)
+    final_rows = norm_rows(residual, final_gain)
+    final_part = lax.dynamic_slice_in_dim(final_rows, shard_index * part_width, part_width, 2)
+    both = final_part.reshape(guide_count * half_rows, part_width)
     logit_part = jnp.dot(both, head_weight, preferred_element_type=jnp.float32)
     conditional_part = logit_part[:half_rows]
     unconditional_part = logit_part[half_rows:]

time: 282 us -> 227 us (0.80)
  blocking collectives: 104 us -> 75.3 us
  waiting for transfers between devices: 75.6 us -> 53.8 us
  between operations: 14.1 us -> 0.71 us
  starting transfers between devices: 40.3 us -> 49.4 us
    psum x1 -> x0, waiting for transfers between devices: 48.4 us -> none  [shards(): output_sum = lax.psum(output_part, 'tp')]
    all_to_all x0 -> x2, waiting for transfers between devices: none -> 27.5 us  [the longest x1 14.6 us: shards(): incoming = lax.all_to_all(outgoing, ('guide', 'tp'), 0, 0, tiled=True)]
    all_to_all x1 -> x0, blocking collectives: 19.1 us -> none  [merge_attention(): lax.all_to_all(jnp.broadcast_to(fraction[None], (count,) + fraction.shape...]
    all_to_all x0 -> x2, starting transfers between devices: none -> 11.1 us  [the longest x1 6.48 us: merge_attention(): lax.all_to_all(jnp.broadcast_to(fraction[None], (count,) + fraction.shape...]
    all_to_all x1, blocking collectives: 47.7 us -> 38 us  [all_reduce(): parts = lax.all_to_all(flat.reshape(count, chunk), axis, 0, 0, tiled=True)]
  transfers between devices with their start and end apart: 5 -> 5, of which waited for: 5 -> 5; matrix products, arithmetic and copies ran while one was open for 6% -> 8% of each run, Pallas kernels for 0% -> 0%
where the time goes in v2:
time: 227 us; the launch traced here: 226 us
  blocking collectives  75.3 us (33%)
  waiting for transfers between devices  53.8 us (24%)
  starting transfers between devices  49.4 us (22%)
  local copies, waits for them, and re-layouts  25.9 us (11%)
  other arithmetic  16.8 us (7%)
  matrix products  3.94 us (2%)
    all_to_all x1, blocking collectives, all_reduce(): parts = lax.all_to_all(flat.reshape(count, chunk), axis, 0, 0, tiled=True)  38 us
    all_to_all x1, blocking collectives, all_reduce(): lax.all_to_all(jnp.broadcast_to(total, (count, chunk)), axis, 0, 0, tiled...  37.3 us
    all_to_all x1, starting transfers between devices, all_reduce(): parts = lax.all_to_all(flat.reshape(count, chunk), axis, 0, 0, tiled=True)  18.8 us
    all_to_all x1, waiting for transfers between devices, shards(): incoming = lax.all_to_all(outgoing, ('guide', 'tp'), 0, 0, tiled=True)  14.6 us
    all_to_all x1, starting transfers between devices, all_reduce(): lax.all_to_all(jnp.broadcast_to(total, (count, chunk)), axis, 0, 0, tiled...  13 us
    all_to_all x1, waiting for transfers between devices, merge_attention(): lax.all_to_all(jnp.broadcast_to(fraction[None], (count,) + fraction.shape...  12.9 us
    all_to_all x1, waiting for transfers between devices, all_reduce(): lax.all_to_all(jnp.broadcast_to(total, (count, chunk)), axis, 0, 0, tiled...  12.7 us
    all_to_all x1, waiting for transfers between devices, merge_attention(): parts = lax.all_to_all(spread, axis, 0, 0, tiled=True)  11.5 us
  transfers between devices with their start and end apart: 5, of which 5 were waited for; matrix products, arithmetic and copies ran while one was open for 8% of the time, Pallas kernels for 0%

profile of v2, /device:TPU:6, one launch (start us, length us, event | category | flops | bytes accessed | tf_op | source)
XLA Modules:
  0.0 225.9 jit_solution(11065161764698395721)
XLA Ops:
  0.0 1.0 bitcast_convert_fusion.1
  1.0 1.0 multiply_reduce_fusion.1
  2.9 1.0 fusion.38
  3.8 0.9 fusion.36
  5.6 18.8 %all-to-all-start = ((f32[64,1,512]{2,1,0:T(1,128)}), f32[64,1,512]{2,1,0:T(1,128)S(1)}, u32[]{:S(2)}, u32[]{:S(2)}) async-start(f32[64,1,512]{2,1,0:T(1,128)} %bitcast.6), calls=%async_computation | async-start | bytes 262144 | tf_op jit(solution)/shard_map/all_to_all | solution.py:49
  24.5 1.3 compare_reduce_fusion
  25.8 1.1 fusion.6
  26.9 4.0 %copy.122 = bf16[1,12,128,640]{2,3,1,0:T(8,128)(2,1)} copy(bf16[1,12,128,640]{3,2,1,0:T(8,128)(2,1)} %param.27) | data formatting | bytes 3932160 | tf_op args[9]
  30.9 2.6 %fusion.40 = (bf16[12,128,320]{1,2,0:T(8,128)(2,1)S(1)}, bf16[12,128,320]{1,2,0:T(8,128)(2,1)}) fusion(bf16[12,128,640]{1,2,0:T(8,128)(2,1)} %bitcast.92), kind=kLoop, calls=%fused_computation.122 | loop fusion | bytes 3932160 | tf_op jit(solution)/shard_map/slice | solution.py:159
  34.2 1.9 gather_fusion.4
  37.8 2.1 all-to-all-done
  40.8 13.0 %all-to-all-start.1 = ((f32[64,1,512]{2,1,0:T(1,128)}), f32[64,1,512]{2,1,0:T(1,128)S(1)}, u32[]{:S(2)}, u32[]{:S(2)}) async-start(f32[64,1,512]{2,1,0:T(1,128)} %broadcast_in_dim.171), calls=%async_computation.1 | async-start | bytes 262144 | tf_op jit(solution)/shard_map/all_to_all | solution.py:51
  54.4 1.5 select_bitcast_fusion.1
  56.0 12.7 %all-to-all-done.1 = f32[64,1,512]{2,1,0:T(1,128)S(1)} async-done(((f32[64,1,512]{2,1,0:T(1,128)}), f32[64,1,512]{2,1,0:T(1,128)S(1)}, u32[]{:S(2)}, u32[]{:S(2)}) %all-to-all-start.1) | async-done | bytes 131104 | tf_op jit(solution)/shard_map/all_to_all | solution.py:51
  70.3 1.2 gather_fusion.5
  71.5 0.9 reshape.397
  73.3 0.8 subtract_convert_fusion
  74.1 1.0 multiply_reduce_fusion.2
  81.9 0.8 reshape.498
  82.7 6.5 %all-to-all-start.2 = ((f32[64,1,198]{2,1,0:T(1,128)}), f32[64,1,198]{2,1,0:T(1,128)S(1)}, u32[]{:S(2)}, u32[]{:S(2)}) async-start(f32[64,1,198]{2,1,0:T(1,128)} %reshape.498), calls=%async_computation.2 | async-start | bytes 131072 | tf_op jit(solution)/shard_map/all_to_all | solution.py:68
  90.5 11.5 %all-to-all-done.2 = f32[64,1,198]{2,1,0:T(1,128)S(1)} async-done(((f32[64,1,198]{2,1,0:T(1,128)}), f32[64,1,198]{2,1,0:T(1,128)S(1)}, u32[]{:S(2)}, u32[]{:S(2)}) %all-to-all-start.2) | async-done | bytes 50720 | tf_op jit(solution)/shard_map/all_to_all | solution.py:68
  102.6 0.8 reduce.10
  105.1 0.8 reshape.500
  105.8 6.5 %all-to-all-start.3 = ((f32[64,1,195]{2,1,0:T(1,128)}), f32[64,1,195]{2,1,0:T(1,128)S(1)}, u32[]{:S(2)}, u32[]{:S(2)}) async-start(f32[64,1,195]{2,1,0:T(1,128)} %reshape.500), calls=%async_computation.3 | async-start | bytes 131072 | tf_op jit(solution)/shard_map/all_to_all | solution.py:82
  112.3 12.9 %all-to-all-done.3 = f32[64,1,195]{2,1,0:T(1,128)S(1)} async-done(((f32[64,1,195]{2,1,0:T(1,128)}), f32[64,1,195]{2,1,0:T(1,128)S(1)}, u32[]{:S(2)}, u32[]{:S(2)}) %all-to-all-start.3) | async-done | bytes 49952 | tf_op jit(solution)/shard_map/all_to_all | solution.py:82
  125.3 0.8 reduce.11
  127.0 1.1 broadcast_in_dim.182
  128.1 4.6 %all-to-all-start.4 = ((f32[8,16,2048]{2,1,0:T(8,128)}), f32[8,16,2048]{2,1,0:T(8,128)S(1)}, u32[]{:S(2)}, u32[]{:S(2)}) async-start(f32[8,16,2048]{2,1,0:T(8,128)} %bitcast.27), calls=%async_computation.4 | async-start | bytes 2097152 | tf_op jit(solution)/shard_map/all_to_all | solution.py:208
  133.5 14.6 %all-to-all-done.4 = f32[8,16,2048]{2,1,0:T(8,128)S(1)} async-done(((f32[8,16,2048]{2,1,0:T(8,128)}), f32[8,16,2048]{2,1,0:T(8,128)S(1)}, u32[]{:S(2)}, u32[]{:S(2)}) %all-to-all-start.4) | async-done | bytes 1048608 | tf_op jit(solution)/shard_map/all_to_all | solution.py:208
  149.0 38.0 %all_to_all.45 = f32[64,1,2048]{2,1,0:T(1,128)S(1)} all-to-all(f32[64,1,2048]{2,1,0:T(1,128)S(1)} %bitcast.93), channel_id=1, replica_groups=mesh['guide'=2,'seq'=64,'tp'=4] {'seq'}, dimensions={0} | all-to-all | bytes 1048576 | tf_op jit(solution)/shard_map/all_to_all | solution.py:49
  187.6 37.3 %all_to_all.46 = f32[64,1,2048]{2,1,0:T(1,128)S(1)} all-to-all(f32[64,1,2048]{2,1,0:T(1,128)S(1)} %broadcast_in_dim.183), channel_id=1, replica_groups=mesh['guide'=2,'seq'=64,'tp'=4] {'seq'}, dimensions={0} | all-to-all | bytes 1048576 | tf_op jit(solution)/shard_map/all_to_all | solution.py:51
  224.9 1.0 reshape.417
  (136 shorter events, 21.1 us)
Async XLA Ops:
  0.0 126.7 %copy-start = (bf16[320,2048]{1,0:T(8,128)(2,1)S(1)}, bf16[320,2048]{1,0:T(8,128)(2,1)}, u32[]{:S(2)}) copy-start(bf16[320,2048]{1,0:T(8,128)(2,1)} %param.25) | copy-start | bytes 3932164
  5.6 34.3 %all-to-all-start = ((f32[64,1,512]{2,1,0:T(1,128)}), f32[64,1,512]{2,1,0:T(1,128)S(1)}, u32[]{:S(2)}, u32[]{:S(2)}) async-start(f32[64,1,512]{2,1,0:T(1,128)} %bitcast.6), calls=%async_computation | async-start | bytes 262144 | tf_op jit(solution)/shard_map/all_to_all | solution.py:49
  24.5 30.0 %copy-start.12 = (pred[5]{0:T(512)(128)(4,1)}, pred[5]{0:T(512)(128)(4,1)S(1)}, u32[]{:S(2)}) copy-start(pred[5]{0:T(512)(128)(4,1)S(1)} %compare_and_fusion) | copy-start | bytes 19
  25.8 10.4 %copy-start.7 = (pred[32,12]{0,1:T(8,128)(4,1)}, pred[32,12]{0,1:T(8,128)(4,1)S(1)}, u32[]{:S(2)}) copy-start(pred[32,12]{0,1:T(8,128)(4,1)S(1)} %get-tuple-element.20) | copy-start | bytes 1156
  33.5 36.8 %copy-start.10 = (s32[1024]{0:T(1024)}, s32[1024]{0:T(1024)S(1)}, u32[]{:S(2)}) copy-start(s32[1024]{0:T(1024)S(1)} %pad_clamp_fusion) | copy-start | bytes 12292
  34.2 2.0 copy-start.1
  36.4 0.7 copy-start.11
  37.8 32.3 %copy-start.6 = (f32[32,32]{1,0:T(8,128)}, f32[32,32]{1,0:T(8,128)S(1)}, u32[]{:S(2)}) copy-start(f32[32,32]{1,0:T(8,128)S(1)} %get-tuple-element.41) | copy-start | bytes 12292
  40.8 27.9 %all-to-all-start.1 = ((f32[64,1,512]{2,1,0:T(1,128)}), f32[64,1,512]{2,1,0:T(1,128)S(1)}, u32[]{:S(2)}, u32[]{:S(2)}) async-start(f32[64,1,512]{2,1,0:T(1,128)} %broadcast_in_dim.171), calls=%async_computation.1 | async-start | bytes 262144 | tf_op jit(solution)/shard_map/all_to_all | solution.py:51
  54.4 15.5 %copy-start.15 = (f32[64]{0:T(128)S(1)}, f32[64]{0:T(128)}, u32[]{:S(2)}) copy-start(f32[64]{0:T(128)} %param.22) | copy-start | bytes 772
  56.0 20.5 %copy-start.4 = (bf16[12,128,5,64]{1,3,0,2:T(8,128)(2,1)S(1)}, bf16[12,128,5,64]{1,3,0,2:T(8,128)(2,1)}, u32[]{:S(2)}) copy-start(bf16[12,128,5,64]{1,3,0,2:T(8,128)(2,1)} %get-tuple-element.42) | copy-start | bytes 2949124
  70.0 9.7 %copy-start.3 = (bf16[12,128,5,64]{1,3,0,2:T(8,128)(2,1)S(1)}, bf16[12,128,5,64]{1,3,0,2:T(8,128)(2,1)}, u32[]{:S(2)}) copy-start(bf16[12,128,5,64]{1,3,0,2:T(8,128)(2,1)} %get-tuple-element.43) | copy-start | bytes 2949124
  73.2 6.2 %copy-start.14 = (pred[12]{0:T(512)(128)(4,1)S(1)}, pred[12]{0:T(512)(128)(4,1)}, u32[]{:S(2)}) copy-start(pred[12]{0:T(512)(128)(4,1)} %get-tuple-element.24) | copy-start | bytes 40
  73.2 6.3 %copy-start.9 = (pred[12,128]{1,0:T(8,128)(4,1)S(1)}, pred[12,128]{1,0:T(8,128)(4,1)}, u32[]{:S(2)}) copy-start(pred[12,128]{1,0:T(8,128)(4,1)} %fusion.20) | copy-start | bytes 4612
  73.2 7.1 %copy-start.8 = (pred[32,12]{0,1:T(8,128)(4,1)S(1)}, pred[32,12]{0,1:T(8,128)(4,1)}, u32[]{:S(2)}) copy-start(pred[32,12]{0,1:T(8,128)(4,1)} %copy-done.7) | copy-start | bytes 1156
  76.9 13.2 %copy-start.13 = (pred[5]{0:T(512)(128)(4,1)S(1)}, pred[5]{0:T(512)(128)(4,1)}, u32[]{:S(2)}) copy-start(pred[5]{0:T(512)(128)(4,1)} %copy-done.12) | copy-start | bytes 19
  82.7 19.4 %all-to-all-start.2 = ((f32[64,1,198]{2,1,0:T(1,128)}), f32[64,1,198]{2,1,0:T(1,128)S(1)}, u32[]{:S(2)}, u32[]{:S(2)}) async-start(f32[64,1,198]{2,1,0:T(1,128)} %reshape.498), calls=%async_computation.2 | async-start | bytes 131072 | tf_op jit(solution)/shard_map/all_to_all | solution.py:68
  89.2 37.5 %copy-start.2 = (bf16[1,32,2048]{2,1,0:T(8,128)(2,1)S(1)}, bf16[1,32,2048]{2,1,0:T(8,128)(2,1)}, u32[]{:S(2)}) copy-start(bf16[1,32,2048]{2,1,0:T(8,128)(2,1)} %param.18) | copy-start | bytes 393220
  105.8 19.4 %all-to-all-start.3 = ((f32[64,1,195]{2,1,0:T(1,128)}), f32[64,1,195]{2,1,0:T(1,128)S(1)}, u32[]{:S(2)}, u32[]{:S(2)}) async-start(f32[64,1,195]{2,1,0:T(1,128)} %reshape.500), calls=%async_computation.3 | async-start | bytes 131072 | tf_op jit(solution)/shard_map/all_to_all | solution.py:82
  128.1 20.2 %copy-start.5 = (bf16[32,8000]{1,0:T(8,128)(2,1)S(1)}, bf16[32,8000]{1,0:T(8,128)(2,1)}, u32[]{:S(2)}) copy-start(bf16[32,8000]{1,0:T(8,128)(2,1)} %param.26) | copy-start | bytes 1536004
  128.1 19.9 %all-to-all-start.4 = ((f32[8,16,2048]{2,1,0:T(8,128)}), f32[8,16,2048]{2,1,0:T(8,128)S(1)}, u32[]{:S(2)}, u32[]{:S(2)}) async-start(f32[8,16,2048]{2,1,0:T(8,128)} %bitcast.27), calls=%async_computation.4 | async-start | bytes 2097152 | tf_op jit(solution)/shard_map/all_to_all | solution.py:208

commit v3 on v2

--- a/solution.py
+++ b/solution.py
@@ -201,12 +201,34 @@
     output_part = output_part + jnp.where(lax.axis_index("tp") == 0, token_rows, 0.0)
     guide_count = lax.axis_size("guide")
     tp_count = lax.axis_size("tp")
-    outgoing = jnp.broadcast_to(
-        output_part.reshape(guide_count, 1, half_rows, -1),
-        (guide_count, tp_count, half_rows, output_part.shape[1]),
-    ).reshape(guide_count * tp_count, half_rows, -1)
-    incoming = lax.all_to_all(outgoing, ("guide", "tp"), 0, 0, tiled=True)
-    residual = jnp.sum(incoming.reshape(guide_count, tp_count, half_rows, -1), axis=1)
+    guide_index = lax.axis_index("guide")
+    group_rows = []
+    for guide_shift in range(guide_count):
+        target_group = (guide_index + guide_shift) % guide_count
+        outgoing = lax.dynamic_slice_in_dim(output_part, target_group * half_rows, half_rows, 0)
+        total = outgoing if guide_shift == 0 else None
+        for tp_shift in range(tp_count):
+            if guide_shift == 0 and tp_shift == 0:
+                continue
+            pairs = [
+                (
+                    source_group * tp_count + source_tp,
+                    ((source_group + guide_shift) % guide_count) * tp_count
+                    + (source_tp + tp_shift) % tp_count,
+                )
+                for source_group in range(guide_count)
+                for source_tp in range(tp_count)
+            ]
+            arrived = lax.ppermute(outgoing, ("guide", "tp"), pairs)
+            total = arrived if total is None else total + arrived
+        group_rows.append(total)
+    own_group, other_group = group_rows
+    residual = jnp.stack(
+        [
+            jnp.where(guide_index == 0, own_group, other_group),
+            jnp.where(guide_index == 0, other_group, own_group),
+        ]
+    )
     final_rows = norm_rows(residual, final_gain)
     final_part = lax.dynamic_slice_in_dim(final_rows, shard_index * part_width, part_width, 2)
     both = final_part.reshape(guide_count * half_rows, part_width)

time: 227 us -> 235 us (1.035)
  starting transfers between devices: 49.4 us -> 66.5 us
  waiting for transfers between devices: 53.8 us -> 44.8 us
    ppermute x0 -> x7, starting transfers between devices: none -> 21.7 us  [shards(): arrived = lax.ppermute(outgoing, ('guide', 'tp'), pairs)]
    all_to_all x1 -> x0, waiting for transfers between devices: 14.6 us -> none  [shards(): incoming = lax.all_to_all(outgoing, ('guide', 'tp'), 0, 0, tiled=True)]
    ppermute x0 -> x7, waiting for transfers between devices: none -> 5.56 us  [shards(): arrived = lax.ppermute(outgoing, ('guide', 'tp'), pairs)]
    all_to_all x1 -> x0, starting transfers between devices: 4.6 us -> none  [shards(): incoming = lax.all_to_all(outgoing, ('guide', 'tp'), 0, 0, tiled=True)]
  transfers between devices with their start and end apart: 5 -> 11, of which waited for: 5 -> 5; matrix products, arithmetic and copies ran while one was open for 8% -> 7% of each run, Pallas kernels for 0% -> 0%
where the time goes in v3:
time: 235 us; the launch traced here: 234 us
  blocking collectives  75.8 us (32%)
  starting transfers between devices  66.5 us (28%)
  waiting for transfers between devices  44.8 us (19%)
  local copies, waits for them, and re-layouts  24.8 us (11%)
  other arithmetic  16.9 us (7%)
  matrix products  3.94 us (2%)
    all_to_all x1, blocking collectives, all_reduce(): parts = lax.all_to_all(flat.reshape(count, chunk), axis, 0, 0, tiled=True)  38.5 us
    all_to_all x1, blocking collectives, all_reduce(): lax.all_to_all(jnp.broadcast_to(total, (count, chunk)), axis, 0, 0, tiled...  37.3 us
    ppermute x7, starting transfers between devices, shards(): arrived = lax.ppermute(outgoing, ('guide', 'tp'), pairs)  21.7 us
    all_to_all x1, starting transfers between devices, all_reduce(): parts = lax.all_to_all(flat.reshape(count, chunk), axis, 0, 0, tiled=True)  18.8 us
    all_to_all x1, starting transfers between devices, all_reduce(): lax.all_to_all(jnp.broadcast_to(total, (count, chunk)), axis, 0, 0, tiled...  13 us
    all_to_all x1, waiting for transfers between devices, merge_attention(): lax.all_to_all(jnp.broadcast_to(fraction[None], (count,) + fraction.shape...  12.9 us
    all_to_all x1, waiting for transfers between devices, all_reduce(): lax.all_to_all(jnp.broadcast_to(total, (count, chunk)), axis, 0, 0, tiled...  12.7 us
    all_to_all x1, waiting for transfers between devices, merge_attention(): parts = lax.all_to_all(spread, axis, 0, 0, tiled=True)  11.5 us
  transfers between devices with their start and end apart: 11, of which 5 were waited for; matrix products, arithmetic and copies ran while one was open for 7% of the time, Pallas kernels for 0%

profile of v3, /device:TPU:6, one launch (start us, length us, event | category | flops | bytes accessed | tf_op | source)
XLA Modules:
  0.0 233.5 jit_solution(12575286075455338198)
XLA Ops:
  0.0 1.0 bitcast_convert_fusion.1
  1.0 1.0 multiply_reduce_fusion
  2.9 1.0 fusion.39
  3.8 0.9 fusion.37
  5.6 18.8 %all-to-all-start = ((f32[64,1,512]{2,1,0:T(1,128)}), f32[64,1,512]{2,1,0:T(1,128)S(1)}, u32[]{:S(2)}, u32[]{:S(2)}) async-start(f32[64,1,512]{2,1,0:T(1,128)} %bitcast.6), calls=%async_computation | async-start | bytes 262144 | tf_op jit(solution)/shard_map/all_to_all | solution.py:49
  24.5 1.3 compare_reduce_fusion
  25.8 1.1 fusion.8
  26.9 4.0 %copy.122 = bf16[1,12,128,640]{2,3,1,0:T(8,128)(2,1)} copy(bf16[1,12,128,640]{3,2,1,0:T(8,128)(2,1)} %param.27) | data formatting | bytes 3932160 | tf_op args[9]
  30.9 2.6 %fusion.41 = (bf16[12,128,320]{1,2,0:T(8,128)(2,1)S(1)}, bf16[12,128,320]{1,2,0:T(8,128)(2,1)}) fusion(bf16[12,128,640]{1,2,0:T(8,128)(2,1)} %bitcast.92), kind=kLoop, calls=%fused_computation.130 | loop fusion | bytes 3932160 | tf_op jit(solution)/shard_map/slice | solution.py:159
  34.2 1.9 gather_fusion.4
  37.8 2.1 all-to-all-done
  40.8 13.0 %all-to-all-start.1 = ((f32[64,1,512]{2,1,0:T(1,128)}), f32[64,1,512]{2,1,0:T(1,128)S(1)}, u32[]{:S(2)}, u32[]{:S(2)}) async-start(f32[64,1,512]{2,1,0:T(1,128)} %broadcast_in_dim.164), calls=%async_computation.1 | async-start | bytes 262144 | tf_op jit(solution)/shard_map/all_to_all | solution.py:51
  54.4 1.5 select_bitcast_fusion.1
  56.0 12.7 %all-to-all-done.1 = f32[64,1,512]{2,1,0:T(1,128)S(1)} async-done(((f32[64,1,512]{2,1,0:T(1,128)}), f32[64,1,512]{2,1,0:T(1,128)S(1)}, u32[]{:S(2)}, u32[]{:S(2)}) %all-to-all-start.1) | async-done | bytes 131104 | tf_op jit(solution)/shard_map/all_to_all | solution.py:51
  70.3 1.2 gather_fusion.5
  71.5 0.9 reshape.389
  74.1 1.0 multiply_reduce_fusion.1
  82.7 6.5 %all-to-all-start.2 = ((f32[64,1,198]{2,1,0:T(1,128)}), f32[64,1,198]{2,1,0:T(1,128)S(1)}, u32[]{:S(2)}, u32[]{:S(2)}) async-start(f32[64,1,198]{2,1,0:T(1,128)} %reshape.488), calls=%async_computation.2 | async-start | bytes 131072 | tf_op jit(solution)/shard_map/all_to_all | solution.py:68
  90.5 11.5 %all-to-all-done.2 = f32[64,1,198]{2,1,0:T(1,128)S(1)} async-done(((f32[64,1,198]{2,1,0:T(1,128)}), f32[64,1,198]{2,1,0:T(1,128)S(1)}, u32[]{:S(2)}, u32[]{:S(2)}) %all-to-all-start.2) | async-done | bytes 50720 | tf_op jit(solution)/shard_map/all_to_all | solution.py:68
  105.8 6.5 %all-to-all-start.3 = ((f32[64,1,195]{2,1,0:T(1,128)}), f32[64,1,195]{2,1,0:T(1,128)S(1)}, u32[]{:S(2)}, u32[]{:S(2)}) async-start(f32[64,1,195]{2,1,0:T(1,128)} %reshape.490), calls=%async_computation.3 | async-start | bytes 131072 | tf_op jit(solution)/shard_map/all_to_all | solution.py:82
  112.4 12.9 %all-to-all-done.3 = f32[64,1,195]{2,1,0:T(1,128)S(1)} async-done(((f32[64,1,195]{2,1,0:T(1,128)}), f32[64,1,195]{2,1,0:T(1,128)S(1)}, u32[]{:S(2)}, u32[]{:S(2)}) %all-to-all-start.3) | async-done | bytes 49952 | tf_op jit(solution)/shard_map/all_to_all | solution.py:82
  127.1 4.9 %collective-permute-start.2 = (f32[16,2048]{1,0:T(8,128)S(1)}, f32[16,2048]{1,0:T(8,128)S(1)}, u32[]{:S(2)}, u32[]{:S(2)}) collective-permute-start(f32[16,2048]{1,0:T(8,128)S(1)} %get-tuple-element.31), channel_id=1, source_target_pairs={{0,3},{1,0},{2,1},{3,2},{256,259},{257,256},{258,257},{259,258},{4... | collective-permute-start | bytes 393224 | tf_op jit(solution)/shard_map/ppermute | solution.py:222
  132.0 2.5 %collective-permute-start.1 = (f32[16,2048]{1,0:T(8,128)S(1)}, f32[16,2048]{1,0:T(8,128)S(1)}, u32[]{:S(2)}, u32[]{:S(2)}) collective-permute-start(f32[16,2048]{1,0:T(8,128)S(1)} %get-tuple-element.31), channel_id=1, source_target_pairs={{0,2},{1,3},{2,0},{3,1},{256,258},{257,259},{258,256},{259,257},{4... | collective-permute-start | bytes 393224 | tf_op jit(solution)/shard_map/ppermute | solution.py:222
  134.6 2.9 %collective-permute-start = (f32[16,2048]{1,0:T(8,128)S(1)}, f32[16,2048]{1,0:T(8,128)S(1)}, u32[]{:S(2)}, u32[]{:S(2)}) collective-permute-start(f32[16,2048]{1,0:T(8,128)S(1)} %get-tuple-element.31), channel_id=1, source_target_pairs={{0,1},{1,2},{2,3},{3,0},{256,257},{257,258},{258,259},{259,256},{4... | collective-permute-start | bytes 393224 | tf_op jit(solution)/shard_map/ppermute | solution.py:222
  137.4 1.9 collective-permute-start.6
  139.4 5.6 %collective-permute-start.5 = (f32[16,2048]{1,0:T(8,128)S(1)}, f32[16,2048]{1,0:T(8,128)S(1)}, u32[]{:S(2)}, u32[]{:S(2)}) collective-permute-start(f32[16,2048]{1,0:T(8,128)S(1)} %get-tuple-element.30), channel_id=1, source_target_pairs={{0,258},{1,259},{2,256},{3,257},{256,2},{257,3},{258,0},{259,1},{4... | collective-permute-start | bytes 393224 | tf_op jit(solution)/shard_map/ppermute | solution.py:222
  145.0 1.9 collective-permute-start.3
  146.9 1.9 collective-permute-start.4
  149.6 5.5 %collective-permute-done.4 = f32[16,2048]{1,0:T(8,128)S(1)} collective-permute-done((f32[16,2048]{1,0:T(8,128)S(1)}, f32[16,2048]{1,0:T(8,128)S(1)}, u32[]{:S(2)}, u32[]{:S(2)}) %collective-permute-start.4) | collective-permute-done | bytes 131104 | tf_op jit(solution)/shard_map/ppermute | solution.py:222
  156.1 38.5 %all_to_all.40 = f32[64,1,2048]{2,1,0:T(1,128)S(1)} all-to-all(f32[64,1,2048]{2,1,0:T(1,128)S(1)} %bitcast.93), channel_id=1, replica_groups=mesh['guide'=2,'seq'=64,'tp'=4] {'seq'}, dimensions={0} | all-to-all | bytes 1048576 | tf_op jit(solution)/shard_map/all_to_all | solution.py:49
  195.2 37.3 %all_to_all.41 = f32[64,1,2048]{2,1,0:T(1,128)S(1)} all-to-all(f32[64,1,2048]{2,1,0:T(1,128)S(1)} %broadcast_in_dim.174), channel_id=1, replica_groups=mesh['guide'=2,'seq'=64,'tp'=4] {'seq'}, dimensions={0} | all-to-all | bytes 1048576 | tf_op jit(solution)/shard_map/all_to_all | solution.py:51
  232.6 1.0 reshape.407
  (149 shorter events, 25.2 us)
Async XLA Ops:
  0.0 126.7 %copy-start = (bf16[320,2048]{1,0:T(8,128)(2,1)S(1)}, bf16[320,2048]{1,0:T(8,128)(2,1)}, u32[]{:S(2)}) copy-start(bf16[320,2048]{1,0:T(8,128)(2,1)} %param.25) | copy-start | bytes 3932164
  5.6 34.3 %all-to-all-start = ((f32[64,1,512]{2,1,0:T(1,128)}), f32[64,1,512]{2,1,0:T(1,128)S(1)}, u32[]{:S(2)}, u32[]{:S(2)}) async-start(f32[64,1,512]{2,1,0:T(1,128)} %bitcast.6), calls=%async_computation | async-start | bytes 262144 | tf_op jit(solution)/shard_map/all_to_all | solution.py:49
  24.5 30.0 %copy-start.12 = (pred[5]{0:T(512)(128)(4,1)}, pred[5]{0:T(512)(128)(4,1)S(1)}, u32[]{:S(2)}) copy-start(pred[5]{0:T(512)(128)(4,1)S(1)} %compare_and_fusion) | copy-start | bytes 19
  25.8 10.4 %copy-start.7 = (pred[32,12]{0,1:T(8,128)(4,1)}, pred[32,12]{0,1:T(8,128)(4,1)S(1)}, u32[]{:S(2)}) copy-start(pred[32,12]{0,1:T(8,128)(4,1)S(1)} %get-tuple-element.20) | copy-start | bytes 1156
  33.5 36.8 %copy-start.10 = (s32[1024]{0:T(1024)}, s32[1024]{0:T(1024)S(1)}, u32[]{:S(2)}) copy-start(s32[1024]{0:T(1024)S(1)} %pad_clamp_fusion) | copy-start | bytes 12292
  34.2 2.0 copy-start.1
  36.4 0.7 copy-start.11
  37.8 32.3 %copy-start.6 = (f32[32,32]{1,0:T(8,128)}, f32[32,32]{1,0:T(8,128)S(1)}, u32[]{:S(2)}) copy-start(f32[32,32]{1,0:T(8,128)S(1)} %get-tuple-element.46) | copy-start | bytes 12292
  40.8 27.9 %all-to-all-start.1 = ((f32[64,1,512]{2,1,0:T(1,128)}), f32[64,1,512]{2,1,0:T(1,128)S(1)}, u32[]{:S(2)}, u32[]{:S(2)}) async-start(f32[64,1,512]{2,1,0:T(1,128)} %broadcast_in_dim.164), calls=%async_computation.1 | async-start | bytes 262144 | tf_op jit(solution)/shard_map/all_to_all | solution.py:51
  54.4 15.5 %copy-start.15 = (f32[64]{0:T(128)S(1)}, f32[64]{0:T(128)}, u32[]{:S(2)}) copy-start(f32[64]{0:T(128)} %param.22) | copy-start | bytes 772
  56.0 20.5 %copy-start.4 = (bf16[12,128,5,64]{1,3,0,2:T(8,128)(2,1)S(1)}, bf16[12,128,5,64]{1,3,0,2:T(8,128)(2,1)}, u32[]{:S(2)}) copy-start(bf16[12,128,5,64]{1,3,0,2:T(8,128)(2,1)} %get-tuple-element.47) | copy-start | bytes 2949124
  70.0 9.7 %copy-start.3 = (bf16[12,128,5,64]{1,3,0,2:T(8,128)(2,1)S(1)}, bf16[12,128,5,64]{1,3,0,2:T(8,128)(2,1)}, u32[]{:S(2)}) copy-start(bf16[12,128,5,64]{1,3,0,2:T(8,128)(2,1)} %get-tuple-element.48) | copy-start | bytes 2949124
  73.2 6.2 %copy-start.14 = (pred[12]{0:T(512)(128)(4,1)S(1)}, pred[12]{0:T(512)(128)(4,1)}, u32[]{:S(2)}) copy-start(pred[12]{0:T(512)(128)(4,1)} %get-tuple-element.27) | copy-start | bytes 40
  73.2 6.3 %copy-start.9 = (pred[12,128]{1,0:T(8,128)(4,1)S(1)}, pred[12,128]{1,0:T(8,128)(4,1)}, u32[]{:S(2)}) copy-start(pred[12,128]{1,0:T(8,128)(4,1)} %fusion.21) | copy-start | bytes 4612
  73.2 7.1 %copy-start.8 = (pred[32,12]{0,1:T(8,128)(4,1)S(1)}, pred[32,12]{0,1:T(8,128)(4,1)}, u32[]{:S(2)}) copy-start(pred[32,12]{0,1:T(8,128)(4,1)} %copy-done.7) | copy-start | bytes 1156
  76.9 13.2 %copy-start.13 = (pred[5]{0:T(512)(128)(4,1)S(1)}, pred[5]{0:T(512)(128)(4,1)}, u32[]{:S(2)}) copy-start(pred[5]{0:T(512)(128)(4,1)} %copy-done.12) | copy-start | bytes 19
  82.7 19.4 %all-to-all-start.2 = ((f32[64,1,198]{2,1,0:T(1,128)}), f32[64,1,198]{2,1,0:T(1,128)S(1)}, u32[]{:S(2)}, u32[]{:S(2)}) async-start(f32[64,1,198]{2,1,0:T(1,128)} %reshape.488), calls=%async_computation.2 | async-start | bytes 131072 | tf_op jit(solution)/shard_map/all_to_all | solution.py:68
  89.2 37.5 %copy-start.2 = (bf16[1,32,2048]{2,1,0:T(8,128)(2,1)S(1)}, bf16[1,32,2048]{2,1,0:T(8,128)(2,1)}, u32[]{:S(2)}) copy-start(bf16[1,32,2048]{2,1,0:T(8,128)(2,1)} %param.18) | copy-start | bytes 393220
  105.8 19.4 %all-to-all-start.3 = ((f32[64,1,195]{2,1,0:T(1,128)}), f32[64,1,195]{2,1,0:T(1,128)S(1)}, u32[]{:S(2)}, u32[]{:S(2)}) async-start(f32[64,1,195]{2,1,0:T(1,128)} %reshape.490), calls=%async_computation.3 | async-start | bytes 131072 | tf_op jit(solution)/shard_map/all_to_all | solution.py:82
  126.7 28.8 %copy-start.5 = (bf16[32,8000]{1,0:T(8,128)(2,1)S(1)}, bf16[32,8000]{1,0:T(8,128)(2,1)}, u32[]{:S(2)}) copy-start(bf16[32,8000]{1,0:T(8,128)(2,1)} %param.26) | copy-start | bytes 1536004
  127.1 17.9 %collective-permute-start.2 = (f32[16,2048]{1,0:T(8,128)S(1)}, f32[16,2048]{1,0:T(8,128)S(1)}, u32[]{:S(2)}, u32[]{:S(2)}) collective-permute-start(f32[16,2048]{1,0:T(8,128)S(1)} %get-tuple-element.31), channel_id=1, source_target_pairs={{0,3},{1,0},{2,1},{3,2},{256,259},{257,256},{258,257},{259,258},{4... | collective-permute-start | bytes 393224 | tf_op jit(solution)/shard_map/ppermute | solution.py:222
  132.0 14.9 %collective-permute-start.1 = (f32[16,2048]{1,0:T(8,128)S(1)}, f32[16,2048]{1,0:T(8,128)S(1)}, u32[]{:S(2)}, u32[]{:S(2)}) collective-permute-start(f32[16,2048]{1,0:T(8,128)S(1)} %get-tuple-element.31), channel_id=1, source_target_pairs={{0,2},{1,3},{2,0},{3,1},{256,258},{257,259},{258,256},{259,257},{4... | collective-permute-start | bytes 393224 | tf_op jit(solution)/shard_map/ppermute | solution.py:222
  134.6 15.0 %collective-permute-start = (f32[16,2048]{1,0:T(8,128)S(1)}, f32[16,2048]{1,0:T(8,128)S(1)}, u32[]{:S(2)}, u32[]{:S(2)}) collective-permute-start(f32[16,2048]{1,0:T(8,128)S(1)} %get-tuple-element.31), channel_id=1, source_target_pairs={{0,1},{1,2},{2,3},{3,0},{256,257},{257,258},{258,259},{259,256},{4... | collective-permute-start | bytes 393224 | tf_op jit(solution)/shard_map/ppermute | solution.py:222
  137.4 12.2 %collective-permute-start.6 = (f32[16,2048]{1,0:T(8,128)S(1)}, f32[16,2048]{1,0:T(8,128)S(1)}, u32[]{:S(2)}, u32[]{:S(2)}) collective-permute-start(f32[16,2048]{1,0:T(8,128)S(1)} %get-tuple-element.30), channel_id=1, source_target_pairs={{0,259},{1,256},{2,257},{3,258},{256,3},{257,0},{258,1},{259,2},{4... | collective-permute-start | bytes 393224 | tf_op jit(solution)/shard_map/ppermute | solution.py:222
  139.4 10.2 %collective-permute-start.5 = (f32[16,2048]{1,0:T(8,128)S(1)}, f32[16,2048]{1,0:T(8,128)S(1)}, u32[]{:S(2)}, u32[]{:S(2)}) collective-permute-start(f32[16,2048]{1,0:T(8,128)S(1)} %get-tuple-element.30), channel_id=1, source_target_pairs={{0,258},{1,259},{2,256},{3,257},{256,2},{257,3},{258,0},{259,1},{4... | collective-permute-start | bytes 393224 | tf_op jit(solution)/shard_map/ppermute | solution.py:222
  145.0 4.7 %collective-permute-start.3 = (f32[16,2048]{1,0:T(8,128)S(1)}, f32[16,2048]{1,0:T(8,128)S(1)}, u32[]{:S(2)}, u32[]{:S(2)}) collective-permute-start(f32[16,2048]{1,0:T(8,128)S(1)} %get-tuple-element.30), channel_id=1, source_target_pairs={{0,256},{1,257},{2,258},{3,259},{256,0},{257,1},{258,2},{259,3},{4... | collective-permute-start | bytes 393224 | tf_op jit(solution)/shard_map/ppermute | solution.py:222
  146.9 8.3 %collective-permute-start.4 = (f32[16,2048]{1,0:T(8,128)S(1)}, f32[16,2048]{1,0:T(8,128)S(1)}, u32[]{:S(2)}, u32[]{:S(2)}) collective-permute-start(f32[16,2048]{1,0:T(8,128)S(1)} %get-tuple-element.30), channel_id=1, source_target_pairs={{0,257},{1,258},{2,259},{3,256},{256,1},{257,2},{258,3},{259,0},{4... | collective-permute-start | bytes 393224 | tf_op jit(solution)/shard_map/ppermute | solution.py:222

commit v4 on v2

--- a/solution.py
+++ b/solution.py
@@ -58,21 +58,22 @@
     return jnp.pad(units, padding, constant_values=fill).reshape((count, per) + units.shape[1:])
 
 
-def merge_attention(local_max, local_total, local_weighted, self_score, fresh_value, axis):
+def merge_attention(local_max, local_total, local_weighted, own_score, own_value, axis):
     count = lax.axis_size(axis)
-    me = lax.axis_index(axis)
     unit_count = local_max.shape[0]
-    stats = jnp.concatenate([local_max[:, None], local_total[:, None], local_weighted], axis=1)
-    spread = spread_units(stats, count, 0.0)
-    spread = spread.at[:, :, 0].set(spread_units(local_max, count, NEG_FILL))
+    spread = jnp.concatenate(
+        [
+            spread_units(local_max[:, None], count, NEG_FILL),
+            spread_units(jnp.concatenate([local_total[:, None], local_weighted], axis=1), count, 0.0),
+        ],
+        axis=2,
+    )
     parts = lax.all_to_all(spread, axis, 0, 0, tiled=True)
     part_max = parts[:, :, 0]
     merged_max = jnp.max(part_max, axis=0)
     rescale = jnp.exp(part_max - merged_max[None, :])
     merged_total = jnp.sum(rescale * parts[:, :, 1], axis=0)
     merged_weighted = jnp.sum(rescale[:, :, None] * parts[:, :, 2:], axis=0)
-    own_score = lax.dynamic_index_in_dim(spread_units(self_score, count, 0.0), me, 0, keepdims=False)
-    own_value = lax.dynamic_index_in_dim(spread_units(fresh_value, count, 0.0), me, 0, keepdims=False)
     row_max = jnp.maximum(merged_max, own_score)
     old_scale = jnp.exp(merged_max - row_max)
     self_weight = jnp.exp(own_score - row_max)
@@ -112,37 +113,43 @@
     shard_index = lax.axis_index("seq")
     normed = norm_rows(token_rows, attn_gain)
     normed_part = lax.dynamic_slice_in_dim(normed, shard_index * part_width, part_width, 1)
-    projected = all_reduce(
-        jnp.concatenate(
-            [
-                jnp.dot(normed_part, query_weight, preferred_element_type=jnp.float32),
-                jnp.dot(normed_part, key_value_weight, preferred_element_type=jnp.float32),
-            ],
-            axis=1,
-        ),
-        "seq",
-    )
-    query_sum = projected[:, :query_width]
-    key_value_sum = projected[:, query_width:]
-    head_mapping = (lax.axis_index("tp") * nearby_heads + jnp.arange(nearby_heads)) // (
-        QUERY_HEADS // KEY_VALUE_HEADS
-    )
+    seq_count = lax.axis_size("seq")
+    group_width = QUERY_HEADS // KEY_VALUE_HEADS
+    unit_count = request_number * nearby_heads
+    unit_per = -(-unit_count // seq_count)
+    unit_index = jnp.minimum(jnp.arange(seq_count * unit_per), unit_count - 1)
+    unit_request = unit_index // nearby_heads
+    unit_kv_head = (lax.axis_index("tp") * nearby_heads + unit_index % nearby_heads) // group_width
+    query_part = jnp.dot(normed_part, query_weight, preferred_element_type=jnp.float32)
+    key_value_part = jnp.dot(normed_part, key_value_weight, preferred_element_type=jnp.float32)
+    unit_key_value = key_value_part.reshape(request_number, 2, KEY_VALUE_HEADS, HEAD_SIZE)[
+        unit_request, :, unit_kv_head, :
+    ]
+    outgoing = jnp.concatenate(
+        [
+            query_part.reshape(seq_count, -1),
+            unit_key_value.reshape(seq_count, unit_per * 2 * HEAD_SIZE),
+        ],
+        axis=1,
+    )
+    summed = jnp.sum(lax.all_to_all(outgoing, "seq", 0, 0, tiled=True), axis=0)
+    query_chunk = summed[: query_width * request_number // seq_count]
+    own_key_value = summed[query_chunk.shape[0] :].reshape(unit_per, 2, HEAD_SIZE)
+    query_sum = lax.all_to_all(
+        jnp.broadcast_to(query_chunk[None], (seq_count,) + query_chunk.shape), "seq", 0, 0, tiled=True
+    ).reshape(request_number, query_width)
     query_normed = per_head_norm(
         query_sum.reshape(request_number, nearby_heads, HEAD_SIZE), query_gain
     )
-    normalized_key = per_head_norm(
-        key_value_sum[:, : KEY_VALUE_HEADS * HEAD_SIZE].reshape(
-            request_number, KEY_VALUE_HEADS, HEAD_SIZE
-        ),
-        new_key_gain,
-    )
     query_rot = rotate(query_normed, lengths).astype(jnp.bfloat16)
-    key_all = rotate(normalized_key, lengths)
-    value_complete = key_value_sum[:, KEY_VALUE_HEADS * HEAD_SIZE :].reshape(
-        request_number, KEY_VALUE_HEADS, HEAD_SIZE
-    )
-    key_new = jnp.take(key_all, head_mapping, axis=1).astype(jnp.bfloat16)
-    fresh_value = jnp.take(value_complete, head_mapping, axis=1).astype(jnp.bfloat16)
+    own_unit = lax.dynamic_slice_in_dim(unit_index, shard_index * unit_per, unit_per, 0)
+    own_positions = jnp.take(lengths, own_unit // nearby_heads)
+    own_key = rotate(per_head_norm(own_key_value[:, None, 0], new_key_gain), own_positions)
+    own_key = own_key[:, 0].astype(jnp.bfloat16).astype(jnp.float32)
+    own_value = own_key_value[:, 1].astype(jnp.bfloat16).astype(jnp.float32)
+    own_query = query_rot.reshape(unit_count, HEAD_SIZE)[own_unit].astype(jnp.float32)
+    own_score = jnp.sum(own_query * own_key, axis=1) * scale
+    head_mapping = (lax.axis_index("tp") * nearby_heads + jnp.arange(nearby_heads)) // group_width
     slot_number = nearby_cache.shape[0]
     page_token_count = nearby_cache.shape[1]
     global_slot = shard_index * slot_number + jnp.arange(slot_number)
@@ -185,16 +192,12 @@
     request_weighted = jnp.einsum(
         "rs,shd->rhd", owner_float, slot_weighted, precision=lax.Precision.HIGHEST
     )
-    self_score = (
-        jnp.sum(query_rot.astype(jnp.float32) * key_new.astype(jnp.float32), axis=2) * scale
-    )
-    unit_count = request_number * nearby_heads
     attended = merge_attention(
         request_max.reshape(unit_count),
         request_total.reshape(unit_count),
         request_weighted.reshape(unit_count, HEAD_SIZE),
-        self_score.reshape(unit_count),
-        fresh_value.astype(jnp.float32).reshape(unit_count, HEAD_SIZE),
+        own_score,
+        own_value,
         "seq",
     ).reshape(request_number, nearby_heads * HEAD_SIZE)
     output_part = jnp.dot(attended, output_weight, preferred_element_type=jnp.float32)

time: 227 us -> 226 us (level)
  other arithmetic: 16.8 us -> 13.2 us
  waiting for transfers between devices: 53.8 us -> 56.7 us
  starting transfers between devices: 49.4 us -> 46.7 us
    all_to_all x2, starting transfers between devices: 31.8 us -> 29.2 us  [the longest x1 18.8 us: shards(): summed = jnp.sum(lax.all_to_all(outgoing, 'seq', 0, 0, tiled=True), axis=0)]
    all_to_all x2, waiting for transfers between devices: 14.8 us -> 17.3 us  [the longest x1 12.5 us: shards(): lax.all_to_all(jnp.broadcast_to(query_chunk[None], (seq_count,) + query_c...]
    unnamed x39 -> x29, local copies, waits for them, and re-layouts: 6.06 us -> 4.94 us
  transfers between devices with their start and end apart: 5 -> 5, of which waited for: 5 -> 5; matrix products, arithmetic and copies ran while one was open for 8% -> 6% of each run, Pallas kernels for 0% -> 0%
where the time goes in v4:
time: 226 us; the launch traced here: 225 us
  blocking collectives  75.3 us (33%)
  waiting for transfers between devices  56.7 us (25%)
  starting transfers between devices  46.7 us (21%)
  local copies, waits for them, and re-layouts  26.7 us (12%)
  other arithmetic  13.2 us (6%)
  matrix products  5.77 us (3%)
    all_to_all x1, blocking collectives, all_reduce(): parts = lax.all_to_all(flat.reshape(count, chunk), axis, 0, 0, tiled=True)  38.1 us
    all_to_all x1, blocking collectives, all_reduce(): lax.all_to_all(jnp.broadcast_to(total, (count, chunk)), axis, 0, 0, tiled...  37.2 us
    all_to_all x1, starting transfers between devices, shards(): summed = jnp.sum(lax.all_to_all(outgoing, 'seq', 0, 0, tiled=True), axis=0)  18.8 us
    all_to_all x1, waiting for transfers between devices, shards(): incoming = lax.all_to_all(outgoing, ('guide', 'tp'), 0, 0, tiled=True)  14.6 us
    all_to_all x1, waiting for transfers between devices, merge_attention(): lax.all_to_all(jnp.broadcast_to(fraction[None], (count,) + fraction.shape...  12.9 us
    all_to_all x1, waiting for transfers between devices, shards(): lax.all_to_all(jnp.broadcast_to(query_chunk[None], (seq_count,) + query_c...  12.5 us
    all_to_all x1, waiting for transfers between devices, merge_attention(): parts = lax.all_to_all(spread, axis, 0, 0, tiled=True)  11.9 us
    all_to_all x1, starting transfers between devices, shards(): lax.all_to_all(jnp.broadcast_to(query_chunk[None], (seq_count,) + query_c...  10.4 us
  transfers between devices with their start and end apart: 5, of which 5 were waited for; matrix products, arithmetic and copies ran while one was open for 6% of the time, Pallas kernels for 0%

profile of v4, /device:TPU:6, one launch (start us, length us, event | category | flops | bytes accessed | tf_op | source)
XLA Modules:
  0.0 225.0 jit_solution(7356091104513146661)
XLA Ops:
  0.0 1.1 bitcast_convert_fusion
  1.1 1.7 multiply_reduce_fusion.1
  2.8 1.2 add_rsqrt_fusion.3
  5.3 1.6 fusion.58
  6.9 1.0 reshape.541
  8.6 2.7 %gather_fusion.1 = f32[192,2,64]{2,1,0:T(2,128)S(1)} fusion(f32[32,2,5,64]{3,1,2,0:T(2,128)} %copy.130, s32[192]{0:T(256)S(1)} %bitcast.86), kind=kCustom, calls=%fused_computation.3 | custom fusion | bytes 198144 | tf_op jit(solution)/shard_map/gather | solution.py:125
  11.4 0.8 reshape.542
  12.2 1.0 fusion.56
  13.2 1.0 maximum_bitcast_fusion
  14.2 0.8 copy.131
  15.0 18.8 %all-to-all-start = ((f32[64,1,544]{2,1,0:T(1,128)}), f32[64,1,544]{2,1,0:T(1,128)S(1)}, u32[]{:S(2)}, u32[]{:S(2)}) async-start(f32[64,1,544]{2,1,0:T(1,128)} %copy.131), calls=%async_computation | async-start | bytes 327680 | tf_op jit(solution)/shard_map/all_to_all | solution.py:135
  34.9 2.3 %copy.132 = bf16[1,12,128,640]{2,3,1,0:T(8,128)(2,1)} copy(bf16[1,12,128,640]{3,2,1,0:T(8,128)(2,1)S(1)} %copy-done.2) | data formatting | bytes 3932160 | tf_op args[9]
  37.2 2.6 %fusion.60 = (bf16[12,128,320]{1,2,0:T(8,128)(2,1)S(1)}, bf16[12,128,320]{1,2,0:T(8,128)(2,1)}) fusion(bf16[12,128,640]{1,2,0:T(8,128)(2,1)} %bitcast.87), kind=kLoop, calls=%fused_computation.155 | loop fusion | bytes 3932160 | tf_op jit(solution)/shard_map/slice | solution.py:166
  40.6 1.9 gather_fusion.7
  44.3 1.5 select_bitcast_fusion.1
  45.8 4.7 %all-to-all-done = f32[64,1,544]{2,1,0:T(1,128)S(1)} async-done(((f32[64,1,544]{2,1,0:T(1,128)}), f32[64,1,544]{2,1,0:T(1,128)S(1)}, u32[]{:S(2)}, u32[]{:S(2)}) %all-to-all-start) | async-done | bytes 139296 | tf_op jit(solution)/shard_map/all_to_all | solution.py:135
  51.4 10.4 %all-to-all-start.1 = ((f32[64,1,160]{2,1,0:T(1,128)}), f32[64,1,160]{2,1,0:T(1,128)S(1)}, u32[]{:S(2)}, u32[]{:S(2)}) async-start(f32[64,1,160]{2,1,0:T(1,128)} %broadcast_in_dim.171), calls=%async_computation.1 | async-start | bytes 131072 | tf_op jit(solution)/shard_map/all_to_all | solution.py:138
  62.3 12.5 %all-to-all-done.1 = f32[64,1,160]{2,1,0:T(1,128)S(1)} async-done(((f32[64,1,160]{2,1,0:T(1,128)}), f32[64,1,160]{2,1,0:T(1,128)S(1)}, u32[]{:S(2)}, u32[]{:S(2)}) %all-to-all-start.1) | async-done | bytes 40992 | tf_op jit(solution)/shard_map/all_to_all | solution.py:138
  76.2 1.6 fusion.2
  80.9 0.8 reshape.645
  81.7 6.4 %all-to-all-start.2 = ((f32[64,1,198]{2,1,0:T(1,128)}), f32[64,1,198]{2,1,0:T(1,128)S(1)}, u32[]{:S(2)}, u32[]{:S(2)}) async-start(f32[64,1,198]{2,1,0:T(1,128)} %reshape.645), calls=%async_computation.2 | async-start | bytes 131072 | tf_op jit(solution)/shard_map/all_to_all | solution.py:71
  89.0 11.9 %all-to-all-done.2 = f32[64,1,198]{2,1,0:T(1,128)S(1)} async-done(((f32[64,1,198]{2,1,0:T(1,128)}), f32[64,1,198]{2,1,0:T(1,128)S(1)}, u32[]{:S(2)}, u32[]{:S(2)}) %all-to-all-start.2) | async-done | bytes 50720 | tf_op jit(solution)/shard_map/all_to_all | solution.py:71
  101.5 0.8 reduce.12
  104.9 6.5 %all-to-all-start.3 = ((f32[64,1,195]{2,1,0:T(1,128)}), f32[64,1,195]{2,1,0:T(1,128)S(1)}, u32[]{:S(2)}, u32[]{:S(2)}) async-start(f32[64,1,195]{2,1,0:T(1,128)} %reshape.647), calls=%async_computation.3 | async-start | bytes 131072 | tf_op jit(solution)/shard_map/all_to_all | solution.py:83
  111.4 12.9 %all-to-all-done.3 = f32[64,1,195]{2,1,0:T(1,128)S(1)} async-done(((f32[64,1,195]{2,1,0:T(1,128)}), f32[64,1,195]{2,1,0:T(1,128)S(1)}, u32[]{:S(2)}, u32[]{:S(2)}) %all-to-all-start.3) | async-done | bytes 49952 | tf_op jit(solution)/shard_map/all_to_all | solution.py:83
  124.3 0.8 reduce.13
  126.1 1.1 broadcast_in_dim.184
  127.2 4.6 %all-to-all-start.4 = ((f32[8,16,2048]{2,1,0:T(8,128)}), f32[8,16,2048]{2,1,0:T(8,128)S(1)}, u32[]{:S(2)}, u32[]{:S(2)}) async-start(f32[8,16,2048]{2,1,0:T(8,128)} %bitcast.25), calls=%async_computation.4 | async-start | bytes 2097152 | tf_op jit(solution)/shard_map/all_to_all | solution.py:211
  132.6 14.6 %all-to-all-done.4 = f32[8,16,2048]{2,1,0:T(8,128)S(1)} async-done(((f32[8,16,2048]{2,1,0:T(8,128)}), f32[8,16,2048]{2,1,0:T(8,128)S(1)}, u32[]{:S(2)}, u32[]{:S(2)}) %all-to-all-start.4) | async-done | bytes 1048608 | tf_op jit(solution)/shard_map/all_to_all | solution.py:211
  148.1 38.1 %all_to_all.45 = f32[64,1,2048]{2,1,0:T(1,128)S(1)} all-to-all(f32[64,1,2048]{2,1,0:T(1,128)S(1)} %bitcast.88), channel_id=1, replica_groups=mesh['guide'=2,'seq'=64,'tp'=4] {'seq'}, dimensions={0} | all-to-all | bytes 1048576 | tf_op jit(solution)/shard_map/all_to_all | solution.py:49
  186.7 37.2 %all_to_all.46 = f32[64,1,2048]{2,1,0:T(1,128)S(1)} all-to-all(f32[64,1,2048]{2,1,0:T(1,128)S(1)} %broadcast_in_dim.185), channel_id=1, replica_groups=mesh['guide'=2,'seq'=64,'tp'=4] {'seq'}, dimensions={0} | all-to-all | bytes 1048576 | tf_op jit(solution)/shard_map/all_to_all | solution.py:51
  224.0 1.0 reshape.556
  (128 shorter events, 18.4 us)
Async XLA Ops:
  0.0 125.8 %copy-start = (bf16[320,2048]{1,0:T(8,128)(2,1)S(1)}, bf16[320,2048]{1,0:T(8,128)(2,1)}, u32[]{:S(2)}) copy-start(bf16[320,2048]{1,0:T(8,128)(2,1)} %param.21) | copy-start | bytes 3932164
  0.0 33.9 %copy-start.7 = (s32[1,32,128]{2,1,0:T(8,128)S(1)}, s32[1,32,128]{2,1,0:T(8,128)}, u32[]{:S(2)}) copy-start(s32[1,32,128]{2,1,0:T(8,128)} %param.25) | copy-start | bytes 49156
  0.0 34.9 %copy-start.2 = (bf16[1,12,128,640]{3,2,1,0:T(8,128)(2,1)S(1)}, bf16[1,12,128,640]{3,2,1,0:T(8,128)(2,1)}, u32[]{:S(2)}) copy-start(bf16[1,12,128,640]{3,2,1,0:T(8,128)(2,1)} %param.23) | copy-start | bytes 5898244
  1.1 3.6 %copy-start.6 = (f32[32,2048]{1,0:T(8,128)}, f32[32,2048]{1,0:T(8,128)S(1)}, u32[]{:S(2)}) copy-start(f32[32,2048]{1,0:T(8,128)S(1)} %bitcast_convert_fusion) | copy-start | bytes 786436
  4.7 0.6 copy-start.8
  15.0 35.5 %all-to-all-start = ((f32[64,1,544]{2,1,0:T(1,128)}), f32[64,1,544]{2,1,0:T(1,128)S(1)}, u32[]{:S(2)}, u32[]{:S(2)}) async-start(f32[64,1,544]{2,1,0:T(1,128)} %copy.131), calls=%async_computation | async-start | bytes 327680 | tf_op jit(solution)/shard_map/all_to_all | solution.py:135
  40.5 2.0 copy-start.1
  44.3 17.8 %copy-start.10 = (f32[64]{0:T(128)S(1)}, f32[64]{0:T(128)}, u32[]{:S(2)}) copy-start(f32[64]{0:T(128)} %param.18) | copy-start | bytes 772
  44.3 30.9 %copy-start.9 = (f32[64]{0:T(128)S(1)}, f32[64]{0:T(128)}, u32[]{:S(2)}) copy-start(f32[64]{0:T(128)} %param.17) | copy-start | bytes 772
  45.8 33.3 %copy-start.4 = (bf16[12,128,5,64]{1,3,0,2:T(8,128)(2,1)S(1)}, bf16[12,128,5,64]{1,3,0,2:T(8,128)(2,1)}, u32[]{:S(2)}) copy-start(bf16[12,128,5,64]{1,3,0,2:T(8,128)(2,1)} %get-tuple-element.29) | copy-start | bytes 2949124
  51.4 23.4 %all-to-all-start.1 = ((f32[64,1,160]{2,1,0:T(1,128)}), f32[64,1,160]{2,1,0:T(1,128)S(1)}, u32[]{:S(2)}, u32[]{:S(2)}) async-start(f32[64,1,160]{2,1,0:T(1,128)} %broadcast_in_dim.171), calls=%async_computation.1 | async-start | bytes 131072 | tf_op jit(solution)/shard_map/all_to_all | solution.py:138
  80.4 45.3 %copy-start.3 = (bf16[1,32,2048]{2,1,0:T(8,128)(2,1)S(1)}, bf16[1,32,2048]{2,1,0:T(8,128)(2,1)}, u32[]{:S(2)}) copy-start(bf16[1,32,2048]{2,1,0:T(8,128)(2,1)} %param.14) | copy-start | bytes 393220
  81.7 19.2 %all-to-all-start.2 = ((f32[64,1,198]{2,1,0:T(1,128)}), f32[64,1,198]{2,1,0:T(1,128)S(1)}, u32[]{:S(2)}, u32[]{:S(2)}) async-start(f32[64,1,198]{2,1,0:T(1,128)} %reshape.645), calls=%async_computation.2 | async-start | bytes 131072 | tf_op jit(solution)/shard_map/all_to_all | solution.py:71
  104.9 19.5 %all-to-all-start.3 = ((f32[64,1,195]{2,1,0:T(1,128)}), f32[64,1,195]{2,1,0:T(1,128)S(1)}, u32[]{:S(2)}, u32[]{:S(2)}) async-start(f32[64,1,195]{2,1,0:T(1,128)} %reshape.647), calls=%async_computation.3 | async-start | bytes 131072 | tf_op jit(solution)/shard_map/all_to_all | solution.py:83
  127.2 20.2 %copy-start.5 = (bf16[32,8000]{1,0:T(8,128)(2,1)S(1)}, bf16[32,8000]{1,0:T(8,128)(2,1)}, u32[]{:S(2)}) copy-start(bf16[32,8000]{1,0:T(8,128)(2,1)} %param.22) | copy-start | bytes 1536004
  127.2 19.9 %all-to-all-start.4 = ((f32[8,16,2048]{2,1,0:T(8,128)}), f32[8,16,2048]{2,1,0:T(8,128)S(1)}, u32[]{:S(2)}, u32[]{:S(2)}) async-start(f32[8,16,2048]{2,1,0:T(8,128)} %bitcast.25), calls=%async_computation.4 | async-start | bytes 2097152 | tf_op jit(solution)/shard_map/all_to_all | solution.py:211

commit v5 on v4

--- a/solution.py
+++ b/solution.py
@@ -53,18 +53,20 @@
 
 
 def spread_units(units, count, fill):
-    per = -(-units.shape[0] // count)
-    padding = [(0, count * per - units.shape[0])] + [(0, 0)] * (units.ndim - 1)
-    return jnp.pad(units, padding, constant_values=fill).reshape((count, per) + units.shape[1:])
+    rows, heads = units.shape[:2]
+    slots = -(-heads * rows // count) * count // rows
+    padding = [(0, 0), (0, slots - heads)] + [(0, 0)] * (units.ndim - 2)
+    padded = jnp.pad(units, padding, constant_values=fill)
+    return padded.reshape((count, rows * slots // count) + units.shape[2:])
 
 
 def merge_attention(local_max, local_total, local_weighted, own_score, own_value, axis):
     count = lax.axis_size(axis)
-    unit_count = local_max.shape[0]
+    rows, heads = local_max.shape
     spread = jnp.concatenate(
         [
-            spread_units(local_max[:, None], count, NEG_FILL),
-            spread_units(jnp.concatenate([local_total[:, None], local_weighted], axis=1), count, 0.0),
+            spread_units(local_max[:, :, None], count, NEG_FILL),
+            spread_units(jnp.concatenate([local_total[:, :, None], local_weighted], axis=2), count, 0.0),
         ],
         axis=2,
     )
@@ -82,8 +84,8 @@
     fraction = jnp.concatenate([weighted, denominator[:, None]], axis=1)
     gathered = lax.all_to_all(
         jnp.broadcast_to(fraction[None], (count,) + fraction.shape), axis, 0, 0, tiled=True
-    ).reshape(-1, fraction.shape[-1])[:unit_count]
-    return (gathered[:, :-1] / gathered[:, -1:]).astype(jnp.bfloat16)
+    ).reshape(rows, -1, fraction.shape[-1])[:, :heads]
+    return (gathered[:, :, :-1] / gathered[:, :, -1:]).astype(jnp.bfloat16)
 
 
 def shards(
@@ -116,40 +118,42 @@
     seq_count = lax.axis_size("seq")
     group_width = QUERY_HEADS // KEY_VALUE_HEADS
     unit_count = request_number * nearby_heads
-    unit_per = -(-unit_count // seq_count)
-    unit_index = jnp.minimum(jnp.arange(seq_count * unit_per), unit_count - 1)
-    unit_request = unit_index // nearby_heads
-    unit_kv_head = (lax.axis_index("tp") * nearby_heads + unit_index % nearby_heads) // group_width
-    query_part = jnp.dot(normed_part, query_weight, preferred_element_type=jnp.float32)
-    key_value_part = jnp.dot(normed_part, key_value_weight, preferred_element_type=jnp.float32)
-    unit_key_value = key_value_part.reshape(request_number, 2, KEY_VALUE_HEADS, HEAD_SIZE)[
-        unit_request, :, unit_kv_head, :
-    ]
-    outgoing = jnp.concatenate(
+    slots_per_request = -(-nearby_heads * request_number // seq_count) * seq_count // request_number
+    unit_per = request_number * slots_per_request // seq_count
+    head_mapping = (lax.axis_index("tp") * nearby_heads + jnp.arange(nearby_heads)) // group_width
+    key_weight = key_value_weight[:, : KEY_VALUE_HEADS * HEAD_SIZE].reshape(
+        part_width, KEY_VALUE_HEADS, HEAD_SIZE
+    )
+    value_weight = key_value_weight[:, KEY_VALUE_HEADS * HEAD_SIZE :].reshape(
+        part_width, KEY_VALUE_HEADS, HEAD_SIZE
+    )
+    unit_weight = jnp.stack(
         [
-            query_part.reshape(seq_count, -1),
-            unit_key_value.reshape(seq_count, unit_per * 2 * HEAD_SIZE),
+            query_weight.reshape(part_width, nearby_heads, HEAD_SIZE),
+            jnp.take(key_weight, head_mapping, axis=1),
+            jnp.take(value_weight, head_mapping, axis=1),
         ],
-        axis=1,
-    )
-    summed = jnp.sum(lax.all_to_all(outgoing, "seq", 0, 0, tiled=True), axis=0)
-    query_chunk = summed[: query_width * request_number // seq_count]
-    own_key_value = summed[query_chunk.shape[0] :].reshape(unit_per, 2, HEAD_SIZE)
+        axis=2,
+    )
+    unit_weight = jnp.pad(
+        unit_weight, ((0, 0), (0, slots_per_request - nearby_heads), (0, 0), (0, 0))
+    ).reshape(part_width, -1)
+    unit_part = jnp.dot(normed_part, unit_weight, preferred_element_type=jnp.float32)
+    summed = jnp.sum(
+        lax.all_to_all(unit_part.reshape(seq_count, -1), "seq", 0, 0, tiled=True), axis=0
+    ).reshape(unit_per, 3, HEAD_SIZE)
     query_sum = lax.all_to_all(
-        jnp.broadcast_to(query_chunk[None], (seq_count,) + query_chunk.shape), "seq", 0, 0, tiled=True
-    ).reshape(request_number, query_width)
-    query_normed = per_head_norm(
-        query_sum.reshape(request_number, nearby_heads, HEAD_SIZE), query_gain
-    )
+        jnp.broadcast_to(summed[None, :, 0], (seq_count, unit_per, HEAD_SIZE)), "seq", 0, 0, tiled=True
+    ).reshape(request_number, slots_per_request, HEAD_SIZE)[:, :nearby_heads]
+    query_normed = per_head_norm(query_sum, query_gain)
     query_rot = rotate(query_normed, lengths).astype(jnp.bfloat16)
-    own_unit = lax.dynamic_slice_in_dim(unit_index, shard_index * unit_per, unit_per, 0)
-    own_positions = jnp.take(lengths, own_unit // nearby_heads)
-    own_key = rotate(per_head_norm(own_key_value[:, None, 0], new_key_gain), own_positions)
-    own_key = own_key[:, 0].astype(jnp.bfloat16).astype(jnp.float32)
-    own_value = own_key_value[:, 1].astype(jnp.bfloat16).astype(jnp.float32)
-    own_query = query_rot.reshape(unit_count, HEAD_SIZE)[own_unit].astype(jnp.float32)
+    own_position = jnp.take(lengths, shard_index * unit_per // slots_per_request)[None]
+    own_query = rotate(per_head_norm(summed[None, :, 0], query_gain), own_position)[0]
+    own_query = own_query.astype(jnp.bfloat16).astype(jnp.float32)
+    own_key = rotate(per_head_norm(summed[None, :, 1], new_key_gain), own_position)[0]
+    own_key = own_key.astype(jnp.bfloat16).astype(jnp.float32)
+    own_value = summed[:, 2].astype(jnp.bfloat16).astype(jnp.float32)
     own_score = jnp.sum(own_query * own_key, axis=1) * scale
-    head_mapping = (lax.axis_index("tp") * nearby_heads + jnp.arange(nearby_heads)) // group_width
     slot_number = nearby_cache.shape[0]
     page_token_count = nearby_cache.shape[1]
     global_slot = shard_index * slot_number + jnp.arange(slot_number)
@@ -193,9 +197,9 @@
         "rs,shd->rhd", owner_float, slot_weighted, precision=lax.Precision.HIGHEST
     )
     attended = merge_attention(
-        request_max.reshape(unit_count),
-        request_total.reshape(unit_count),
-        request_weighted.reshape(unit_count, HEAD_SIZE),
+        request_max,
+        request_total,
+        request_weighted,
         own_score,
         own_value,
         "seq",

time: 226 us -> 229 us (1.013)
  other arithmetic: 13.2 us -> 21.4 us
  waiting for transfers between devices: 56.7 us -> 51.6 us
  starting transfers between devices: 46.7 us -> 51.6 us
  local copies, waits for them, and re-layouts: 26.7 us -> 23.7 us
  matrix products: 5.77 us -> 2.86 us
    all_to_all x2, waiting for transfers between devices: 17.3 us -> 12 us  [the longest x1 12 us: shards(): lax.all_to_all(jnp.broadcast_to(summed[None, :, 0], (seq_count, unit_per,...]
    all_to_all x2, starting transfers between devices: 29.2 us -> 34.1 us  [the longest x1 19 us: shards(): lax.all_to_all(unit_part.reshape(seq_count, -1), 'seq', 0, 0, tiled=True)]
    gather x3 -> x2, local copies, waits for them, and re-layouts: 3.93 us -> 1.12 us  [the longest x1 0.56 us: shards(): jnp.take(key_weight, head_mapping, axis=1)]
    unnamed x29 -> x51, local copies, waits for them, and re-layouts: 4.94 us -> 5.48 us
  transfers between devices with their start and end apart: 5 -> 5, of which waited for: 5 -> 4; matrix products, arithmetic and copies ran while one was open for 6% -> 8% of each run, Pallas kernels for 0% -> 0%
where the time goes in v5:
time: 229 us; the launch traced here: 228 us
  blocking collectives  75.3 us (33%)
  starting transfers between devices  51.6 us (23%)
  waiting for transfers between devices  51.6 us (23%)
  local copies, waits for them, and re-layouts  23.7 us (10%)
  other arithmetic  21.4 us (9%)
  matrix products  2.86 us (1%)
    all_to_all x1, blocking collectives, all_reduce(): parts = lax.all_to_all(flat.reshape(count, chunk), axis, 0, 0, tiled=True)  38 us
    all_to_all x1, blocking collectives, all_reduce(): lax.all_to_all(jnp.broadcast_to(total, (count, chunk)), axis, 0, 0, tiled...  37.2 us
    all_to_all x1, starting transfers between devices, shards(): lax.all_to_all(unit_part.reshape(seq_count, -1), 'seq', 0, 0, tiled=True)  19 us
    all_to_all x1, starting transfers between devices, shards(): lax.all_to_all(jnp.broadcast_to(summed[None, :, 0], (seq_count, unit_per,...  15.1 us
    all_to_all x1, waiting for transfers between devices, shards(): incoming = lax.all_to_all(outgoing, ('guide', 'tp'), 0, 0, tiled=True)  14.6 us
    all_to_all x1, waiting for transfers between devices, merge_attention(): lax.all_to_all(jnp.broadcast_to(fraction[None], (count,) + fraction.shape...  12.9 us
    all_to_all x1, waiting for transfers between devices, merge_attention(): parts = lax.all_to_all(spread, axis, 0, 0, tiled=True)  12.1 us
    all_to_all x1, waiting for transfers between devices, shards(): lax.all_to_all(jnp.broadcast_to(summed[None, :, 0], (seq_count, unit_per,...  12 us
  transfers between devices with their start and end apart: 5, of which 4 were waited for; matrix products, arithmetic and copies ran while one was open for 8% of the time, Pallas kernels for 0%

profile of v5, /device:TPU:6, one launch (start us, length us, event | category | flops | bytes accessed | tf_op | source)
XLA Modules:
  0.0 227.8 jit_solution(16803625224568497564)
XLA Ops:
  0.1 1.8 bitcast_convert_fusion
  1.8 1.6 multiply_reduce_fusion.1
  3.5 0.9 fusion.46
  5.7 0.8 stack_reshape.3
  7.8 0.8 dynamic-slice.4
  8.6 0.9 fusion.20
  9.5 0.9 all_to_all.37
  10.4 19.0 %all-to-all-start = ((f32[64,1,576]{2,1,0:T(1,128)}), f32[64,1,576]{2,1,0:T(1,128)}, u32[]{:S(2)}, u32[]{:S(2)}) async-start(f32[64,1,576]{2,1,0:T(1,128)} %all_to_all.37), calls=%async_computation | async-start | bytes 327680 | tf_op jit(solution)/shard_map/all_to_all | solution.py:143
  29.3 1.3 compare_reduce_fusion
  30.6 1.1 fusion.6
  32.4 2.3 %copy.146 = bf16[1,12,128,640]{2,3,1,0:T(8,128)(2,1)} copy(bf16[1,12,128,640]{3,2,1,0:T(8,128)(2,1)S(1)} %copy-done.3) | data formatting | bytes 3932160 | tf_op args[9]
  34.7 1.6 fusion.45
  39.1 1.7 gather_fusion.5
  40.8 1.7 gather_fusion.6
  43.2 2.8 %select_bitcast_fusion.1 = (bf16[12,128,5,64]{1,3,0,2:T(8,128)(2,1)}, bf16[12,128,5,64]{1,3,0,2:T(8,128)(2,1)}) fusion(bf16[5,12,128,64]{2,3,1,0:T(8,128)(2,1)S(1)} %copy-done.2, pred[5]{0:T(512)(128)(4,1)S(1)} %copy-done.15, bf16[5,12,128,64]{2,3,1,0:T(8,128)(2,1)} %gather_fusion.6), kind=kLoop, calls=%fused_computation.15 | loop fusion | flops 983040 | bytes 3932165 | tf_op jit(solution)/shard_map/jit(_take)/select_n | solution.py:176
  46.0 1.2 reduce_sum.134
  48.2 15.1 %all-to-all-start.1 = ((f32[64,1,192]{2,1,0:T(1,128)}), f32[64,1,192]{2,1,0:T(1,128)S(1)}, u32[]{:S(2)}, u32[]{:S(2)}) async-start(f32[64,1,192]{2,1,0:T(1,128)} %reshape.638), calls=%async_computation.1 | async-start | bytes 131072 | tf_op jit(solution)/shard_map/all_to_all | solution.py:145
  63.5 0.8 fusion.38
  64.3 12.0 %all-to-all-done.1 = f32[64,1,192]{2,1,0:T(1,128)S(1)} async-done(((f32[64,1,192]{2,1,0:T(1,128)}), f32[64,1,192]{2,1,0:T(1,128)S(1)}, u32[]{:S(2)}, u32[]{:S(2)}) %all-to-all-start.1) | async-done | bytes 49184 | tf_op jit(solution)/shard_map/all_to_all | solution.py:145
  78.6 0.8 subtract_convert_fusion
  84.4 0.8 reshape.640
  85.2 6.4 %all-to-all-start.2 = ((f32[64,1,198]{2,1,0:T(1,128)}), f32[64,1,198]{2,1,0:T(1,128)S(1)}, u32[]{:S(2)}, u32[]{:S(2)}) async-start(f32[64,1,198]{2,1,0:T(1,128)} %reshape.640), calls=%async_computation.2 | async-start | bytes 131072 | tf_op jit(solution)/shard_map/all_to_all | solution.py:73
  92.3 12.1 %all-to-all-done.2 = f32[64,1,198]{2,1,0:T(1,128)S(1)} async-done(((f32[64,1,198]{2,1,0:T(1,128)}), f32[64,1,198]{2,1,0:T(1,128)S(1)}, u32[]{:S(2)}, u32[]{:S(2)}) %all-to-all-start.2) | async-done | bytes 50720 | tf_op jit(solution)/shard_map/all_to_all | solution.py:73
  106.8 0.8 reshape.642
  107.6 6.5 %all-to-all-start.3 = ((f32[64,1,195]{2,1,0:T(1,128)}), f32[64,1,195]{2,1,0:T(1,128)S(1)}, u32[]{:S(2)}, u32[]{:S(2)}) async-start(f32[64,1,195]{2,1,0:T(1,128)} %reshape.642), calls=%async_computation.3 | async-start | bytes 131072 | tf_op jit(solution)/shard_map/all_to_all | solution.py:85
  114.1 12.9 %all-to-all-done.3 = f32[64,1,195]{2,1,0:T(1,128)S(1)} async-done(((f32[64,1,195]{2,1,0:T(1,128)}), f32[64,1,195]{2,1,0:T(1,128)S(1)}, u32[]{:S(2)}, u32[]{:S(2)}) %all-to-all-start.3) | async-done | bytes 49952 | tf_op jit(solution)/shard_map/all_to_all | solution.py:85
  128.9 1.1 broadcast_in_dim.204
  130.1 4.6 %all-to-all-start.4 = ((f32[8,16,2048]{2,1,0:T(8,128)}), f32[8,16,2048]{2,1,0:T(8,128)S(1)}, u32[]{:S(2)}, u32[]{:S(2)}) async-start(f32[8,16,2048]{2,1,0:T(8,128)} %bitcast.35), calls=%async_computation.4 | async-start | bytes 2097152 | tf_op jit(solution)/shard_map/all_to_all | solution.py:215
  135.4 14.6 %all-to-all-done.4 = f32[8,16,2048]{2,1,0:T(8,128)S(1)} async-done(((f32[8,16,2048]{2,1,0:T(8,128)}), f32[8,16,2048]{2,1,0:T(8,128)S(1)}, u32[]{:S(2)}, u32[]{:S(2)}) %all-to-all-start.4) | async-done | bytes 1048608 | tf_op jit(solution)/shard_map/all_to_all | solution.py:215
  150.9 38.0 %all_to_all.45 = f32[64,1,2048]{2,1,0:T(1,128)S(1)} all-to-all(f32[64,1,2048]{2,1,0:T(1,128)S(1)} %bitcast.112), channel_id=1, replica_groups=mesh['guide'=2,'seq'=64,'tp'=4] {'seq'}, dimensions={0} | all-to-all | bytes 1048576 | tf_op jit(solution)/shard_map/all_to_all | solution.py:49
  189.5 37.2 %all_to_all.46 = f32[64,1,2048]{2,1,0:T(1,128)S(1)} all-to-all(f32[64,1,2048]{2,1,0:T(1,128)S(1)} %broadcast_in_dim.205), channel_id=1, replica_groups=mesh['guide'=2,'seq'=64,'tp'=4] {'seq'}, dimensions={0} | all-to-all | bytes 1048576 | tf_op jit(solution)/shard_map/all_to_all | solution.py:51
  226.8 1.0 reshape.530
  (145 shorter events, 21.4 us)
Async XLA Ops:
  0.0 128.6 %copy-start = (bf16[320,2048]{1,0:T(8,128)(2,1)S(1)}, bf16[320,2048]{1,0:T(8,128)(2,1)}, u32[]{:S(2)}) copy-start(bf16[320,2048]{1,0:T(8,128)(2,1)} %param.23) | copy-start | bytes 3932164
  0.0 31.8 %copy-start.1 = (s32[1,32]{1,0:T(1,128)S(1)}, s32[1,32]{1,0:T(1,128)}, u32[]{:S(2)}) copy-start(s32[1,32]{1,0:T(1,128)} %param.26) | copy-start | bytes 388
  0.0 32.4 %copy-start.3 = (bf16[1,12,128,640]{3,2,1,0:T(8,128)(2,1)S(1)}, bf16[1,12,128,640]{3,2,1,0:T(8,128)(2,1)}, u32[]{:S(2)}) copy-start(bf16[1,12,128,640]{3,2,1,0:T(8,128)(2,1)} %param.25) | copy-start | bytes 5898244
  0.1 6.7 %copy-start.14 = (pred[5]{0:T(512)(128)(4,1)}, pred[5]{0:T(512)(128)(4,1)S(1)}, u32[]{:S(2)}) copy-start(pred[5]{0:T(512)(128)(4,1)S(1)} %compare_and_fusion) | copy-start | bytes 19
  10.4 35.6 %all-to-all-start = ((f32[64,1,576]{2,1,0:T(1,128)}), f32[64,1,576]{2,1,0:T(1,128)}, u32[]{:S(2)}, u32[]{:S(2)}) async-start(f32[64,1,576]{2,1,0:T(1,128)} %all_to_all.37), calls=%async_computation | async-start | bytes 327680 | tf_op jit(solution)/shard_map/all_to_all | solution.py:143
  30.6 5.7 %copy-start.8 = (pred[32,12]{0,1:T(8,128)(4,1)}, pred[32,12]{0,1:T(8,128)(4,1)S(1)}, u32[]{:S(2)}) copy-start(pred[32,12]{0,1:T(8,128)(4,1)S(1)} %get-tuple-element.19) | copy-start | bytes 1156
  36.5 4.3 %copy-start.12 = (s32[1024]{0:T(1024)}, s32[1024]{0:T(1024)S(1)}, u32[]{:S(2)}) copy-start(s32[1024]{0:T(1024)S(1)} %pad_clamp_fusion.1) | copy-start | bytes 12292
  40.8 2.5 %copy-start.2 = (bf16[5,12,128,64]{2,3,1,0:T(8,128)(2,1)S(1)}, bf16[5,12,128,64]{2,3,1,0:T(8,128)(2,1)}, u32[]{:S(2)}) copy-start(bf16[5,12,128,64]{2,3,1,0:T(8,128)(2,1)} %gather_fusion.5) | copy-start | bytes 2949124
  40.8 2.5 %copy-start.15 = (pred[5]{0:T(512)(128)(4,1)S(1)}, pred[5]{0:T(512)(128)(4,1)}, u32[]{:S(2)}) copy-start(pred[5]{0:T(512)(128)(4,1)} %copy-done.14) | copy-start | bytes 19
  43.2 20.1 %copy-start.16 = (f32[64]{0:T(128)S(1)}, f32[64]{0:T(128)}, u32[]{:S(2)}) copy-start(f32[64]{0:T(128)} %param.19) | copy-start | bytes 772
  43.2 20.1 %copy-start.18 = (f32[64]{0:T(128)S(1)}, f32[64]{0:T(128)}, u32[]{:S(2)}) copy-start(f32[64]{0:T(128)} %param.20) | copy-start | bytes 772
  46.0 35.0 %copy-start.6 = (bf16[12,128,5,64]{1,3,0,2:T(8,128)(2,1)S(1)}, bf16[12,128,5,64]{1,3,0,2:T(8,128)(2,1)}, u32[]{:S(2)}) copy-start(bf16[12,128,5,64]{1,3,0,2:T(8,128)(2,1)} %get-tuple-element.50) | copy-start | bytes 2949124
  46.0 36.6 %copy-start.5 = (bf16[12,128,5,64]{1,3,0,2:T(8,128)(2,1)S(1)}, bf16[12,128,5,64]{1,3,0,2:T(8,128)(2,1)}, u32[]{:S(2)}) copy-start(bf16[12,128,5,64]{1,3,0,2:T(8,128)(2,1)} %get-tuple-element.51) | copy-start | bytes 2949124
  47.3 29.5 %copy-start.10 = (f32[3,3,64]{2,1,0:T(4,128)}, f32[3,3,64]{2,1,0:T(4,128)S(1)}, u32[]{:S(2)}) copy-start(f32[3,3,64]{2,1,0:T(4,128)S(1)} %reshape.517) | copy-start | bytes 6916
  48.2 28.1 %all-to-all-start.1 = ((f32[64,1,192]{2,1,0:T(1,128)}), f32[64,1,192]{2,1,0:T(1,128)S(1)}, u32[]{:S(2)}, u32[]{:S(2)}) async-start(f32[64,1,192]{2,1,0:T(1,128)} %reshape.638), calls=%async_computation.1 | async-start | bytes 131072 | tf_op jit(solution)/shard_map/all_to_all | solution.py:145
  77.7 3.7 %copy-start.11 = (pred[12,128]{1,0:T(8,128)(4,1)S(1)}, pred[12,128]{1,0:T(8,128)(4,1)}, u32[]{:S(2)}) copy-start(pred[12,128]{1,0:T(8,128)(4,1)} %fusion.24) | copy-start | bytes 4612
  77.7 3.8 %copy-start.9 = (pred[32,12]{0,1:T(8,128)(4,1)S(1)}, pred[32,12]{0,1:T(8,128)(4,1)}, u32[]{:S(2)}) copy-start(pred[32,12]{0,1:T(8,128)(4,1)} %copy-done.8) | copy-start | bytes 1156
  77.7 4.6 %copy-start.13 = (pred[12]{0:T(512)(128)(4,1)S(1)}, pred[12]{0:T(512)(128)(4,1)}, u32[]{:S(2)}) copy-start(pred[12]{0:T(512)(128)(4,1)} %get-tuple-element.23) | copy-start | bytes 40
  83.3 22.8 %copy-start.17 = (f32[3]{0:T(128)S(1)}, f32[3]{0:T(128)}, u32[]{:S(2)}) copy-start(f32[3]{0:T(128)} %fusion.38) | copy-start | bytes 40
  84.2 44.4 %copy-start.4 = (bf16[1,32,2048]{2,1,0:T(8,128)(2,1)S(1)}, bf16[1,32,2048]{2,1,0:T(8,128)(2,1)}, u32[]{:S(2)}) copy-start(bf16[1,32,2048]{2,1,0:T(8,128)(2,1)} %param.16) | copy-start | bytes 393220
  85.2 19.2 %all-to-all-start.2 = ((f32[64,1,198]{2,1,0:T(1,128)}), f32[64,1,198]{2,1,0:T(1,128)S(1)}, u32[]{:S(2)}, u32[]{:S(2)}) async-start(f32[64,1,198]{2,1,0:T(1,128)} %reshape.640), calls=%async_computation.2 | async-start | bytes 131072 | tf_op jit(solution)/shard_map/all_to_all | solution.py:73
  107.6 19.5 %all-to-all-start.3 = ((f32[64,1,195]{2,1,0:T(1,128)}), f32[64,1,195]{2,1,0:T(1,128)S(1)}, u32[]{:S(2)}, u32[]{:S(2)}) async-start(f32[64,1,195]{2,1,0:T(1,128)} %reshape.642), calls=%async_computation.3 | async-start | bytes 131072 | tf_op jit(solution)/shard_map/all_to_all | solution.py:85
  130.1 20.2 %copy-start.7 = (bf16[32,8000]{1,0:T(8,128)(2,1)S(1)}, bf16[32,8000]{1,0:T(8,128)(2,1)}, u32[]{:S(2)}) copy-start(bf16[32,8000]{1,0:T(8,128)(2,1)} %param.24) | copy-start | bytes 1536004
  130.1 19.9 %all-to-all-start.4 = ((f32[8,16,2048]{2,1,0:T(8,128)}), f32[8,16,2048]{2,1,0:T(8,128)S(1)}, u32[]{:S(2)}, u32[]{:S(2)}) async-start(f32[8,16,2048]{2,1,0:T(8,128)} %bitcast.35), calls=%async_computation.4 | async-start | bytes 2097152 | tf_op jit(solution)/shard_map/all_to_all | solution.py:215

commit v6 on v4

--- a/solution.py
+++ b/solution.py
@@ -52,6 +52,19 @@
     return whole.reshape(-1)[: value.size].reshape(value.shape)
 
 
+def all_reduce_columns(value, axis):
+    count = lax.axis_size(axis)
+    rows, columns = value.shape
+    if columns % count:
+        return all_reduce(value, axis)
+    parts = lax.all_to_all(value, axis, 1, 0, tiled=True)
+    total = jnp.sum(parts.reshape(count, rows, columns // count), axis=0)
+    whole = lax.all_to_all(
+        jnp.broadcast_to(total[None], (count, rows, columns // count)), axis, 0, 2, tiled=True
+    )
+    return whole[0]
+
+
 def spread_units(units, count, fill):
     per = -(-units.shape[0] // count)
     padding = [(0, count * per - units.shape[0])] + [(0, 0)] * (units.ndim - 1)
@@ -81,7 +94,7 @@
     weighted = merged_weighted * old_scale[:, None] + self_weight[:, None] * own_value
     fraction = jnp.concatenate([weighted, denominator[:, None]], axis=1)
     gathered = lax.all_to_all(
-        jnp.broadcast_to(fraction[None], (count,) + fraction.shape), axis, 0, 0, tiled=True
+        jnp.broadcast_to(fraction.reshape(1, -1), (count, fraction.size)), axis, 0, 0, tiled=True
     ).reshape(-1, fraction.shape[-1])[:unit_count]
     return (gathered[:, :-1] / gathered[:, -1:]).astype(jnp.bfloat16)
 
@@ -217,7 +230,7 @@
     conditional_part = logit_part[:half_rows]
     unconditional_part = logit_part[half_rows:]
     guided_part = unconditional_part + GUIDE_WEIGHT * (conditional_part - unconditional_part)
-    return all_reduce(guided_part, "seq")
+    return all_reduce_columns(guided_part, "seq")
 
 
 def solution(mesh):

time: 226 us -> 226 us (level)
    unnamed x29 -> x27, local copies, waits for them, and re-layouts: 4.94 us -> 4.04 us
where the time goes in v6:
time: 226 us; the launch traced here: 225 us
  blocking collectives  75.3 us (33%)
  waiting for transfers between devices  56.7 us (25%)
  starting transfers between devices  46.7 us (21%)
  local copies, waits for them, and re-layouts  27.6 us (12%)
  other arithmetic  12.3 us (5%)
  matrix products  5.78 us (3%)
    all_to_all x1, blocking collectives, all_reduce_columns(): parts = lax.all_to_all(value, axis, 1, 0, tiled=True)  38 us
    all_to_all x1, blocking collectives, all_reduce_columns(): lax.all_to_all(jnp.broadcast_to(total[None], (count, rows, columns // cou...  37.2 us
    all_to_all x1, starting transfers between devices, shards(): summed = jnp.sum(lax.all_to_all(outgoing, 'seq', 0, 0, tiled=True), axis=0)  18.8 us
    all_to_all x1, waiting for transfers between devices, shards(): incoming = lax.all_to_all(outgoing, ('guide', 'tp'), 0, 0, tiled=True)  14.6 us
    all_to_all x1, waiting for transfers between devices, merge_attention(): lax.all_to_all(jnp.broadcast_to(fraction.reshape(1, -1), (count, fraction...  12.9 us
    all_to_all x1, waiting for transfers between devices, shards(): lax.all_to_all(jnp.broadcast_to(query_chunk[None], (seq_count,) + query_c...  12.5 us
    all_to_all x1, waiting for transfers between devices, merge_attention(): parts = lax.all_to_all(spread, axis, 0, 0, tiled=True)  11.9 us
    all_to_all x1, starting transfers between devices, shards(): lax.all_to_all(jnp.broadcast_to(query_chunk[None], (seq_count,) + query_c...  10.4 us
  transfers between devices with their start and end apart: 5, of which 5 were waited for; matrix products, arithmetic and copies ran while one was open for 6% of the time, Pallas kernels for 0%

profile of v6, /device:TPU:6, one launch (start us, length us, event | category | flops | bytes accessed | tf_op | source)
XLA Modules:
  0.0 224.8 jit_solution(1792939755283523809)
XLA Ops:
  0.0 1.1 bitcast_convert_fusion
  1.1 1.7 multiply_reduce_fusion.1
  2.8 1.2 add_rsqrt_fusion.3
  5.3 1.6 fusion.58
  6.9 1.0 reshape.537
  8.6 2.7 %gather_fusion.1 = f32[192,2,64]{2,1,0:T(2,128)S(1)} fusion(f32[32,2,5,64]{3,1,2,0:T(2,128)} %copy.133, s32[192]{0:T(256)S(1)} %bitcast.89), kind=kCustom, calls=%fused_computation.3 | custom fusion | bytes 198144 | tf_op jit(solution)/shard_map/gather | solution.py:138
  11.4 0.8 reshape.538
  12.2 1.0 fusion.56
  13.2 1.0 maximum_bitcast_fusion
  14.2 0.8 copy.134
  15.0 18.8 %all-to-all-start = ((f32[64,1,544]{2,1,0:T(1,128)}), f32[64,1,544]{2,1,0:T(1,128)S(1)}, u32[]{:S(2)}, u32[]{:S(2)}) async-start(f32[64,1,544]{2,1,0:T(1,128)} %copy.134), calls=%async_computation | async-start | bytes 327680 | tf_op jit(solution)/shard_map/all_to_all | solution.py:148
  34.9 2.3 %copy.135 = bf16[1,12,128,640]{2,3,1,0:T(8,128)(2,1)} copy(bf16[1,12,128,640]{3,2,1,0:T(8,128)(2,1)S(1)} %copy-done.2) | data formatting | bytes 3932160 | tf_op args[9]
  37.2 2.6 %fusion.60 = (bf16[12,128,320]{1,2,0:T(8,128)(2,1)S(1)}, bf16[12,128,320]{1,2,0:T(8,128)(2,1)}) fusion(bf16[12,128,640]{1,2,0:T(8,128)(2,1)} %bitcast.90), kind=kLoop, calls=%fused_computation.155 | loop fusion | bytes 3932160 | tf_op jit(solution)/shard_map/slice | solution.py:179
  40.6 1.9 gather_fusion.7
  44.3 1.5 select_bitcast_fusion.1
  45.8 4.7 %all-to-all-done = f32[64,1,544]{2,1,0:T(1,128)S(1)} async-done(((f32[64,1,544]{2,1,0:T(1,128)}), f32[64,1,544]{2,1,0:T(1,128)S(1)}, u32[]{:S(2)}, u32[]{:S(2)}) %all-to-all-start) | async-done | bytes 139296 | tf_op jit(solution)/shard_map/all_to_all | solution.py:148
  51.4 10.4 %all-to-all-start.1 = ((f32[64,1,160]{2,1,0:T(1,128)}), f32[64,1,160]{2,1,0:T(1,128)S(1)}, u32[]{:S(2)}, u32[]{:S(2)}) async-start(f32[64,1,160]{2,1,0:T(1,128)} %broadcast_in_dim.172), calls=%async_computation.1 | async-start | bytes 131072 | tf_op jit(solution)/shard_map/all_to_all | solution.py:151
  62.3 12.5 %all-to-all-done.1 = f32[64,1,160]{2,1,0:T(1,128)S(1)} async-done(((f32[64,1,160]{2,1,0:T(1,128)}), f32[64,1,160]{2,1,0:T(1,128)S(1)}, u32[]{:S(2)}, u32[]{:S(2)}) %all-to-all-start.1) | async-done | bytes 40992 | tf_op jit(solution)/shard_map/all_to_all | solution.py:151
  76.2 1.6 fusion.2
  80.9 0.8 reshape.639
  81.7 6.4 %all-to-all-start.2 = ((f32[64,1,198]{2,1,0:T(1,128)}), f32[64,1,198]{2,1,0:T(1,128)S(1)}, u32[]{:S(2)}, u32[]{:S(2)}) async-start(f32[64,1,198]{2,1,0:T(1,128)} %reshape.639), calls=%async_computation.2 | async-start | bytes 131072 | tf_op jit(solution)/shard_map/all_to_all | solution.py:84
  89.0 11.9 %all-to-all-done.2 = f32[64,1,198]{2,1,0:T(1,128)S(1)} async-done(((f32[64,1,198]{2,1,0:T(1,128)}), f32[64,1,198]{2,1,0:T(1,128)S(1)}, u32[]{:S(2)}, u32[]{:S(2)}) %all-to-all-start.2) | async-done | bytes 50720 | tf_op jit(solution)/shard_map/all_to_all | solution.py:84
  101.4 0.8 reduce.14
  104.7 6.5 %all-to-all-start.3 = ((f32[64,1,195]{2,1,0:T(1,128)}), f32[64,1,195]{2,1,0:T(1,128)S(1)}, u32[]{:S(2)}, u32[]{:S(2)}) async-start(f32[64,1,195]{2,1,0:T(1,128)} %broadcast_in_dim.183), calls=%async_computation.3 | async-start | bytes 131072 | tf_op jit(solution)/shard_map/all_to_all | solution.py:96
  111.2 12.9 %all-to-all-done.3 = f32[64,1,195]{2,1,0:T(1,128)S(1)} async-done(((f32[64,1,195]{2,1,0:T(1,128)}), f32[64,1,195]{2,1,0:T(1,128)S(1)}, u32[]{:S(2)}, u32[]{:S(2)}) %all-to-all-start.3) | async-done | bytes 49952 | tf_op jit(solution)/shard_map/all_to_all | solution.py:96
  125.2 1.1 broadcast_in_dim.186
  126.3 4.6 %all-to-all-start.4 = ((f32[8,16,2048]{2,1,0:T(8,128)}), f32[8,16,2048]{2,1,0:T(8,128)S(1)}, u32[]{:S(2)}, u32[]{:S(2)}) async-start(f32[8,16,2048]{2,1,0:T(8,128)} %bitcast.25), calls=%async_computation.4 | async-start | bytes 2097152 | tf_op jit(solution)/shard_map/all_to_all | solution.py:224
  131.6 14.6 %all-to-all-done.4 = f32[8,16,2048]{2,1,0:T(8,128)S(1)} async-done(((f32[8,16,2048]{2,1,0:T(8,128)}), f32[8,16,2048]{2,1,0:T(8,128)S(1)}, u32[]{:S(2)}, u32[]{:S(2)}) %all-to-all-start.4) | async-done | bytes 1048608 | tf_op jit(solution)/shard_map/all_to_all | solution.py:224
  146.8 1.0 all_to_all.47
  148.1 38.0 %all_to_all.59 = f32[16,64,125]{2,0,1:T(8,128)S(1)} all-to-all(f32[16,64,125]{2,0,1:T(8,128)S(1)} %copy.152), channel_id=1, replica_groups=mesh['guide'=2,'seq'=64,'tp'=4] {'seq'}, dimensions={1} | all-to-all | bytes 1024000 | tf_op jit(solution)/shard_map/all_to_all | solution.py:60
  186.3 37.2 %all_to_all.60 = f32[64,16,125]{2,1,0:T(8,128)S(1)} all-to-all(f32[64,16,125]{2,1,0:T(8,128)S(1)} %broadcast_in_dim.187), channel_id=1, replica_groups=mesh['guide'=2,'seq'=64,'tp'=4] {'seq'}, dimensions={0} | all-to-all | bytes 1024000 | tf_op jit(solution)/shard_map/all_to_all | solution.py:62
  223.7 1.1 squeeze.22
  (127 shorter events, 18.1 us)
Async XLA Ops:
  0.0 124.8 %copy-start = (bf16[320,2048]{1,0:T(8,128)(2,1)S(1)}, bf16[320,2048]{1,0:T(8,128)(2,1)}, u32[]{:S(2)}) copy-start(bf16[320,2048]{1,0:T(8,128)(2,1)} %param.21) | copy-start | bytes 3932164
  0.0 33.9 %copy-start.7 = (s32[1,32,128]{2,1,0:T(8,128)S(1)}, s32[1,32,128]{2,1,0:T(8,128)}, u32[]{:S(2)}) copy-start(s32[1,32,128]{2,1,0:T(8,128)} %param.25) | copy-start | bytes 49156
  0.0 34.9 %copy-start.2 = (bf16[1,12,128,640]{3,2,1,0:T(8,128)(2,1)S(1)}, bf16[1,12,128,640]{3,2,1,0:T(8,128)(2,1)}, u32[]{:S(2)}) copy-start(bf16[1,12,128,640]{3,2,1,0:T(8,128)(2,1)} %param.23) | copy-start | bytes 5898244
  1.1 3.6 %copy-start.6 = (f32[32,2048]{1,0:T(8,128)}, f32[32,2048]{1,0:T(8,128)S(1)}, u32[]{:S(2)}) copy-start(f32[32,2048]{1,0:T(8,128)S(1)} %bitcast_convert_fusion) | copy-start | bytes 786436
  4.7 0.6 copy-start.8
  15.0 35.5 %all-to-all-start = ((f32[64,1,544]{2,1,0:T(1,128)}), f32[64,1,544]{2,1,0:T(1,128)S(1)}, u32[]{:S(2)}, u32[]{:S(2)}) async-start(f32[64,1,544]{2,1,0:T(1,128)} %copy.134), calls=%async_computation | async-start | bytes 327680 | tf_op jit(solution)/shard_map/all_to_all | solution.py:148
  40.5 2.0 copy-start.1
  44.3 17.8 %copy-start.10 = (f32[64]{0:T(128)S(1)}, f32[64]{0:T(128)}, u32[]{:S(2)}) copy-start(f32[64]{0:T(128)} %param.18) | copy-start | bytes 772
  44.3 30.9 %copy-start.9 = (f32[64]{0:T(128)S(1)}, f32[64]{0:T(128)}, u32[]{:S(2)}) copy-start(f32[64]{0:T(128)} %param.17) | copy-start | bytes 772
  45.8 33.3 %copy-start.4 = (bf16[12,128,5,64]{1,3,0,2:T(8,128)(2,1)S(1)}, bf16[12,128,5,64]{1,3,0,2:T(8,128)(2,1)}, u32[]{:S(2)}) copy-start(bf16[12,128,5,64]{1,3,0,2:T(8,128)(2,1)} %get-tuple-element.29) | copy-start | bytes 2949124
  51.4 23.4 %all-to-all-start.1 = ((f32[64,1,160]{2,1,0:T(1,128)}), f32[64,1,160]{2,1,0:T(1,128)S(1)}, u32[]{:S(2)}, u32[]{:S(2)}) async-start(f32[64,1,160]{2,1,0:T(1,128)} %broadcast_in_dim.172), calls=%async_computation.1 | async-start | bytes 131072 | tf_op jit(solution)/shard_map/all_to_all | solution.py:151
  80.1 44.8 %copy-start.3 = (bf16[1,32,2048]{2,1,0:T(8,128)(2,1)S(1)}, bf16[1,32,2048]{2,1,0:T(8,128)(2,1)}, u32[]{:S(2)}) copy-start(bf16[1,32,2048]{2,1,0:T(8,128)(2,1)} %param.14) | copy-start | bytes 393220
  81.7 19.2 %all-to-all-start.2 = ((f32[64,1,198]{2,1,0:T(1,128)}), f32[64,1,198]{2,1,0:T(1,128)S(1)}, u32[]{:S(2)}, u32[]{:S(2)}) async-start(f32[64,1,198]{2,1,0:T(1,128)} %reshape.639), calls=%async_computation.2 | async-start | bytes 131072 | tf_op jit(solution)/shard_map/all_to_all | solution.py:84
  104.7 19.5 %all-to-all-start.3 = ((f32[64,1,195]{2,1,0:T(1,128)}), f32[64,1,195]{2,1,0:T(1,128)S(1)}, u32[]{:S(2)}, u32[]{:S(2)}) async-start(f32[64,1,195]{2,1,0:T(1,128)} %broadcast_in_dim.183), calls=%async_computation.3 | async-start | bytes 131072 | tf_op jit(solution)/shard_map/all_to_all | solution.py:96
  126.3 20.2 %copy-start.5 = (bf16[32,8000]{1,0:T(8,128)(2,1)S(1)}, bf16[32,8000]{1,0:T(8,128)(2,1)}, u32[]{:S(2)}) copy-start(bf16[32,8000]{1,0:T(8,128)(2,1)} %param.22) | copy-start | bytes 1536004
  126.3 19.9 %all-to-all-start.4 = ((f32[8,16,2048]{2,1,0:T(8,128)}), f32[8,16,2048]{2,1,0:T(8,128)S(1)}, u32[]{:S(2)}, u32[]{:S(2)}) async-start(f32[8,16,2048]{2,1,0:T(8,128)} %bitcast.25), calls=%async_computation.4 | async-start | bytes 2097152 | tf_op jit(solution)/shard_map/all_to_all | solution.py:224

commit v7 on v6

--- a/solution.py
+++ b/solution.py
@@ -1,6 +1,9 @@
+import functools
+
 import jax
 import jax.numpy as jnp
 from jax import lax
+from jax.experimental import pallas as pl
 from jax.sharding import PartitionSpec as P
 
 QUERY_HEADS = 20
@@ -11,6 +14,41 @@
 GUIDE_WEIGHT = 2.5
 NORM_EPS = 1e-06
 NEG_FILL = -1e30
+
+
+def page_attention_kernel(scale, q_ref, owner_t_ref, owner_ref, valid_ref, k_ref, v_ref, out_ref):
+    heads = q_ref.shape[0]
+    slots = owner_t_ref.shape[0]
+    owner_t = owner_t_ref[...] > 0.5
+    owner = owner_ref[...] > 0.5
+    valid = valid_ref[...] > 0.5
+    owner_t_bf = owner_t_ref[...].astype(jnp.bfloat16)
+    eye = lax.broadcasted_iota(jnp.int32, (slots, slots), 0) == lax.broadcasted_iota(jnp.int32, (slots, slots), 1)
+    for h in range(heads):
+        slot_query = jnp.dot(owner_t_bf, q_ref[h], preferred_element_type=jnp.float32).astype(jnp.bfloat16)
+        scores = lax.dot_general(slot_query, k_ref[h], (((1,), (1,)), ((), ())), preferred_element_type=jnp.float32) * scale
+        scores = jnp.where(valid, scores, NEG_FILL)
+        slot_max = jnp.max(scores, axis=1, keepdims=True)
+        request_max_row = jnp.max(jnp.where(owner_t, slot_max, NEG_FILL), axis=0, keepdims=True)
+        owner_max = jnp.max(jnp.where(owner_t, request_max_row, NEG_FILL), axis=1, keepdims=True)
+        weights = jnp.where(valid, jnp.exp(scores - owner_max), 0.0).astype(jnp.bfloat16)
+        slot_total = jnp.sum(weights.astype(jnp.float32), axis=1, keepdims=True)
+        slot_weighted = jnp.dot(weights, v_ref[h], preferred_element_type=jnp.float32)
+        slot_max_row = jnp.max(jnp.where(eye, slot_max, NEG_FILL), axis=0, keepdims=True)
+        slot_total_row = jnp.sum(jnp.where(eye, slot_total, 0.0), axis=0, keepdims=True)
+        request_max = jnp.max(jnp.where(owner, slot_max_row, NEG_FILL), axis=1, keepdims=True)
+        request_total = jnp.sum(jnp.where(owner, slot_total_row, 0.0), axis=1, keepdims=True)
+        request_weighted = jnp.dot(owner_ref[...], slot_weighted, precision=lax.Precision.HIGHEST, preferred_element_type=jnp.float32)
+        lane = lax.broadcasted_iota(jnp.int32, request_weighted.shape, 1)
+        out_ref[h, :, : request_weighted.shape[1]] = request_weighted
+        out_ref[h, :, request_weighted.shape[1]:] = jnp.where(lane == 0, request_total, jnp.where(lane == 1, request_max, 0.0))
+
+def page_attention(query_heads, owner_t, owner, valid, key_heads, value_heads, scale):
+    heads, requests, size = query_heads.shape
+    return pl.pallas_call(
+        functools.partial(page_attention_kernel, scale),
+        out_shape=jax.ShapeDtypeStruct((heads, requests, 2 * size), jnp.float32),
+    )(query_heads, owner_t, owner, valid, key_heads, value_heads)
 
 
 def norm_rows(token_rows, scale_gain):
@@ -184,27 +222,25 @@
     )
     key_heads = jnp.take(key_tile, head_mapping, axis=2)
     value_heads = jnp.take(value_tile, head_mapping, axis=2)
-    slot_query = jnp.take(query_rot, owner_req, axis=0)
-    scores = (
-        jnp.einsum("shd,skhd->shk", slot_query, key_heads, preferred_element_type=jnp.float32)
-        * scale
-    )
-    scores = jnp.where(is_valid[:, None, :], scores, NEG_FILL)
-    slot_max = jnp.max(scores, axis=2)
-    request_max = jnp.max(jnp.where(owner_mask[:, :, None], slot_max[None, :, :], NEG_FILL), axis=1)
-    owner_max = jnp.take(request_max, owner_req, axis=0)
-    weights = jnp.where(is_valid[:, None, :], jnp.exp(scores - owner_max[:, :, None]), 0.0).astype(
-        jnp.bfloat16
-    )
-    slot_total = jnp.sum(weights.astype(jnp.float32), axis=2)
-    slot_weighted = jnp.einsum(
-        "shk,skhd->shd", weights, value_heads, preferred_element_type=jnp.float32
-    )
-    owner_float = owner_mask.astype(jnp.float32)
-    request_total = jnp.dot(owner_float, slot_total, precision=lax.Precision.HIGHEST)
-    request_weighted = jnp.einsum(
-        "rs,shd->rhd", owner_float, slot_weighted, precision=lax.Precision.HIGHEST
-    )
+    padded_slots = -(-slot_number // 8) * 8
+    owner = jnp.pad(owner_mask.astype(jnp.float32), ((0, 0), (0, padded_slots - slot_number)))
+    block_valid = (
+        (jnp.arange(padded_slots)[:, None, None] == jnp.arange(slot_number)[None, :, None])
+        & is_valid[None]
+    ).reshape(padded_slots, slot_number * page_token_count)
+    request_stats = page_attention(
+        jnp.transpose(query_rot, (1, 0, 2)),
+        owner.T,
+        owner,
+        block_valid.astype(jnp.float32),
+        jnp.transpose(key_heads, (2, 0, 1, 3)).reshape(nearby_heads, -1, HEAD_SIZE),
+        jnp.transpose(value_heads, (2, 0, 1, 3)).reshape(nearby_heads, -1, HEAD_SIZE),
+        scale,
+    )
+    request_stats = jnp.transpose(request_stats, (1, 0, 2))
+    request_weighted = request_stats[:, :, :HEAD_SIZE]
+    request_total = request_stats[:, :, HEAD_SIZE]
+    request_max = request_stats[:, :, HEAD_SIZE + 1]
     attended = merge_attention(
         request_max.reshape(unit_count),
         request_total.reshape(unit_count),

time: 226 us -> 238 us (1.053)
  local copies, waits for them, and re-layouts: 27.6 us -> 34.5 us
  Pallas kernels: 0 us -> 6.27 us
  starting transfers between devices: 46.7 us -> 51.6 us
  waiting for transfers between devices: 56.7 us -> 52.2 us
  matrix products: 5.78 us -> 3.15 us
    pallas_call x0 -> x1, Pallas kernels: none -> 6.27 us  [page_attention(): pl.pallas_call(functools.partial(page_attention_kernel, scale), out_shape...]
    transpose x0 -> x3, local copies, waits for them, and re-layouts: none -> 5.19 us  [the longest x1 2.79 us: shards(): jnp.transpose(value_heads, (2, 0, 1, 3))]
    all_to_all x1, waiting for transfers between devices: 4.73 us -> 0.01 us  [shards(): summed = jnp.sum(lax.all_to_all(outgoing, 'seq', 0, 0, tiled=True), axis=0)]
    all_to_all x1, starting transfers between devices: 10.4 us -> 15.1 us  [shards(): lax.all_to_all(jnp.broadcast_to(query_chunk[None], (seq_count,) + query_c...]
    slice x1 -> x5, local copies, waits for them, and re-layouts: 2.59 us -> 5.2 us  [the longest x1 2.59 us: shards(): nearby_cache[:, :, KEY_VALUE_HEADS * HEAD_SIZE:]]
    dot_general x4 -> x0, matrix products: 2.6 us -> none  [the longest x1 1.55 us: shards(): jnp.einsum('shd,skhd->shk', slot_query, key_heads, preferred_element_type...]
  transfers between devices with their start and end apart: 5 -> 5, of which waited for: 5 -> 4; matrix products, arithmetic and copies ran while one was open for 6% -> 9% of each run, Pallas kernels for 0% -> 0%
where the time goes in v7:
time: 238 us; the launch traced here: 237 us
  blocking collectives  75.3 us (32%)
  waiting for transfers between devices  52.2 us (22%)
  starting transfers between devices  51.6 us (22%)
  local copies, waits for them, and re-layouts  34.5 us (14%)
  other arithmetic  13.2 us (6%)
  Pallas kernels  6.27 us (3%)
  matrix products  3.15 us (1%)
    all_to_all x1, blocking collectives, all_reduce_columns(): parts = lax.all_to_all(value, axis, 1, 0, tiled=True)  38 us
    all_to_all x1, blocking collectives, all_reduce_columns(): lax.all_to_all(jnp.broadcast_to(total[None], (count, rows, columns // cou...  37.2 us
    all_to_all x1, starting transfers between devices, shards(): summed = jnp.sum(lax.all_to_all(outgoing, 'seq', 0, 0, tiled=True), axis=0)  18.8 us
    all_to_all x1, starting transfers between devices, shards(): lax.all_to_all(jnp.broadcast_to(query_chunk[None], (seq_count,) + query_c...  15.1 us
    all_to_all x1, waiting for transfers between devices, shards(): incoming = lax.all_to_all(outgoing, ('guide', 'tp'), 0, 0, tiled=True)  14.6 us
    all_to_all x1, waiting for transfers between devices, merge_attention(): lax.all_to_all(jnp.broadcast_to(fraction.reshape(1, -1), (count, fraction...  12.9 us
    all_to_all x1, waiting for transfers between devices, shards(): lax.all_to_all(jnp.broadcast_to(query_chunk[None], (seq_count,) + query_c...  12.7 us
    all_to_all x1, waiting for transfers between devices, merge_attention(): parts = lax.all_to_all(spread, axis, 0, 0, tiled=True)  11.9 us
  transfers between devices with their start and end apart: 5, of which 4 were waited for; matrix products, arithmetic and copies ran while one was open for 9% of the time, Pallas kernels for 0%

profile of v7, /device:TPU:6, one launch (start us, length us, event | category | flops | bytes accessed | tf_op | source)
XLA Modules:
  0.0 236.7 jit_solution(12223722015755555559)
XLA Ops:
  0.0 1.2 multiply_reduce_fusion.1
  1.2 0.9 bitcast_convert_fusion
  2.9 0.9 fusion.44
  3.8 1.6 fusion.46
  6.2 1.0 reshape.544
  7.9 2.7 %gather_fusion = f32[192,2,64]{2,1,0:T(2,128)S(1)} fusion(f32[32,2,5,64]{3,1,2,0:T(2,128)} %copy.171, s32[192]{0:T(256)S(1)} %bitcast.101), kind=kCustom, calls=%fused_computation.2 | custom fusion | bytes 198144 | tf_op jit(solution)/shard_map/gather | solution.py:176
  11.4 1.0 maximum_bitcast_fusion
  13.3 18.8 %all-to-all-start = ((f32[64,1,544]{2,1,0:T(1,128)}), f32[64,1,544]{2,1,0:T(1,128)S(1)}, u32[]{:S(2)}, u32[]{:S(2)}) async-start(f32[64,1,544]{2,1,0:T(1,128)} %copy.172), calls=%async_computation | async-start | bytes 327680 | tf_op jit(solution)/shard_map/all_to_all | solution.py:186
  32.2 1.1 fusion.2
  33.3 1.3 compare_reduce_fusion
  37.5 2.3 copy.176
  39.8 2.6 %fusion.48 = (bf16[12,128,320]{1,2,0:T(8,128)(2,1)S(1)}, bf16[12,128,320]{1,2,0:T(8,128)(2,1)}) fusion(bf16[12,128,640]{1,2,0:T(8,128)(2,1)} %bitcast.104), kind=kLoop, calls=%fused_computation.140 | loop fusion | bytes 3932160 | tf_op jit(solution)/shard_map/slice | solution.py:220
  43.2 1.9 gather_fusion.4
  45.1 1.5 broadcast_select_fusion
  46.6 2.8 %copy.178 = bf16[5,12,128,64]{3,2,1,0:T(8,128)(2,1)} copy(bf16[5,12,128,64]{2,3,1,0:T(8,128)(2,1)} %get-tuple-element.28) | data formatting | bytes 1966080 | tf_op jit(solution)/shard_map/transpose | solution.py:237
  49.4 1.7 copy.177
  53.4 15.1 %all-to-all-start.1 = ((f32[64,1,160]{2,1,0:T(1,128)}), f32[64,1,160]{2,1,0:T(1,128)S(1)}, u32[]{:S(2)}, u32[]{:S(2)}) async-start(f32[64,1,160]{2,1,0:T(1,128)} %broadcast_in_dim.56), calls=%async_computation.1 | async-start | bytes 131072 | tf_op jit(solution)/shard_map/all_to_all | solution.py:189
  68.7 12.7 %all-to-all-done.1 = f32[64,1,160]{2,1,0:T(1,128)S(1)} async-done(((f32[64,1,160]{2,1,0:T(1,128)}), f32[64,1,160]{2,1,0:T(1,128)S(1)}, u32[]{:S(2)}, u32[]{:S(2)}) %all-to-all-start.1) | async-done | bytes 40992 | tf_op jit(solution)/shard_map/all_to_all | solution.py:189
  83.0 6.3 %shard_map.118 = f32[5,32,128]{2,1,0:T(8,128)} custom-call(bf16[5,32,64]{2,1,0:T(8,128)(2,1)} %maximum_bitcast_fusion.1.q_ref, f32[16,32]{1,0:T(8,128)} %copy.179.owner_t_ref, f32[32,16]{1,0:T(8,128)} %get-tuple-element.17.owner_ref, f32[16,1536]{1,0:T(8,128)} %fusion.4.valid_ref, bf16[5,1536,64]{2,1,0:T(8,128)(2,1)} %bitcast.103, bf16[5,1536,64]{2,1,0:T(8,128)(2,1)} %bitcast.102), custom_call_target="tpu_custom_call" | custom-call | tf_op jit(solution)/shard_map/pallas_call | solution.py:48
  89.2 1.1 fusion.49
  90.3 0.9 copy.182
  93.4 6.4 %all-to-all-start.2 = ((f32[64,1,198]{2,1,0:T(1,128)}), f32[64,1,198]{2,1,0:T(1,128)S(1)}, u32[]{:S(2)}, u32[]{:S(2)}) async-start(f32[64,1,198]{2,1,0:T(1,128)} %reshape.629), calls=%async_computation.2 | async-start | bytes 131072 | tf_op jit(solution)/shard_map/all_to_all | solution.py:122
  100.7 11.9 %all-to-all-done.2 = f32[64,1,198]{2,1,0:T(1,128)S(1)} async-done(((f32[64,1,198]{2,1,0:T(1,128)}), f32[64,1,198]{2,1,0:T(1,128)S(1)}, u32[]{:S(2)}, u32[]{:S(2)}) %all-to-all-start.2) | async-done | bytes 50720 | tf_op jit(solution)/shard_map/all_to_all | solution.py:122
  116.4 6.7 %all-to-all-start.3 = ((f32[64,1,195]{2,1,0:T(1,128)}), f32[64,1,195]{2,1,0:T(1,128)S(1)}, u32[]{:S(2)}, u32[]{:S(2)}) async-start(f32[64,1,195]{2,1,0:T(1,128)} %broadcast_in_dim.64), calls=%async_computation.3 | async-start | bytes 131072 | tf_op jit(solution)/shard_map/all_to_all | solution.py:134
  123.1 12.9 %all-to-all-done.3 = f32[64,1,195]{2,1,0:T(1,128)S(1)} async-done(((f32[64,1,195]{2,1,0:T(1,128)}), f32[64,1,195]{2,1,0:T(1,128)S(1)}, u32[]{:S(2)}, u32[]{:S(2)}) %all-to-all-start.3) | async-done | bytes 49952 | tf_op jit(solution)/shard_map/all_to_all | solution.py:134
  137.0 1.1 broadcast_in_dim.68
  138.2 4.6 %all-to-all-start.4 = ((f32[8,16,2048]{2,1,0:T(8,128)}), f32[8,16,2048]{2,1,0:T(8,128)S(1)}, u32[]{:S(2)}, u32[]{:S(2)}) async-start(f32[8,16,2048]{2,1,0:T(8,128)} %bitcast.29), calls=%async_computation.4 | async-start | bytes 2097152 | tf_op jit(solution)/shard_map/all_to_all | solution.py:260
  143.5 14.6 %all-to-all-done.4 = f32[8,16,2048]{2,1,0:T(8,128)S(1)} async-done(((f32[8,16,2048]{2,1,0:T(8,128)}), f32[8,16,2048]{2,1,0:T(8,128)S(1)}, u32[]{:S(2)}, u32[]{:S(2)}) %all-to-all-start.4) | async-done | bytes 1048608 | tf_op jit(solution)/shard_map/all_to_all | solution.py:260
  158.7 1.0 all_to_all.47
  160.0 38.0 %all_to_all.59 = f32[16,64,125]{2,0,1:T(8,128)S(1)} all-to-all(f32[16,64,125]{2,0,1:T(8,128)S(1)} %copy.196), channel_id=1, replica_groups=mesh['guide'=2,'seq'=64,'tp'=4] {'seq'}, dimensions={1} | all-to-all | bytes 1024000 | tf_op jit(solution)/shard_map/all_to_all | solution.py:98
  198.2 37.2 %all_to_all.60 = f32[64,16,125]{2,1,0:T(8,128)S(1)} all-to-all(f32[64,16,125]{2,1,0:T(8,128)S(1)} %broadcast_in_dim.69), channel_id=1, replica_groups=mesh['guide'=2,'seq'=64,'tp'=4] {'seq'}, dimensions={0} | all-to-all | bytes 1024000 | tf_op jit(solution)/shard_map/all_to_all | solution.py:100
  235.6 1.1 squeeze.22
  (125 shorter events, 21.0 us)
Async XLA Ops:
  0.0 136.7 %copy-start = (bf16[320,2048]{1,0:T(8,128)(2,1)S(1)}, bf16[320,2048]{1,0:T(8,128)(2,1)}, u32[]{:S(2)}) copy-start(bf16[320,2048]{1,0:T(8,128)(2,1)} %param.21) | copy-start | bytes 3932164
  0.0 34.8 %copy-start.1 = (s32[1,32]{1,0:T(1,128)S(1)}, s32[1,32]{1,0:T(1,128)}, u32[]{:S(2)}) copy-start(s32[1,32]{1,0:T(1,128)} %param.24) | copy-start | bytes 388
  5.5 32.1 %copy-start.3 = (bf16[1,12,128,640]{3,2,1,0:T(8,128)(2,1)S(1)}, bf16[1,12,128,640]{3,2,1,0:T(8,128)(2,1)}, u32[]{:S(2)}) copy-start(bf16[1,12,128,640]{3,2,1,0:T(8,128)(2,1)} %param.23) | copy-start | bytes 5898244
  13.3 39.0 %all-to-all-start = ((f32[64,1,544]{2,1,0:T(1,128)}), f32[64,1,544]{2,1,0:T(1,128)S(1)}, u32[]{:S(2)}, u32[]{:S(2)}) async-start(f32[64,1,544]{2,1,0:T(1,128)} %copy.172), calls=%async_computation | async-start | bytes 327680 | tf_op jit(solution)/shard_map/all_to_all | solution.py:186
  46.6 2.8 %copy-start.2 = (bf16[5,12,128,64]{2,3,1,0:T(8,128)(2,1)S(1)}, bf16[5,12,128,64]{2,3,1,0:T(8,128)(2,1)}, u32[]{:S(2)}) copy-start(bf16[5,12,128,64]{2,3,1,0:T(8,128)(2,1)} %get-tuple-element.29) | copy-start | bytes 2949124
  49.4 19.1 %copy-start.7 = (f32[64]{0:T(128)S(1)}, f32[64]{0:T(128)}, u32[]{:S(2)}) copy-start(f32[64]{0:T(128)} %param.18) | copy-start | bytes 772
  49.4 32.5 %copy-start.6 = (f32[64]{0:T(128)S(1)}, f32[64]{0:T(128)}, u32[]{:S(2)}) copy-start(f32[64]{0:T(128)} %param.17) | copy-start | bytes 772
  53.4 28.1 %all-to-all-start.1 = ((f32[64,1,160]{2,1,0:T(1,128)}), f32[64,1,160]{2,1,0:T(1,128)S(1)}, u32[]{:S(2)}, u32[]{:S(2)}) async-start(f32[64,1,160]{2,1,0:T(1,128)} %broadcast_in_dim.56), calls=%async_computation.1 | async-start | bytes 131072 | tf_op jit(solution)/shard_map/all_to_all | solution.py:189
  91.7 45.0 %copy-start.4 = (bf16[1,32,2048]{2,1,0:T(8,128)(2,1)S(1)}, bf16[1,32,2048]{2,1,0:T(8,128)(2,1)}, u32[]{:S(2)}) copy-start(bf16[1,32,2048]{2,1,0:T(8,128)(2,1)} %param.14) | copy-start | bytes 393220
  93.4 19.2 %all-to-all-start.2 = ((f32[64,1,198]{2,1,0:T(1,128)}), f32[64,1,198]{2,1,0:T(1,128)S(1)}, u32[]{:S(2)}, u32[]{:S(2)}) async-start(f32[64,1,198]{2,1,0:T(1,128)} %reshape.629), calls=%async_computation.2 | async-start | bytes 131072 | tf_op jit(solution)/shard_map/all_to_all | solution.py:122
  116.4 19.7 %all-to-all-start.3 = ((f32[64,1,195]{2,1,0:T(1,128)}), f32[64,1,195]{2,1,0:T(1,128)S(1)}, u32[]{:S(2)}, u32[]{:S(2)}) async-start(f32[64,1,195]{2,1,0:T(1,128)} %broadcast_in_dim.64), calls=%async_computation.3 | async-start | bytes 131072 | tf_op jit(solution)/shard_map/all_to_all | solution.py:134
  138.2 20.2 %copy-start.5 = (bf16[32,8000]{1,0:T(8,128)(2,1)S(1)}, bf16[32,8000]{1,0:T(8,128)(2,1)}, u32[]{:S(2)}) copy-start(bf16[32,8000]{1,0:T(8,128)(2,1)} %param.22) | copy-start | bytes 1536004
  138.2 19.9 %all-to-all-start.4 = ((f32[8,16,2048]{2,1,0:T(8,128)}), f32[8,16,2048]{2,1,0:T(8,128)S(1)}, u32[]{:S(2)}, u32[]{:S(2)}) async-start(f32[8,16,2048]{2,1,0:T(8,128)} %bitcast.29), calls=%async_computation.4 | async-start | bytes 2097152 | tf_op jit(solution)/shard_map/all_to_all | solution.py:260

commit v8 on v6

--- a/solution.py
+++ b/solution.py
@@ -176,14 +176,16 @@
     owner_length = jnp.take(lengths, owner_req)
     positions = page_number[:, None] * page_token_count + jnp.arange(page_token_count)[None, :]
     is_valid = slot_live[:, None] & (positions < owner_length[:, None])
-    key_tile = nearby_cache[:, :, : KEY_VALUE_HEADS * HEAD_SIZE].reshape(
-        slot_number, page_token_count, KEY_VALUE_HEADS, HEAD_SIZE
-    )
-    value_tile = nearby_cache[:, :, KEY_VALUE_HEADS * HEAD_SIZE :].reshape(
-        slot_number, page_token_count, KEY_VALUE_HEADS, HEAD_SIZE
-    )
-    key_heads = jnp.take(key_tile, head_mapping, axis=2)
-    value_heads = jnp.take(value_tile, head_mapping, axis=2)
+    first_kv = jnp.minimum(head_mapping[0], KEY_VALUE_HEADS - 2)
+    second = (head_mapping - first_kv)[None, None, :, None] == 1
+    key_pair = lax.dynamic_slice_in_dim(nearby_cache, first_kv * HEAD_SIZE, 2 * HEAD_SIZE, 2)
+    value_pair = lax.dynamic_slice_in_dim(
+        nearby_cache, (KEY_VALUE_HEADS + first_kv) * HEAD_SIZE, 2 * HEAD_SIZE, 2
+    )
+    key_heads = jnp.where(second, key_pair[:, :, None, HEAD_SIZE:], key_pair[:, :, None, :HEAD_SIZE])
+    value_heads = jnp.where(
+        second, value_pair[:, :, None, HEAD_SIZE:], value_pair[:, :, None, :HEAD_SIZE]
+    )
     slot_query = jnp.take(query_rot, owner_req, axis=0)
     scores = (
         jnp.einsum("shd,skhd->shk", slot_query, key_heads, preferred_element_type=jnp.float32)

time: 226 us -> 213 us (0.942)
  local copies, waits for them, and re-layouts: 27.6 us -> 19.3 us
  waiting for transfers between devices: 56.7 us -> 62.9 us
  other arithmetic: 12.3 us -> 8 us
  starting transfers between devices: 46.7 us -> 42.8 us
  matrix products: 5.78 us -> 3.32 us
    all_to_all x1, waiting for transfers between devices: 4.73 us -> 10.9 us  [shards(): summed = jnp.sum(lax.all_to_all(outgoing, 'seq', 0, 0, tiled=True), axis=0)]
    all_to_all x1, starting transfers between devices: 10.4 us -> 6.56 us  [shards(): lax.all_to_all(jnp.broadcast_to(query_chunk[None], (seq_count,) + query_c...]
    unnamed x27 -> x20, local copies, waits for them, and re-layouts: 4.04 us -> 1.14 us
    gather x2 -> x0, local copies, waits for them, and re-layouts: 2.68 us -> none  [the longest x1 1.94 us: shards(): value_heads = jnp.take(value_tile, head_mapping, axis=2)]
  transfers between devices with their start and end apart: 5 -> 5, of which waited for: 5 -> 5; matrix products, arithmetic and copies ran while one was open for 6% -> 4% of each run, Pallas kernels for 0% -> 0%
where the time goes in v8:
time: 213 us; the launch traced here: 212 us
  blocking collectives  75.3 us (35%)
  waiting for transfers between devices  62.9 us (30%)
  starting transfers between devices  42.8 us (20%)
  local copies, waits for them, and re-layouts  19.3 us (9%)
  other arithmetic  8 us (4%)
  matrix products  3.32 us (2%)
    all_to_all x1, blocking collectives, all_reduce_columns(): parts = lax.all_to_all(value, axis, 1, 0, tiled=True)  38 us
    all_to_all x1, blocking collectives, all_reduce_columns(): lax.all_to_all(jnp.broadcast_to(total[None], (count, rows, columns // cou...  37.2 us
    all_to_all x1, starting transfers between devices, shards(): summed = jnp.sum(lax.all_to_all(outgoing, 'seq', 0, 0, tiled=True), axis=0)  18.8 us
    all_to_all x1, waiting for transfers between devices, shards(): incoming = lax.all_to_all(outgoing, ('guide', 'tp'), 0, 0, tiled=True)  14.5 us
    all_to_all x1, waiting for transfers between devices, merge_attention(): lax.all_to_all(jnp.broadcast_to(fraction.reshape(1, -1), (count, fraction...  12.9 us
    all_to_all x1, waiting for transfers between devices, shards(): lax.all_to_all(jnp.broadcast_to(query_chunk[None], (seq_count,) + query_c...  12.5 us
    all_to_all x1, waiting for transfers between devices, merge_attention(): parts = lax.all_to_all(spread, axis, 0, 0, tiled=True)  12.1 us
    all_to_all x1, waiting for transfers between devices, shards(): summed = jnp.sum(lax.all_to_all(outgoing, 'seq', 0, 0, tiled=True), axis=0)  10.9 us
  transfers between devices with their start and end apart: 5, of which 5 were waited for; matrix products, arithmetic and copies ran while one was open for 4% of the time, Pallas kernels for 0%

profile of v8, /device:TPU:6, one launch (start us, length us, event | category | flops | bytes accessed | tf_op | source)
XLA Modules:
  0.0 212.2 jit_solution(13303878497426747023)
XLA Ops:
  0.0 1.0 bitcast_convert_fusion
  1.0 1.0 multiply_reduce_fusion.1
  2.1 0.8 dynamic-slice.2
  2.9 1.0 fusion.64
  4.1 1.8 gather_fusion.1
  6.4 0.8 copy.157
  7.3 18.8 %all-to-all-start = ((f32[64,1,544]{2,1,0:T(1,128)}), f32[64,1,544]{2,1,0:T(1,128)S(1)}, u32[]{:S(2)}, u32[]{:S(2)}) async-start(f32[64,1,544]{2,1,0:T(1,128)} %copy.157), calls=%async_computation | async-start | bytes 327680 | tf_op jit(solution)/shard_map/all_to_all | solution.py:148
  26.2 0.6 compare_reduce_fusion
  27.2 1.7 dynamic-slice_bitcast_fusion.1
  30.3 0.7 gather_fusion
  31.0 0.6 gather_fusion.5
  31.9 10.9 %all-to-all-done = f32[64,1,544]{2,1,0:T(1,128)S(1)} async-done(((f32[64,1,544]{2,1,0:T(1,128)}), f32[64,1,544]{2,1,0:T(1,128)S(1)}, u32[]{:S(2)}, u32[]{:S(2)}) %all-to-all-start) | async-done | bytes 139296 | tf_op jit(solution)/shard_map/all_to_all | solution.py:148
  43.0 0.7 broadcast_in_dim.205
  43.7 6.6 %all-to-all-start.1 = ((f32[64,1,160]{2,1,0:T(1,128)}), f32[64,1,160]{2,1,0:T(1,128)S(1)}, u32[]{:S(2)}, u32[]{:S(2)}) async-start(f32[64,1,160]{2,1,0:T(1,128)} %broadcast_in_dim.205), calls=%async_computation.1 | async-start | bytes 131072 | tf_op jit(solution)/shard_map/all_to_all | solution.py:151
  50.7 12.5 %all-to-all-done.1 = f32[64,1,160]{2,1,0:T(1,128)S(1)} async-done(((f32[64,1,160]{2,1,0:T(1,128)}), f32[64,1,160]{2,1,0:T(1,128)S(1)}, u32[]{:S(2)}, u32[]{:S(2)}) %all-to-all-start.1) | async-done | bytes 40992 | tf_op jit(solution)/shard_map/all_to_all | solution.py:151
  63.9 0.6 gather_fusion.2
  66.3 0.7 fusion
  68.2 0.8 reshape.634
  69.0 6.6 %all-to-all-start.2 = ((f32[64,1,198]{2,1,0:T(1,128)}), f32[64,1,198]{2,1,0:T(1,128)S(1)}, u32[]{:S(2)}, u32[]{:S(2)}) async-start(f32[64,1,198]{2,1,0:T(1,128)} %reshape.634), calls=%async_computation.2 | async-start | bytes 131072 | tf_op jit(solution)/shard_map/all_to_all | solution.py:84
  76.5 12.1 %all-to-all-done.2 = f32[64,1,198]{2,1,0:T(1,128)S(1)} async-done(((f32[64,1,198]{2,1,0:T(1,128)}), f32[64,1,198]{2,1,0:T(1,128)S(1)}, u32[]{:S(2)}, u32[]{:S(2)}) %all-to-all-start.2) | async-done | bytes 50720 | tf_op jit(solution)/shard_map/all_to_all | solution.py:84
  89.0 0.8 reduce.14
  91.6 0.7 broadcast_in_dim.221
  92.3 6.4 %all-to-all-start.3 = ((f32[64,1,195]{2,1,0:T(1,128)}), f32[64,1,195]{2,1,0:T(1,128)S(1)}, u32[]{:S(2)}, u32[]{:S(2)}) async-start(f32[64,1,195]{2,1,0:T(1,128)} %broadcast_in_dim.221), calls=%async_computation.3 | async-start | bytes 131072 | tf_op jit(solution)/shard_map/all_to_all | solution.py:96
  98.7 12.9 %all-to-all-done.3 = f32[64,1,195]{2,1,0:T(1,128)S(1)} async-done(((f32[64,1,195]{2,1,0:T(1,128)}), f32[64,1,195]{2,1,0:T(1,128)S(1)}, u32[]{:S(2)}, u32[]{:S(2)}) %all-to-all-start.3) | async-done | bytes 49952 | tf_op jit(solution)/shard_map/all_to_all | solution.py:96
  112.6 1.1 broadcast_in_dim.224
  113.7 4.5 %all-to-all-start.4 = ((f32[8,16,2048]{2,1,0:T(8,128)}), f32[8,16,2048]{2,1,0:T(8,128)S(1)}, u32[]{:S(2)}, u32[]{:S(2)}) async-start(f32[8,16,2048]{2,1,0:T(8,128)} %bitcast.23), calls=%async_computation.4 | async-start | bytes 2097152 | tf_op jit(solution)/shard_map/all_to_all | solution.py:226
  118.2 0.8 dynamic-slice.3
  119.0 14.5 %all-to-all-done.4 = f32[8,16,2048]{2,1,0:T(8,128)S(1)} async-done(((f32[8,16,2048]{2,1,0:T(8,128)}), f32[8,16,2048]{2,1,0:T(8,128)S(1)}, u32[]{:S(2)}, u32[]{:S(2)}) %all-to-all-start.4) | async-done | bytes 1048608 | tf_op jit(solution)/shard_map/all_to_all | solution.py:226
  134.2 1.0 all_to_all.47
  135.5 38.0 %all_to_all.59 = f32[16,64,125]{2,0,1:T(8,128)S(1)} all-to-all(f32[16,64,125]{2,0,1:T(8,128)S(1)} %copy.178), channel_id=1, replica_groups=mesh['guide'=2,'seq'=64,'tp'=4] {'seq'}, dimensions={1} | all-to-all | bytes 1024000 | tf_op jit(solution)/shard_map/all_to_all | solution.py:60
  173.6 37.2 %all_to_all.60 = f32[64,16,125]{2,1,0:T(8,128)S(1)} all-to-all(f32[64,16,125]{2,1,0:T(8,128)S(1)} %broadcast_in_dim.225), channel_id=1, replica_groups=mesh['guide'=2,'seq'=64,'tp'=4] {'seq'}, dimensions={0} | all-to-all | bytes 1024000 | tf_op jit(solution)/shard_map/all_to_all | solution.py:62
  211.0 1.1 squeeze.20
  (121 shorter events, 12.3 us)
Async XLA Ops:
  0.0 112.3 %copy-start = (bf16[320,2048]{1,0:T(8,128)(2,1)S(1)}, bf16[320,2048]{1,0:T(8,128)(2,1)}, u32[]{:S(2)}) copy-start(bf16[320,2048]{1,0:T(8,128)(2,1)} %param.19) | copy-start | bytes 3932164
  0.0 6.1 %copy-start.5 = (bf16[32,320]{1,0:T(8,128)(2,1)S(1)}, bf16[32,320]{1,0:T(8,128)(2,1)}, u32[]{:S(2)}) copy-start(bf16[32,320]{1,0:T(8,128)(2,1)} %param.17) | copy-start | bytes 61444
  3.8 22.4 %copy-start.4 = (s32[1,32,128]{2,1,0:T(8,128)S(1)}, s32[1,32,128]{2,1,0:T(8,128)}, u32[]{:S(2)}) copy-start(s32[1,32,128]{2,1,0:T(8,128)} %param.23) | copy-start | bytes 49156
  7.3 35.5 %all-to-all-start = ((f32[64,1,544]{2,1,0:T(1,128)}), f32[64,1,544]{2,1,0:T(1,128)S(1)}, u32[]{:S(2)}, u32[]{:S(2)}) async-start(f32[64,1,544]{2,1,0:T(1,128)} %copy.157), calls=%async_computation | async-start | bytes 327680 | tf_op jit(solution)/shard_map/all_to_all | solution.py:148
  29.3 0.8 copy-start.1
  29.7 20.8 %copy-start.7 = (f32[64]{0:T(128)S(1)}, f32[64]{0:T(128)}, u32[]{:S(2)}) copy-start(f32[64]{0:T(128)} %param.16) | copy-start | bytes 772
  29.9 33.6 %copy-start.6 = (f32[64]{0:T(128)S(1)}, f32[64]{0:T(128)}, u32[]{:S(2)}) copy-start(f32[64]{0:T(128)} %param.15) | copy-start | bytes 772
  43.7 19.5 %all-to-all-start.1 = ((f32[64,1,160]{2,1,0:T(1,128)}), f32[64,1,160]{2,1,0:T(1,128)S(1)}, u32[]{:S(2)}, u32[]{:S(2)}) async-start(f32[64,1,160]{2,1,0:T(1,128)} %broadcast_in_dim.205), calls=%async_computation.1 | async-start | bytes 131072 | tf_op jit(solution)/shard_map/all_to_all | solution.py:151
  69.0 43.3 %copy-start.2 = (bf16[1,32,2048]{2,1,0:T(8,128)(2,1)S(1)}, bf16[1,32,2048]{2,1,0:T(8,128)(2,1)}, u32[]{:S(2)}) copy-start(bf16[1,32,2048]{2,1,0:T(8,128)(2,1)} %param.12) | copy-start | bytes 393220
  69.0 19.5 %all-to-all-start.2 = ((f32[64,1,198]{2,1,0:T(1,128)}), f32[64,1,198]{2,1,0:T(1,128)S(1)}, u32[]{:S(2)}, u32[]{:S(2)}) async-start(f32[64,1,198]{2,1,0:T(1,128)} %reshape.634), calls=%async_computation.2 | async-start | bytes 131072 | tf_op jit(solution)/shard_map/all_to_all | solution.py:84
  92.3 19.3 %all-to-all-start.3 = ((f32[64,1,195]{2,1,0:T(1,128)}), f32[64,1,195]{2,1,0:T(1,128)S(1)}, u32[]{:S(2)}, u32[]{:S(2)}) async-start(f32[64,1,195]{2,1,0:T(1,128)} %broadcast_in_dim.221), calls=%async_computation.3 | async-start | bytes 131072 | tf_op jit(solution)/shard_map/all_to_all | solution.py:96
  113.7 19.8 %all-to-all-start.4 = ((f32[8,16,2048]{2,1,0:T(8,128)}), f32[8,16,2048]{2,1,0:T(8,128)S(1)}, u32[]{:S(2)}, u32[]{:S(2)}) async-start(f32[8,16,2048]{2,1,0:T(8,128)} %bitcast.23), calls=%async_computation.4 | async-start | bytes 2097152 | tf_op jit(solution)/shard_map/all_to_all | solution.py:226
  118.2 15.6 %copy-start.3 = (bf16[32,8000]{1,0:T(8,128)(2,1)S(1)}, bf16[32,8000]{1,0:T(8,128)(2,1)}, u32[]{:S(2)}) copy-start(bf16[32,8000]{1,0:T(8,128)(2,1)} %param.20) | copy-start | bytes 1536004

commit v9 on v8

--- a/solution.py
+++ b/solution.py
@@ -1,6 +1,7 @@
 import jax
 import jax.numpy as jnp
 from jax import lax
+from jax.experimental import pallas as pl
 from jax.sharding import PartitionSpec as P
 
 QUERY_HEADS = 20
@@ -11,6 +12,25 @@
 GUIDE_WEIGHT = 2.5
 NORM_EPS = 1e-06
 NEG_FILL = -1e30
+
+
+def project_kernel(rows_ref, weight_ref, out_ref):
+    out_ref[...] = jnp.dot(rows_ref[...], weight_ref[...], preferred_element_type=jnp.float32)
+
+
+def project(rows, weight, block=512):
+    count, depth = rows.shape
+    width = weight.shape[1]
+    return pl.pallas_call(
+        project_kernel,
+        grid=(width // block,),
+        in_specs=[
+            pl.BlockSpec((count, depth), lambda j: (0, 0)),
+            pl.BlockSpec((depth, block), lambda j: (0, j)),
+        ],
+        out_specs=pl.BlockSpec((count, block), lambda j: (0, j)),
+        out_shape=jax.ShapeDtypeStruct((count, width), jnp.float32),
+    )(rows, weight)
 
 
 def norm_rows(token_rows, scale_gain):
@@ -215,7 +235,7 @@
         own_value,
         "seq",
     ).reshape(request_number, nearby_heads * HEAD_SIZE)
-    output_part = jnp.dot(attended, output_weight, preferred_element_type=jnp.float32)
+    output_part = project(attended, output_weight)
     output_part = output_part + jnp.where(lax.axis_index("tp") == 0, token_rows, 0.0)
     guide_count = lax.axis_size("guide")
     tp_count = lax.axis_size("tp")
@@ -228,7 +248,7 @@
     final_rows = norm_rows(residual, final_gain)
     final_part = lax.dynamic_slice_in_dim(final_rows, shard_index * part_width, part_width, 2)
     both = final_part.reshape(guide_count * half_rows, part_width)
-    logit_part = jnp.dot(both, head_weight, preferred_element_type=jnp.float32)
+    logit_part = project(both, head_weight, block=head_weight.shape[1])
     conditional_part = logit_part[:half_rows]
     unconditional_part = logit_part[half_rows:]
     guided_part = unconditional_part + GUIDE_WEIGHT * (conditional_part - unconditional_part)

time: 213 us -> 221 us (1.038)
  Pallas kernels: 0 us -> 5.88 us
  other arithmetic: 8 us -> 10.7 us
    pallas_call x0 -> x2, Pallas kernels: none -> 5.88 us  [project(): pl.pallas_call(project_kernel, grid=(width // block,), in_specs=[pl.Block...]
  transfers between devices with their start and end apart: 5 -> 5, of which waited for: 5 -> 5; matrix products, arithmetic and copies ran while one was open for 4% -> 3% of each run, Pallas kernels for 0% -> 0%
where the time goes in v9:
time: 221 us; the launch traced here: 220 us
  blocking collectives  75.3 us (34%)
  waiting for transfers between devices  63 us (29%)
  starting transfers between devices  42.7 us (19%)
  local copies, waits for them, and re-layouts  19.8 us (9%)
  other arithmetic  10.7 us (5%)
  Pallas kernels  5.88 us (3%)
    all_to_all x1, blocking collectives, all_reduce_columns(): parts = lax.all_to_all(value, axis, 1, 0, tiled=True)  38 us
    all_to_all x1, blocking collectives, all_reduce_columns(): lax.all_to_all(jnp.broadcast_to(total[None], (count, rows, columns // cou...  37.2 us
    all_to_all x1, starting transfers between devices, shards(): summed = jnp.sum(lax.all_to_all(outgoing, 'seq', 0, 0, tiled=True), axis=0)  18.8 us
    all_to_all x1, waiting for transfers between devices, shards(): incoming = lax.all_to_all(outgoing, ('guide', 'tp'), 0, 0, tiled=True)  14.6 us
    all_to_all x1, waiting for transfers between devices, merge_attention(): lax.all_to_all(jnp.broadcast_to(fraction.reshape(1, -1), (count, fraction...  12.9 us
    all_to_all x1, waiting for transfers between devices, shards(): lax.all_to_all(jnp.broadcast_to(query_chunk[None], (seq_count,) + query_c...  12.5 us
    all_to_all x1, waiting for transfers between devices, merge_attention(): parts = lax.all_to_all(spread, axis, 0, 0, tiled=True)  12.1 us
    all_to_all x1, waiting for transfers between devices, shards(): summed = jnp.sum(lax.all_to_all(outgoing, 'seq', 0, 0, tiled=True), axis=0)  10.9 us
  transfers between devices with their start and end apart: 5, of which 5 were waited for; matrix products, arithmetic and copies ran while one was open for 3% of the time, Pallas kernels for 0%

profile of v9, /device:TPU:6, one launch (start us, length us, event | category | flops | bytes accessed | tf_op | source)
XLA Modules:
  0.0 219.8 jit_solution(4286365742642309377)
XLA Ops:
  0.0 1.0 bitcast_convert_fusion
  1.0 1.0 multiply_reduce_fusion.1
  2.0 0.8 dynamic-slice.2
  3.2 1.8 gather_fusion.1
  5.6 0.8 copy.157
  6.5 18.8 %all-to-all-start = ((f32[64,1,544]{2,1,0:T(1,128)}), f32[64,1,544]{2,1,0:T(1,128)S(1)}, u32[]{:S(2)}, u32[]{:S(2)}) async-start(f32[64,1,544]{2,1,0:T(1,128)} %copy.157), calls=%async_computation | async-start | bytes 327680 | tf_op jit(solution)/shard_map/all_to_all | solution.py:168
  26.3 1.7 dynamic-slice_bitcast_fusion.1
  31.1 10.9 %all-to-all-done = f32[64,1,544]{2,1,0:T(1,128)S(1)} async-done(((f32[64,1,544]{2,1,0:T(1,128)}), f32[64,1,544]{2,1,0:T(1,128)S(1)}, u32[]{:S(2)}, u32[]{:S(2)}) %all-to-all-start) | async-done | bytes 139296 | tf_op jit(solution)/shard_map/all_to_all | solution.py:168
  42.9 6.6 %all-to-all-start.1 = ((f32[64,1,160]{2,1,0:T(1,128)}), f32[64,1,160]{2,1,0:T(1,128)S(1)}, u32[]{:S(2)}, u32[]{:S(2)}) async-start(f32[64,1,160]{2,1,0:T(1,128)} %broadcast_in_dim.205), calls=%async_computation.1 | async-start | bytes 131072 | tf_op jit(solution)/shard_map/all_to_all | solution.py:171
  49.9 12.5 %all-to-all-done.1 = f32[64,1,160]{2,1,0:T(1,128)S(1)} async-done(((f32[64,1,160]{2,1,0:T(1,128)}), f32[64,1,160]{2,1,0:T(1,128)S(1)}, u32[]{:S(2)}, u32[]{:S(2)}) %all-to-all-start.1) | async-done | bytes 40992 | tf_op jit(solution)/shard_map/all_to_all | solution.py:171
  65.5 0.7 fusion
  67.4 0.8 reshape.634
  68.2 6.5 %all-to-all-start.2 = ((f32[64,1,198]{2,1,0:T(1,128)}), f32[64,1,198]{2,1,0:T(1,128)S(1)}, u32[]{:S(2)}, u32[]{:S(2)}) async-start(f32[64,1,198]{2,1,0:T(1,128)} %reshape.634), calls=%async_computation.2 | async-start | bytes 131072 | tf_op jit(solution)/shard_map/all_to_all | solution.py:104
  75.5 12.1 %all-to-all-done.2 = f32[64,1,198]{2,1,0:T(1,128)S(1)} async-done(((f32[64,1,198]{2,1,0:T(1,128)}), f32[64,1,198]{2,1,0:T(1,128)S(1)}, u32[]{:S(2)}, u32[]{:S(2)}) %all-to-all-start.2) | async-done | bytes 50720 | tf_op jit(solution)/shard_map/all_to_all | solution.py:104
  88.1 0.8 reduce.14
  90.7 0.7 broadcast_in_dim.221
  91.3 6.4 %all-to-all-start.3 = ((f32[64,1,195]{2,1,0:T(1,128)}), f32[64,1,195]{2,1,0:T(1,128)S(1)}, u32[]{:S(2)}, u32[]{:S(2)}) async-start(f32[64,1,195]{2,1,0:T(1,128)} %broadcast_in_dim.221), calls=%async_computation.3 | async-start | bytes 131072 | tf_op jit(solution)/shard_map/all_to_all | solution.py:116
  97.7 12.9 %all-to-all-done.3 = f32[64,1,195]{2,1,0:T(1,128)S(1)} async-done(((f32[64,1,195]{2,1,0:T(1,128)}), f32[64,1,195]{2,1,0:T(1,128)S(1)}, u32[]{:S(2)}, u32[]{:S(2)}) %all-to-all-start.3) | async-done | bytes 49952 | tf_op jit(solution)/shard_map/all_to_all | solution.py:116
  111.2 0.7 reshape.563.rows_ref
  111.9 3.6 %shard_map.118 = f32[32,2048]{1,0:T(8,128)} custom-call(bf16[32,320]{1,0:T(8,128)(2,1)} %reshape.563.rows_ref, bf16[320,2048]{1,0:T(8,128)(2,1)} %weight_ref.2), custom_call_target="tpu_custom_call" | custom-call | tf_op jit(solution)/shard_map/pallas_call | solution.py:24
  115.5 1.0 select_add_fusion
  116.5 1.1 broadcast_in_dim.224
  117.5 4.5 %all-to-all-start.4 = ((f32[8,16,2048]{2,1,0:T(8,128)}), f32[8,16,2048]{2,1,0:T(8,128)S(1)}, u32[]{:S(2)}, u32[]{:S(2)}) async-start(f32[8,16,2048]{2,1,0:T(8,128)} %bitcast.23), calls=%async_computation.4 | async-start | bytes 2097152 | tf_op jit(solution)/shard_map/all_to_all | solution.py:246
  122.0 0.8 dynamic-slice.3
  122.8 14.6 %all-to-all-done.4 = f32[8,16,2048]{2,1,0:T(8,128)S(1)} async-done(((f32[8,16,2048]{2,1,0:T(8,128)}), f32[8,16,2048]{2,1,0:T(8,128)S(1)}, u32[]{:S(2)}, u32[]{:S(2)}) %all-to-all-start.4) | async-done | bytes 1048608 | tf_op jit(solution)/shard_map/all_to_all | solution.py:246
  137.5 0.7 fusion.23
  138.2 2.3 %shard_map.119 = f32[32,8000]{1,0:T(8,128)} custom-call(bf16[32,32]{1,0:T(8,128)(2,1)} %bitcast.88, bf16[32,8000]{1,0:T(8,128)(2,1)} %weight_ref.3), custom_call_target="tpu_custom_call" | custom-call | tf_op jit(solution)/shard_map/pallas_call | solution.py:24
  140.5 1.2 fusion.7
  141.8 1.0 all_to_all.47
  143.1 38.0 %all_to_all.59 = f32[16,64,125]{2,0,1:T(8,128)S(1)} all-to-all(f32[16,64,125]{2,0,1:T(8,128)S(1)} %copy.178), channel_id=1, replica_groups=mesh['guide'=2,'seq'=64,'tp'=4] {'seq'}, dimensions={1} | all-to-all | bytes 1024000 | tf_op jit(solution)/shard_map/all_to_all | solution.py:80
  181.3 37.2 %all_to_all.60 = f32[64,16,125]{2,1,0:T(8,128)S(1)} all-to-all(f32[64,16,125]{2,1,0:T(8,128)S(1)} %broadcast_in_dim.225), channel_id=1, replica_groups=mesh['guide'=2,'seq'=64,'tp'=4] {'seq'}, dimensions={0} | all-to-all | bytes 1024000 | tf_op jit(solution)/shard_map/all_to_all | solution.py:82
  218.7 1.1 squeeze.20
  (120 shorter events, 14.8 us)
Async XLA Ops:
  0.0 2.8 %copy-start = (bf16[32,640]{1,0:T(8,128)(2,1)S(1)}, bf16[32,640]{1,0:T(8,128)(2,1)}, u32[]{:S(2)}) copy-start(bf16[32,640]{1,0:T(8,128)(2,1)} %param.18) | copy-start | bytes 122884
  0.0 5.2 %copy-start.4 = (bf16[32,320]{1,0:T(8,128)(2,1)S(1)}, bf16[32,320]{1,0:T(8,128)(2,1)}, u32[]{:S(2)}) copy-start(bf16[32,320]{1,0:T(8,128)(2,1)} %param.17) | copy-start | bytes 61444
  0.0 25.4 %copy-start.3 = (s32[1,32,128]{2,1,0:T(8,128)S(1)}, s32[1,32,128]{2,1,0:T(8,128)}, u32[]{:S(2)}) copy-start(s32[1,32,128]{2,1,0:T(8,128)} %param.23) | copy-start | bytes 49156
  6.5 35.5 %all-to-all-start = ((f32[64,1,544]{2,1,0:T(1,128)}), f32[64,1,544]{2,1,0:T(1,128)S(1)}, u32[]{:S(2)}, u32[]{:S(2)}) async-start(f32[64,1,544]{2,1,0:T(1,128)} %copy.157), calls=%async_computation | async-start | bytes 327680 | tf_op jit(solution)/shard_map/all_to_all | solution.py:168
  28.4 0.8 copy-start.1
  28.5 21.2 %copy-start.6 = (f32[64]{0:T(128)S(1)}, f32[64]{0:T(128)}, u32[]{:S(2)}) copy-start(f32[64]{0:T(128)} %param.16) | copy-start | bytes 772
  28.7 34.0 %copy-start.5 = (f32[64]{0:T(128)S(1)}, f32[64]{0:T(128)}, u32[]{:S(2)}) copy-start(f32[64]{0:T(128)} %param.15) | copy-start | bytes 772
  42.9 19.5 %all-to-all-start.1 = ((f32[64,1,160]{2,1,0:T(1,128)}), f32[64,1,160]{2,1,0:T(1,128)S(1)}, u32[]{:S(2)}, u32[]{:S(2)}) async-start(f32[64,1,160]{2,1,0:T(1,128)} %broadcast_in_dim.205), calls=%async_computation.1 | async-start | bytes 131072 | tf_op jit(solution)/shard_map/all_to_all | solution.py:171
  68.2 19.4 %all-to-all-start.2 = ((f32[64,1,198]{2,1,0:T(1,128)}), f32[64,1,198]{2,1,0:T(1,128)S(1)}, u32[]{:S(2)}, u32[]{:S(2)}) async-start(f32[64,1,198]{2,1,0:T(1,128)} %reshape.634), calls=%async_computation.2 | async-start | bytes 131072 | tf_op jit(solution)/shard_map/all_to_all | solution.py:104
  74.7 40.7 %copy-start.2 = (bf16[1,32,2048]{2,1,0:T(8,128)(2,1)S(1)}, bf16[1,32,2048]{2,1,0:T(8,128)(2,1)}, u32[]{:S(2)}) copy-start(bf16[1,32,2048]{2,1,0:T(8,128)(2,1)} %param.12) | copy-start | bytes 393220
  91.3 19.3 %all-to-all-start.3 = ((f32[64,1,195]{2,1,0:T(1,128)}), f32[64,1,195]{2,1,0:T(1,128)S(1)}, u32[]{:S(2)}, u32[]{:S(2)}) async-start(f32[64,1,195]{2,1,0:T(1,128)} %broadcast_in_dim.221), calls=%async_computation.3 | async-start | bytes 131072 | tf_op jit(solution)/shard_map/all_to_all | solution.py:116
  117.5 19.8 %all-to-all-start.4 = ((f32[8,16,2048]{2,1,0:T(8,128)}), f32[8,16,2048]{2,1,0:T(8,128)S(1)}, u32[]{:S(2)}, u32[]{:S(2)}) async-start(f32[8,16,2048]{2,1,0:T(8,128)} %bitcast.23), calls=%async_computation.4 | async-start | bytes 2097152 | tf_op jit(solution)/shard_map/all_to_all | solution.py:246

commit v10 on v5

--- a/solution.py
+++ b/solution.py
@@ -167,14 +167,16 @@
     owner_length = jnp.take(lengths, owner_req)
     positions = page_number[:, None] * page_token_count + jnp.arange(page_token_count)[None, :]
     is_valid = slot_live[:, None] & (positions < owner_length[:, None])
-    key_tile = nearby_cache[:, :, : KEY_VALUE_HEADS * HEAD_SIZE].reshape(
-        slot_number, page_token_count, KEY_VALUE_HEADS, HEAD_SIZE
-    )
-    value_tile = nearby_cache[:, :, KEY_VALUE_HEADS * HEAD_SIZE :].reshape(
-        slot_number, page_token_count, KEY_VALUE_HEADS, HEAD_SIZE
-    )
-    key_heads = jnp.take(key_tile, head_mapping, axis=2)
-    value_heads = jnp.take(value_tile, head_mapping, axis=2)
+    first_kv = jnp.minimum(head_mapping[0], KEY_VALUE_HEADS - 2)
+    second = (head_mapping - first_kv)[None, None, :, None] == 1
+    key_pair = lax.dynamic_slice_in_dim(nearby_cache, first_kv * HEAD_SIZE, 2 * HEAD_SIZE, 2)
+    value_pair = lax.dynamic_slice_in_dim(
+        nearby_cache, (KEY_VALUE_HEADS + first_kv) * HEAD_SIZE, 2 * HEAD_SIZE, 2
+    )
+    key_heads = jnp.where(second, key_pair[:, :, None, HEAD_SIZE:], key_pair[:, :, None, :HEAD_SIZE])
+    value_heads = jnp.where(
+        second, value_pair[:, :, None, HEAD_SIZE:], value_pair[:, :, None, :HEAD_SIZE]
+    )
     slot_query = jnp.take(query_rot, owner_req, axis=0)
     scores = (
         jnp.einsum("shd,skhd->shk", slot_query, key_heads, preferred_element_type=jnp.float32)

time: 229 us -> 213 us (0.930)
  other arithmetic: 21.4 us -> 9.49 us
  waiting for transfers between devices: 51.6 us -> 63.3 us
  starting transfers between devices: 51.6 us -> 42.7 us
  local copies, waits for them, and re-layouts: 23.7 us -> 18.3 us
    all_to_all x1, waiting for transfers between devices: 0.01 us -> 10.5 us  [shards(): lax.all_to_all(unit_part.reshape(seq_count, -1), 'seq', 0, 0, tiled=True)]
    all_to_all x1, starting transfers between devices: 15.1 us -> 6.56 us  [shards(): lax.all_to_all(jnp.broadcast_to(summed[None, :, 0], (seq_count, unit_per,...]
    gather x2 -> x0, local copies, waits for them, and re-layouts: 3.4 us -> none  [the longest x1 1.71 us: shards(): value_heads = jnp.take(value_tile, head_mapping, axis=2)]
    select_n x1 -> x0, other arithmetic: 2.76 us -> none  [shards(): key_heads = jnp.take(key_tile, head_mapping, axis=2)]
    unnamed x51 -> x28, local copies, waits for them, and re-layouts: 5.48 us -> 3.13 us
  transfers between devices with their start and end apart: 5 -> 5, of which waited for: 4 -> 5; matrix products, arithmetic and copies ran while one was open for 8% -> 3% of each run, Pallas kernels for 0% -> 0%
where the time goes in v10:
time: 213 us
  blocking collectives  75.3 us (35%)
  waiting for transfers between devices  63.3 us (30%)
  starting transfers between devices  42.7 us (20%)
  local copies, waits for them, and re-layouts  18.3 us (9%)
  other arithmetic  9.49 us (4%)
  matrix products  2.29 us (1%)
    all_to_all x1, blocking collectives, all_reduce(): parts = lax.all_to_all(flat.reshape(count, chunk), axis, 0, 0, tiled=True)  38 us
    all_to_all x1, blocking collectives, all_reduce(): lax.all_to_all(jnp.broadcast_to(total, (count, chunk)), axis, 0, 0, tiled...  37.3 us
    all_to_all x1, starting transfers between devices, shards(): lax.all_to_all(unit_part.reshape(seq_count, -1), 'seq', 0, 0, tiled=True)  18.8 us
    all_to_all x1, waiting for transfers between devices, shards(): incoming = lax.all_to_all(outgoing, ('guide', 'tp'), 0, 0, tiled=True)  14.5 us
    all_to_all x1, waiting for transfers between devices, merge_attention(): lax.all_to_all(jnp.broadcast_to(fraction[None], (count,) + fraction.shape...  12.9 us
    all_to_all x1, waiting for transfers between devices, merge_attention(): parts = lax.all_to_all(spread, axis, 0, 0, tiled=True)  12.9 us
    all_to_all x1, waiting for transfers between devices, shards(): lax.all_to_all(jnp.broadcast_to(summed[None, :, 0], (seq_count, unit_per,...  12.5 us
    all_to_all x1, waiting for transfers between devices, shards(): lax.all_to_all(unit_part.reshape(seq_count, -1), 'seq', 0, 0, tiled=True)  10.5 us
  transfers between devices with their start and end apart: 5, of which 5 were waited for; matrix products, arithmetic and copies ran while one was open for 3% of the time, Pallas kernels for 0%

profile of v10, /device:TPU:6, one launch (start us, length us, event | category | flops | bytes accessed | tf_op | source)
XLA Modules:
  0.0 212.7 jit_solution(8789326545336204349)
XLA Ops:
  0.0 1.0 bitcast_convert_fusion
  1.1 1.0 multiply_reduce_fusion.1
  2.1 0.9 fusion.53
  5.0 0.8 dynamic-slice.6
  6.0 0.9 all_to_all.37
  6.9 18.8 %all-to-all-start = ((f32[64,1,576]{2,1,0:T(1,128)}), f32[64,1,576]{2,1,0:T(1,128)S(1)}, u32[]{:S(2)}, u32[]{:S(2)}) async-start(f32[64,1,576]{2,1,0:T(1,128)} %all_to_all.37), calls=%async_computation | async-start | bytes 327680 | tf_op jit(solution)/shard_map/all_to_all | solution.py:143
  25.7 0.6 compare_reduce_fusion
  26.9 1.7 dynamic-slice_bitcast_fusion.1
  29.0 0.7 gather_fusion
  29.7 0.6 constant_dynamic-slice_fusion
  32.0 10.5 %all-to-all-done = f32[64,1,576]{2,1,0:T(1,128)S(1)} async-done(((f32[64,1,576]{2,1,0:T(1,128)}), f32[64,1,576]{2,1,0:T(1,128)S(1)}, u32[]{:S(2)}, u32[]{:S(2)}) %all-to-all-start) | async-done | bytes 147488 | tf_op jit(solution)/shard_map/all_to_all | solution.py:143
  42.8 0.8 reshape.633
  43.6 6.6 %all-to-all-start.1 = ((f32[64,1,192]{2,1,0:T(1,128)}), f32[64,1,192]{2,1,0:T(1,128)S(1)}, u32[]{:S(2)}, u32[]{:S(2)}) async-start(f32[64,1,192]{2,1,0:T(1,128)} %reshape.633), calls=%async_computation.1 | async-start | bytes 131072 | tf_op jit(solution)/shard_map/all_to_all | solution.py:145
  50.5 12.5 %all-to-all-done.1 = f32[64,1,192]{2,1,0:T(1,128)S(1)} async-done(((f32[64,1,192]{2,1,0:T(1,128)}), f32[64,1,192]{2,1,0:T(1,128)S(1)}, u32[]{:S(2)}, u32[]{:S(2)}) %all-to-all-start.1) | async-done | bytes 49184 | tf_op jit(solution)/shard_map/all_to_all | solution.py:145
  63.0 0.6 broadcast.547
  63.6 0.8 reduce.7
  67.3 0.7 fusion
  69.1 0.8 reshape.635
  69.9 6.5 %all-to-all-start.2 = ((f32[64,1,198]{2,1,0:T(1,128)}), f32[64,1,198]{2,1,0:T(1,128)S(1)}, u32[]{:S(2)}, u32[]{:S(2)}) async-start(f32[64,1,198]{2,1,0:T(1,128)} %reshape.635), calls=%async_computation.2 | async-start | bytes 131072 | tf_op jit(solution)/shard_map/all_to_all | solution.py:73
  76.4 12.9 %all-to-all-done.2 = f32[64,1,198]{2,1,0:T(1,128)S(1)} async-done(((f32[64,1,198]{2,1,0:T(1,128)}), f32[64,1,198]{2,1,0:T(1,128)S(1)}, u32[]{:S(2)}, u32[]{:S(2)}) %all-to-all-start.2) | async-done | bytes 50720 | tf_op jit(solution)/shard_map/all_to_all | solution.py:73
  89.3 0.8 reduce.8
  91.9 0.8 reshape.637
  92.7 6.4 %all-to-all-start.3 = ((f32[64,1,195]{2,1,0:T(1,128)}), f32[64,1,195]{2,1,0:T(1,128)S(1)}, u32[]{:S(2)}, u32[]{:S(2)}) async-start(f32[64,1,195]{2,1,0:T(1,128)} %reshape.637), calls=%async_computation.3 | async-start | bytes 131072 | tf_op jit(solution)/shard_map/all_to_all | solution.py:85
  99.1 12.9 %all-to-all-done.3 = f32[64,1,195]{2,1,0:T(1,128)S(1)} async-done(((f32[64,1,195]{2,1,0:T(1,128)}), f32[64,1,195]{2,1,0:T(1,128)S(1)}, u32[]{:S(2)}, u32[]{:S(2)}) %all-to-all-start.3) | async-done | bytes 49952 | tf_op jit(solution)/shard_map/all_to_all | solution.py:85
  112.0 0.8 reduce.9
  114.0 1.1 broadcast_in_dim.242
  115.1 4.5 %all-to-all-start.4 = ((f32[8,16,2048]{2,1,0:T(8,128)}), f32[8,16,2048]{2,1,0:T(8,128)S(1)}, u32[]{:S(2)}, u32[]{:S(2)}) async-start(f32[8,16,2048]{2,1,0:T(8,128)} %bitcast.33), calls=%async_computation.4 | async-start | bytes 2097152 | tf_op jit(solution)/shard_map/all_to_all | solution.py:217
  119.6 0.8 dynamic-slice.7
  120.4 14.5 %all-to-all-done.4 = f32[8,16,2048]{2,1,0:T(8,128)S(1)} async-done(((f32[8,16,2048]{2,1,0:T(8,128)}), f32[8,16,2048]{2,1,0:T(8,128)S(1)}, u32[]{:S(2)}, u32[]{:S(2)}) %all-to-all-start.4) | async-done | bytes 1048608 | tf_op jit(solution)/shard_map/all_to_all | solution.py:217
  135.8 38.0 %all_to_all.45 = f32[64,1,2048]{2,1,0:T(1,128)S(1)} all-to-all(f32[64,1,2048]{2,1,0:T(1,128)S(1)} %bitcast.108), channel_id=1, replica_groups=mesh['guide'=2,'seq'=64,'tp'=4] {'seq'}, dimensions={0} | all-to-all | bytes 1048576 | tf_op jit(solution)/shard_map/all_to_all | solution.py:49
  174.5 37.3 %all_to_all.46 = f32[64,1,2048]{2,1,0:T(1,128)S(1)} all-to-all(f32[64,1,2048]{2,1,0:T(1,128)S(1)} %broadcast_in_dim.243), channel_id=1, replica_groups=mesh['guide'=2,'seq'=64,'tp'=4] {'seq'}, dimensions={0} | all-to-all | bytes 1048576 | tf_op jit(solution)/shard_map/all_to_all | solution.py:51
  211.8 1.0 reshape.547
  (127 shorter events, 13.0 us)
Async XLA Ops:
  0.0 113.7 %copy-start = (bf16[320,2048]{1,0:T(8,128)(2,1)S(1)}, bf16[320,2048]{1,0:T(8,128)(2,1)}, u32[]{:S(2)}) copy-start(bf16[320,2048]{1,0:T(8,128)(2,1)} %param.21) | copy-start | bytes 3932164
  0.0 4.4 %copy-start.5 = (bf16[32,320]{1,0:T(8,128)(2,1)S(1)}, bf16[32,320]{1,0:T(8,128)(2,1)}, u32[]{:S(2)}) copy-start(bf16[32,320]{1,0:T(8,128)(2,1)} %param.19) | copy-start | bytes 61444
  3.8 21.9 %copy-start.4 = (s32[1,32,128]{2,1,0:T(8,128)S(1)}, s32[1,32,128]{2,1,0:T(8,128)}, u32[]{:S(2)}) copy-start(s32[1,32,128]{2,1,0:T(8,128)} %param.25) | copy-start | bytes 49156
  3.8 22.9 %copy-start.1 = (s32[1,32]{1,0:T(1,128)S(1)}, s32[1,32]{1,0:T(1,128)}, u32[]{:S(2)}) copy-start(s32[1,32]{1,0:T(1,128)} %param.24) | copy-start | bytes 388
  6.9 35.5 %all-to-all-start = ((f32[64,1,576]{2,1,0:T(1,128)}), f32[64,1,576]{2,1,0:T(1,128)S(1)}, u32[]{:S(2)}, u32[]{:S(2)}) async-start(f32[64,1,576]{2,1,0:T(1,128)} %all_to_all.37), calls=%async_computation | async-start | bytes 327680 | tf_op jit(solution)/shard_map/all_to_all | solution.py:143
  30.5 19.6 %copy-start.6 = (f32[64]{0:T(128)S(1)}, f32[64]{0:T(128)}, u32[]{:S(2)}) copy-start(f32[64]{0:T(128)} %param.17) | copy-start | bytes 772
  30.5 19.6 %copy-start.7 = (f32[64]{0:T(128)S(1)}, f32[64]{0:T(128)}, u32[]{:S(2)}) copy-start(f32[64]{0:T(128)} %param.18) | copy-start | bytes 772
  43.6 19.5 %all-to-all-start.1 = ((f32[64,1,192]{2,1,0:T(1,128)}), f32[64,1,192]{2,1,0:T(1,128)S(1)}, u32[]{:S(2)}, u32[]{:S(2)}) async-start(f32[64,1,192]{2,1,0:T(1,128)} %reshape.633), calls=%async_computation.1 | async-start | bytes 131072 | tf_op jit(solution)/shard_map/all_to_all | solution.py:145
  69.9 19.4 %all-to-all-start.2 = ((f32[64,1,198]{2,1,0:T(1,128)}), f32[64,1,198]{2,1,0:T(1,128)S(1)}, u32[]{:S(2)}, u32[]{:S(2)}) async-start(f32[64,1,198]{2,1,0:T(1,128)} %reshape.635), calls=%async_computation.2 | async-start | bytes 131072 | tf_op jit(solution)/shard_map/all_to_all | solution.py:73
  90.5 23.2 %copy-start.2 = (bf16[1,32,2048]{2,1,0:T(8,128)(2,1)S(1)}, bf16[1,32,2048]{2,1,0:T(8,128)(2,1)}, u32[]{:S(2)}) copy-start(bf16[1,32,2048]{2,1,0:T(8,128)(2,1)} %param.14) | copy-start | bytes 393220
  92.7 19.3 %all-to-all-start.3 = ((f32[64,1,195]{2,1,0:T(1,128)}), f32[64,1,195]{2,1,0:T(1,128)S(1)}, u32[]{:S(2)}, u32[]{:S(2)}) async-start(f32[64,1,195]{2,1,0:T(1,128)} %reshape.637), calls=%async_computation.3 | async-start | bytes 131072 | tf_op jit(solution)/shard_map/all_to_all | solution.py:85
  115.1 19.8 %all-to-all-start.4 = ((f32[8,16,2048]{2,1,0:T(8,128)}), f32[8,16,2048]{2,1,0:T(8,128)S(1)}, u32[]{:S(2)}, u32[]{:S(2)}) async-start(f32[8,16,2048]{2,1,0:T(8,128)} %bitcast.33), calls=%async_computation.4 | async-start | bytes 2097152 | tf_op jit(solution)/shard_map/all_to_all | solution.py:217
  119.6 15.6 %copy-start.3 = (bf16[32,8000]{1,0:T(8,128)(2,1)S(1)}, bf16[32,8000]{1,0:T(8,128)(2,1)}, u32[]{:S(2)}) copy-start(bf16[32,8000]{1,0:T(8,128)(2,1)} %param.22) | copy-start | bytes 1536004

commit v11 on v8

--- a/solution.py
+++ b/solution.py
@@ -186,7 +186,9 @@
     value_heads = jnp.where(
         second, value_pair[:, :, None, HEAD_SIZE:], value_pair[:, :, None, :HEAD_SIZE]
     )
-    slot_query = jnp.take(query_rot, owner_req, axis=0)
+    slot_query = jnp.einsum(
+        "rs,rhd->shd", owner_mask.astype(jnp.bfloat16), query_rot, preferred_element_type=jnp.float32
+    ).astype(jnp.bfloat16)
     scores = (
         jnp.einsum("shd,skhd->shk", slot_query, key_heads, preferred_element_type=jnp.float32)
         * scale
@@ -194,7 +196,7 @@
     scores = jnp.where(is_valid[:, None, :], scores, NEG_FILL)
     slot_max = jnp.max(scores, axis=2)
     request_max = jnp.max(jnp.where(owner_mask[:, :, None], slot_max[None, :, :], NEG_FILL), axis=1)
-    owner_max = jnp.take(request_max, owner_req, axis=0)
+    owner_max = jnp.max(jnp.where(owner_mask[:, :, None], request_max[:, None, :], NEG_FILL), axis=0)
     weights = jnp.where(is_valid[:, None, :], jnp.exp(scores - owner_max[:, :, None]), 0.0).astype(
         jnp.bfloat16
     )

time: 213 us -> 212 us (level)
  no operation moved by 1% of the time
where the time goes in v11:
time: 212 us; the launch traced here: 211 us
  blocking collectives  75.3 us (36%)
  waiting for transfers between devices  62.8 us (30%)
  starting transfers between devices  42.7 us (20%)
  local copies, waits for them, and re-layouts  18.2 us (9%)
  other arithmetic  7.82 us (4%)
  matrix products  3.52 us (2%)
    all_to_all x1, blocking collectives, all_reduce_columns(): parts = lax.all_to_all(value, axis, 1, 0, tiled=True)  38 us
    all_to_all x1, blocking collectives, all_reduce_columns(): lax.all_to_all(jnp.broadcast_to(total[None], (count, rows, columns // cou...  37.2 us
    all_to_all x1, starting transfers between devices, shards(): summed = jnp.sum(lax.all_to_all(outgoing, 'seq', 0, 0, tiled=True), axis=0)  18.8 us
    all_to_all x1, waiting for transfers between devices, shards(): incoming = lax.all_to_all(outgoing, ('guide', 'tp'), 0, 0, tiled=True)  14.5 us
    all_to_all x1, waiting for transfers between devices, merge_attention(): lax.all_to_all(jnp.broadcast_to(fraction.reshape(1, -1), (count, fraction...  12.9 us
    all_to_all x1, waiting for transfers between devices, shards(): lax.all_to_all(jnp.broadcast_to(query_chunk[None], (seq_count,) + query_c...  12.5 us
    all_to_all x1, waiting for transfers between devices, merge_attention(): parts = lax.all_to_all(spread, axis, 0, 0, tiled=True)  12 us
    all_to_all x1, waiting for transfers between devices, shards(): summed = jnp.sum(lax.all_to_all(outgoing, 'seq', 0, 0, tiled=True), axis=0)  10.9 us
  transfers between devices with their start and end apart: 5, of which 5 were waited for; matrix products, arithmetic and copies ran while one was open for 4% of the time, Pallas kernels for 0%

profile of v11, /device:TPU:6, one launch (start us, length us, event | category | flops | bytes accessed | tf_op | source)
XLA Modules:
  0.0 210.9 jit_solution(5274767495059572776)
XLA Ops:
  0.0 1.0 bitcast_convert_fusion
  1.0 1.0 multiply_reduce_fusion.1
  2.1 0.8 dynamic-slice.2
  2.9 1.0 fusion.71
  4.1 1.8 gather_fusion.1
  6.4 0.8 copy.174
  7.3 18.8 %all-to-all-start = ((f32[64,1,544]{2,1,0:T(1,128)}), f32[64,1,544]{2,1,0:T(1,128)S(1)}, u32[]{:S(2)}, u32[]{:S(2)}) async-start(f32[64,1,544]{2,1,0:T(1,128)} %copy.174), calls=%async_computation | async-start | bytes 327680 | tf_op jit(solution)/shard_map/all_to_all | solution.py:148
  26.2 0.6 compare_reduce_fusion
  27.2 1.7 dynamic-slice_bitcast_fusion.1
  30.3 0.7 gather_fusion
  31.0 0.6 gather_fusion.3
  31.9 10.9 %all-to-all-done = f32[64,1,544]{2,1,0:T(1,128)S(1)} async-done(((f32[64,1,544]{2,1,0:T(1,128)}), f32[64,1,544]{2,1,0:T(1,128)S(1)}, u32[]{:S(2)}, u32[]{:S(2)}) %all-to-all-start) | async-done | bytes 139296 | tf_op jit(solution)/shard_map/all_to_all | solution.py:148
  43.0 0.7 broadcast_in_dim.202
  43.7 6.6 %all-to-all-start.1 = ((f32[64,1,160]{2,1,0:T(1,128)}), f32[64,1,160]{2,1,0:T(1,128)S(1)}, u32[]{:S(2)}, u32[]{:S(2)}) async-start(f32[64,1,160]{2,1,0:T(1,128)} %broadcast_in_dim.202), calls=%async_computation.1 | async-start | bytes 131072 | tf_op jit(solution)/shard_map/all_to_all | solution.py:151
  50.7 12.5 %all-to-all-done.1 = f32[64,1,160]{2,1,0:T(1,128)S(1)} async-done(((f32[64,1,160]{2,1,0:T(1,128)}), f32[64,1,160]{2,1,0:T(1,128)S(1)}, u32[]{:S(2)}, u32[]{:S(2)}) %all-to-all-start.1) | async-done | bytes 40992 | tf_op jit(solution)/shard_map/all_to_all | solution.py:151
  65.0 0.7 fusion.1
  67.0 0.8 reshape.604
  67.8 6.5 %all-to-all-start.2 = ((f32[64,1,198]{2,1,0:T(1,128)}), f32[64,1,198]{2,1,0:T(1,128)S(1)}, u32[]{:S(2)}, u32[]{:S(2)}) async-start(f32[64,1,198]{2,1,0:T(1,128)} %reshape.604), calls=%async_computation.2 | async-start | bytes 131072 | tf_op jit(solution)/shard_map/all_to_all | solution.py:84
  74.5 0.6 gather_fusion.2
  75.2 12.0 %all-to-all-done.2 = f32[64,1,198]{2,1,0:T(1,128)S(1)} async-done(((f32[64,1,198]{2,1,0:T(1,128)}), f32[64,1,198]{2,1,0:T(1,128)S(1)}, u32[]{:S(2)}, u32[]{:S(2)}) %all-to-all-start.2) | async-done | bytes 50720 | tf_op jit(solution)/shard_map/all_to_all | solution.py:84
  87.7 0.8 reduce.14
  90.3 0.7 broadcast_in_dim.216
  91.0 6.4 %all-to-all-start.3 = ((f32[64,1,195]{2,1,0:T(1,128)}), f32[64,1,195]{2,1,0:T(1,128)S(1)}, u32[]{:S(2)}, u32[]{:S(2)}) async-start(f32[64,1,195]{2,1,0:T(1,128)} %broadcast_in_dim.216), calls=%async_computation.3 | async-start | bytes 131072 | tf_op jit(solution)/shard_map/all_to_all | solution.py:96
  97.4 12.9 %all-to-all-done.3 = f32[64,1,195]{2,1,0:T(1,128)S(1)} async-done(((f32[64,1,195]{2,1,0:T(1,128)}), f32[64,1,195]{2,1,0:T(1,128)S(1)}, u32[]{:S(2)}, u32[]{:S(2)}) %all-to-all-start.3) | async-done | bytes 49952 | tf_op jit(solution)/shard_map/all_to_all | solution.py:96
  111.3 1.1 broadcast_in_dim.219
  112.4 4.5 %all-to-all-start.4 = ((f32[8,16,2048]{2,1,0:T(8,128)}), f32[8,16,2048]{2,1,0:T(8,128)S(1)}, u32[]{:S(2)}, u32[]{:S(2)}) async-start(f32[8,16,2048]{2,1,0:T(8,128)} %bitcast.23), calls=%async_computation.4 | async-start | bytes 2097152 | tf_op jit(solution)/shard_map/all_to_all | solution.py:228
  116.9 0.8 dynamic-slice.3
  117.7 14.5 %all-to-all-done.4 = f32[8,16,2048]{2,1,0:T(8,128)S(1)} async-done(((f32[8,16,2048]{2,1,0:T(8,128)}), f32[8,16,2048]{2,1,0:T(8,128)S(1)}, u32[]{:S(2)}, u32[]{:S(2)}) %all-to-all-start.4) | async-done | bytes 1048608 | tf_op jit(solution)/shard_map/all_to_all | solution.py:228
  132.9 1.0 all_to_all.47
  134.2 38.0 %all_to_all.59 = f32[16,64,125]{2,0,1:T(8,128)S(1)} all-to-all(f32[16,64,125]{2,0,1:T(8,128)S(1)} %copy.197), channel_id=1, replica_groups=mesh['guide'=2,'seq'=64,'tp'=4] {'seq'}, dimensions={1} | all-to-all | bytes 1024000 | tf_op jit(solution)/shard_map/all_to_all | solution.py:60
  172.3 37.2 %all_to_all.60 = f32[64,16,125]{2,1,0:T(8,128)S(1)} all-to-all(f32[64,16,125]{2,1,0:T(8,128)S(1)} %broadcast_in_dim.220), channel_id=1, replica_groups=mesh['guide'=2,'seq'=64,'tp'=4] {'seq'}, dimensions={0} | all-to-all | bytes 1024000 | tf_op jit(solution)/shard_map/all_to_all | solution.py:62
  209.8 1.1 squeeze.20
  (120 shorter events, 11.3 us)
Async XLA Ops:
  0.0 111.0 %copy-start = (bf16[320,2048]{1,0:T(8,128)(2,1)S(1)}, bf16[320,2048]{1,0:T(8,128)(2,1)}, u32[]{:S(2)}) copy-start(bf16[320,2048]{1,0:T(8,128)(2,1)} %param.19) | copy-start | bytes 3932164
  0.0 6.1 %copy-start.5 = (bf16[32,320]{1,0:T(8,128)(2,1)S(1)}, bf16[32,320]{1,0:T(8,128)(2,1)}, u32[]{:S(2)}) copy-start(bf16[32,320]{1,0:T(8,128)(2,1)} %param.17) | copy-start | bytes 61444
  3.8 22.4 %copy-start.4 = (s32[1,32,128]{2,1,0:T(8,128)S(1)}, s32[1,32,128]{2,1,0:T(8,128)}, u32[]{:S(2)}) copy-start(s32[1,32,128]{2,1,0:T(8,128)} %param.23) | copy-start | bytes 49156
  7.3 35.5 %all-to-all-start = ((f32[64,1,544]{2,1,0:T(1,128)}), f32[64,1,544]{2,1,0:T(1,128)S(1)}, u32[]{:S(2)}, u32[]{:S(2)}) async-start(f32[64,1,544]{2,1,0:T(1,128)} %copy.174), calls=%async_computation | async-start | bytes 327680 | tf_op jit(solution)/shard_map/all_to_all | solution.py:148
  29.3 0.8 copy-start.1
  29.7 20.8 %copy-start.7 = (f32[64]{0:T(128)S(1)}, f32[64]{0:T(128)}, u32[]{:S(2)}) copy-start(f32[64]{0:T(128)} %param.16) | copy-start | bytes 772
  29.9 33.7 %copy-start.6 = (f32[64]{0:T(128)S(1)}, f32[64]{0:T(128)}, u32[]{:S(2)}) copy-start(f32[64]{0:T(128)} %param.15) | copy-start | bytes 772
  43.7 19.5 %all-to-all-start.1 = ((f32[64,1,160]{2,1,0:T(1,128)}), f32[64,1,160]{2,1,0:T(1,128)S(1)}, u32[]{:S(2)}, u32[]{:S(2)}) async-start(f32[64,1,160]{2,1,0:T(1,128)} %broadcast_in_dim.202), calls=%async_computation.1 | async-start | bytes 131072 | tf_op jit(solution)/shard_map/all_to_all | solution.py:151
  67.8 19.4 %all-to-all-start.2 = ((f32[64,1,198]{2,1,0:T(1,128)}), f32[64,1,198]{2,1,0:T(1,128)S(1)}, u32[]{:S(2)}, u32[]{:S(2)}) async-start(f32[64,1,198]{2,1,0:T(1,128)} %reshape.604), calls=%async_computation.2 | async-start | bytes 131072 | tf_op jit(solution)/shard_map/all_to_all | solution.py:84
  74.3 36.7 %copy-start.2 = (bf16[1,32,2048]{2,1,0:T(8,128)(2,1)S(1)}, bf16[1,32,2048]{2,1,0:T(8,128)(2,1)}, u32[]{:S(2)}) copy-start(bf16[1,32,2048]{2,1,0:T(8,128)(2,1)} %param.12) | copy-start | bytes 393220
  91.0 19.3 %all-to-all-start.3 = ((f32[64,1,195]{2,1,0:T(1,128)}), f32[64,1,195]{2,1,0:T(1,128)S(1)}, u32[]{:S(2)}, u32[]{:S(2)}) async-start(f32[64,1,195]{2,1,0:T(1,128)} %broadcast_in_dim.216), calls=%async_computation.3 | async-start | bytes 131072 | tf_op jit(solution)/shard_map/all_to_all | solution.py:96
  112.4 19.8 %all-to-all-start.4 = ((f32[8,16,2048]{2,1,0:T(8,128)}), f32[8,16,2048]{2,1,0:T(8,128)S(1)}, u32[]{:S(2)}, u32[]{:S(2)}) async-start(f32[8,16,2048]{2,1,0:T(8,128)} %bitcast.23), calls=%async_computation.4 | async-start | bytes 2097152 | tf_op jit(solution)/shard_map/all_to_all | solution.py:228
  116.9 15.6 %copy-start.3 = (bf16[32,8000]{1,0:T(8,128)(2,1)S(1)}, bf16[32,8000]{1,0:T(8,128)(2,1)}, u32[]{:S(2)}) copy-start(bf16[32,8000]{1,0:T(8,128)(2,1)} %param.20) | copy-start | bytes 1536004

commit v12 on v11

--- a/solution.py
+++ b/solution.py
@@ -234,7 +234,7 @@
     conditional_part = logit_part[:half_rows]
     unconditional_part = logit_part[half_rows:]
     guided_part = unconditional_part + GUIDE_WEIGHT * (conditional_part - unconditional_part)
-    return all_reduce_columns(guided_part, "seq")
+    return all_reduce(guided_part, "seq")
 
 
 def solution(mesh):

time: 212 us -> 211 us (level)
  no operation moved by 1% of the time
where the time goes in v12:
time: 211 us; the launch traced here: 210 us
  blocking collectives  75.3 us (36%)
  waiting for transfers between devices  62.8 us (30%)
  starting transfers between devices  42.7 us (20%)
  local copies, waits for them, and re-layouts  17.1 us (8%)
  other arithmetic  8.06 us (4%)
  matrix products  3.52 us (2%)
    all_to_all x1, blocking collectives, all_reduce(): parts = lax.all_to_all(flat.reshape(count, chunk), axis, 0, 0, tiled=True)  38 us
    all_to_all x1, blocking collectives, all_reduce(): lax.all_to_all(jnp.broadcast_to(total, (count, chunk)), axis, 0, 0, tiled...  37.2 us
    all_to_all x1, starting transfers between devices, shards(): summed = jnp.sum(lax.all_to_all(outgoing, 'seq', 0, 0, tiled=True), axis=0)  18.8 us
    all_to_all x1, waiting for transfers between devices, shards(): incoming = lax.all_to_all(outgoing, ('guide', 'tp'), 0, 0, tiled=True)  14.5 us
    all_to_all x1, waiting for transfers between devices, merge_attention(): lax.all_to_all(jnp.broadcast_to(fraction.reshape(1, -1), (count, fraction...  12.9 us
    all_to_all x1, waiting for transfers between devices, shards(): lax.all_to_all(jnp.broadcast_to(query_chunk[None], (seq_count,) + query_c...  12.5 us
    all_to_all x1, waiting for transfers between devices, merge_attention(): parts = lax.all_to_all(spread, axis, 0, 0, tiled=True)  12 us
    all_to_all x1, waiting for transfers between devices, shards(): summed = jnp.sum(lax.all_to_all(outgoing, 'seq', 0, 0, tiled=True), axis=0)  10.9 us
  transfers between devices with their start and end apart: 5, of which 5 were waited for; matrix products, arithmetic and copies ran while one was open for 4% of the time, Pallas kernels for 0%

profile of v12, /device:TPU:6, one launch (start us, length us, event | category | flops | bytes accessed | tf_op | source)
XLA Modules:
  0.0 210.0 jit_solution(5958054987901008708)
XLA Ops:
  0.0 1.0 bitcast_convert_fusion
  1.0 1.0 multiply_reduce_fusion.1
  2.1 0.8 dynamic-slice.2
  2.9 1.0 fusion.71
  4.1 1.8 gather_fusion.1
  6.4 0.8 copy.171
  7.3 18.8 %all-to-all-start = ((f32[64,1,544]{2,1,0:T(1,128)}), f32[64,1,544]{2,1,0:T(1,128)S(1)}, u32[]{:S(2)}, u32[]{:S(2)}) async-start(f32[64,1,544]{2,1,0:T(1,128)} %copy.171), calls=%async_computation | async-start | bytes 327680 | tf_op jit(solution)/shard_map/all_to_all | solution.py:148
  26.2 0.6 compare_reduce_fusion
  27.2 1.7 dynamic-slice_bitcast_fusion.1
  30.3 0.7 gather_fusion
  31.0 0.6 gather_fusion.3
  31.9 10.9 %all-to-all-done = f32[64,1,544]{2,1,0:T(1,128)S(1)} async-done(((f32[64,1,544]{2,1,0:T(1,128)}), f32[64,1,544]{2,1,0:T(1,128)S(1)}, u32[]{:S(2)}, u32[]{:S(2)}) %all-to-all-start) | async-done | bytes 139296 | tf_op jit(solution)/shard_map/all_to_all | solution.py:148
  43.0 0.7 broadcast_in_dim.202
  43.7 6.6 %all-to-all-start.1 = ((f32[64,1,160]{2,1,0:T(1,128)}), f32[64,1,160]{2,1,0:T(1,128)S(1)}, u32[]{:S(2)}, u32[]{:S(2)}) async-start(f32[64,1,160]{2,1,0:T(1,128)} %broadcast_in_dim.202), calls=%async_computation.1 | async-start | bytes 131072 | tf_op jit(solution)/shard_map/all_to_all | solution.py:151
  50.7 12.5 %all-to-all-done.1 = f32[64,1,160]{2,1,0:T(1,128)S(1)} async-done(((f32[64,1,160]{2,1,0:T(1,128)}), f32[64,1,160]{2,1,0:T(1,128)S(1)}, u32[]{:S(2)}, u32[]{:S(2)}) %all-to-all-start.1) | async-done | bytes 40992 | tf_op jit(solution)/shard_map/all_to_all | solution.py:151
  65.0 0.7 fusion.1
  67.0 0.8 reshape.620
  67.8 6.5 %all-to-all-start.2 = ((f32[64,1,198]{2,1,0:T(1,128)}), f32[64,1,198]{2,1,0:T(1,128)S(1)}, u32[]{:S(2)}, u32[]{:S(2)}) async-start(f32[64,1,198]{2,1,0:T(1,128)} %reshape.620), calls=%async_computation.2 | async-start | bytes 131072 | tf_op jit(solution)/shard_map/all_to_all | solution.py:84
  74.5 0.6 gather_fusion.2
  75.2 12.0 %all-to-all-done.2 = f32[64,1,198]{2,1,0:T(1,128)S(1)} async-done(((f32[64,1,198]{2,1,0:T(1,128)}), f32[64,1,198]{2,1,0:T(1,128)S(1)}, u32[]{:S(2)}, u32[]{:S(2)}) %all-to-all-start.2) | async-done | bytes 50720 | tf_op jit(solution)/shard_map/all_to_all | solution.py:84
  87.2 0.5 broadcast.604
  87.7 0.8 reduce.13
  90.3 0.7 broadcast_in_dim.216
  91.0 6.4 %all-to-all-start.3 = ((f32[64,1,195]{2,1,0:T(1,128)}), f32[64,1,195]{2,1,0:T(1,128)S(1)}, u32[]{:S(2)}, u32[]{:S(2)}) async-start(f32[64,1,195]{2,1,0:T(1,128)} %broadcast_in_dim.216), calls=%async_computation.3 | async-start | bytes 131072 | tf_op jit(solution)/shard_map/all_to_all | solution.py:96
  97.4 12.9 %all-to-all-done.3 = f32[64,1,195]{2,1,0:T(1,128)S(1)} async-done(((f32[64,1,195]{2,1,0:T(1,128)}), f32[64,1,195]{2,1,0:T(1,128)S(1)}, u32[]{:S(2)}, u32[]{:S(2)}) %all-to-all-start.3) | async-done | bytes 49952 | tf_op jit(solution)/shard_map/all_to_all | solution.py:96
  111.3 1.1 broadcast_in_dim.219
  112.4 4.5 %all-to-all-start.4 = ((f32[8,16,2048]{2,1,0:T(8,128)}), f32[8,16,2048]{2,1,0:T(8,128)S(1)}, u32[]{:S(2)}, u32[]{:S(2)}) async-start(f32[8,16,2048]{2,1,0:T(8,128)} %bitcast.23), calls=%async_computation.4 | async-start | bytes 2097152 | tf_op jit(solution)/shard_map/all_to_all | solution.py:228
  116.9 0.8 dynamic-slice.3
  117.7 14.5 %all-to-all-done.4 = f32[8,16,2048]{2,1,0:T(8,128)S(1)} async-done(((f32[8,16,2048]{2,1,0:T(8,128)}), f32[8,16,2048]{2,1,0:T(8,128)S(1)}, u32[]{:S(2)}, u32[]{:S(2)}) %all-to-all-start.4) | async-done | bytes 1048608 | tf_op jit(solution)/shard_map/all_to_all | solution.py:228
  133.2 38.0 %all_to_all.46 = f32[64,1,2048]{2,1,0:T(1,128)S(1)} all-to-all(f32[64,1,2048]{2,1,0:T(1,128)S(1)} %bitcast.86), channel_id=1, replica_groups=mesh['guide'=2,'seq'=64,'tp'=4] {'seq'}, dimensions={0} | all-to-all | bytes 1048576 | tf_op jit(solution)/shard_map/all_to_all | solution.py:49
  171.8 37.2 %all_to_all.47 = f32[64,1,2048]{2,1,0:T(1,128)S(1)} all-to-all(f32[64,1,2048]{2,1,0:T(1,128)S(1)} %broadcast_in_dim.220), channel_id=1, replica_groups=mesh['guide'=2,'seq'=64,'tp'=4] {'seq'}, dimensions={0} | all-to-all | bytes 1048576 | tf_op jit(solution)/shard_map/all_to_all | solution.py:51
  209.1 1.0 reshape.568
  (120 shorter events, 11.0 us)
Async XLA Ops:
  0.0 111.0 %copy-start = (bf16[320,2048]{1,0:T(8,128)(2,1)S(1)}, bf16[320,2048]{1,0:T(8,128)(2,1)}, u32[]{:S(2)}) copy-start(bf16[320,2048]{1,0:T(8,128)(2,1)} %param.19) | copy-start | bytes 3932164
  0.0 6.1 %copy-start.5 = (bf16[32,320]{1,0:T(8,128)(2,1)S(1)}, bf16[32,320]{1,0:T(8,128)(2,1)}, u32[]{:S(2)}) copy-start(bf16[32,320]{1,0:T(8,128)(2,1)} %param.17) | copy-start | bytes 61444
  3.8 22.4 %copy-start.4 = (s32[1,32,128]{2,1,0:T(8,128)S(1)}, s32[1,32,128]{2,1,0:T(8,128)}, u32[]{:S(2)}) copy-start(s32[1,32,128]{2,1,0:T(8,128)} %param.23) | copy-start | bytes 49156
  7.3 35.5 %all-to-all-start = ((f32[64,1,544]{2,1,0:T(1,128)}), f32[64,1,544]{2,1,0:T(1,128)S(1)}, u32[]{:S(2)}, u32[]{:S(2)}) async-start(f32[64,1,544]{2,1,0:T(1,128)} %copy.171), calls=%async_computation | async-start | bytes 327680 | tf_op jit(solution)/shard_map/all_to_all | solution.py:148
  29.3 0.8 copy-start.1
  29.7 20.8 %copy-start.7 = (f32[64]{0:T(128)S(1)}, f32[64]{0:T(128)}, u32[]{:S(2)}) copy-start(f32[64]{0:T(128)} %param.16) | copy-start | bytes 772
  29.9 33.7 %copy-start.6 = (f32[64]{0:T(128)S(1)}, f32[64]{0:T(128)}, u32[]{:S(2)}) copy-start(f32[64]{0:T(128)} %param.15) | copy-start | bytes 772
  43.7 19.5 %all-to-all-start.1 = ((f32[64,1,160]{2,1,0:T(1,128)}), f32[64,1,160]{2,1,0:T(1,128)S(1)}, u32[]{:S(2)}, u32[]{:S(2)}) async-start(f32[64,1,160]{2,1,0:T(1,128)} %broadcast_in_dim.202), calls=%async_computation.1 | async-start | bytes 131072 | tf_op jit(solution)/shard_map/all_to_all | solution.py:151
  67.8 19.4 %all-to-all-start.2 = ((f32[64,1,198]{2,1,0:T(1,128)}), f32[64,1,198]{2,1,0:T(1,128)S(1)}, u32[]{:S(2)}, u32[]{:S(2)}) async-start(f32[64,1,198]{2,1,0:T(1,128)} %reshape.620), calls=%async_computation.2 | async-start | bytes 131072 | tf_op jit(solution)/shard_map/all_to_all | solution.py:84
  74.3 36.7 %copy-start.2 = (bf16[1,32,2048]{2,1,0:T(8,128)(2,1)S(1)}, bf16[1,32,2048]{2,1,0:T(8,128)(2,1)}, u32[]{:S(2)}) copy-start(bf16[1,32,2048]{2,1,0:T(8,128)(2,1)} %param.12) | copy-start | bytes 393220
  91.0 19.3 %all-to-all-start.3 = ((f32[64,1,195]{2,1,0:T(1,128)}), f32[64,1,195]{2,1,0:T(1,128)S(1)}, u32[]{:S(2)}, u32[]{:S(2)}) async-start(f32[64,1,195]{2,1,0:T(1,128)} %broadcast_in_dim.216), calls=%async_computation.3 | async-start | bytes 131072 | tf_op jit(solution)/shard_map/all_to_all | solution.py:96
  112.4 19.8 %all-to-all-start.4 = ((f32[8,16,2048]{2,1,0:T(8,128)}), f32[8,16,2048]{2,1,0:T(8,128)S(1)}, u32[]{:S(2)}, u32[]{:S(2)}) async-start(f32[8,16,2048]{2,1,0:T(8,128)} %bitcast.23), calls=%async_computation.4 | async-start | bytes 2097152 | tf_op jit(solution)/shard_map/all_to_all | solution.py:228
  116.9 15.6 %copy-start.3 = (bf16[32,8000]{1,0:T(8,128)(2,1)S(1)}, bf16[32,8000]{1,0:T(8,128)(2,1)}, u32[]{:S(2)}) copy-start(bf16[32,8000]{1,0:T(8,128)(2,1)} %param.20) | copy-start | bytes 1536004

commit v13 on v12

--- a/solution.py
+++ b/solution.py
@@ -217,14 +217,20 @@
         own_value,
         "seq",
     ).reshape(request_number, nearby_heads * HEAD_SIZE)
-    output_part = jnp.dot(attended, output_weight, preferred_element_type=jnp.float32)
-    output_part = output_part + jnp.where(lax.axis_index("tp") == 0, token_rows, 0.0)
     guide_count = lax.axis_size("guide")
     tp_count = lax.axis_size("tp")
-    outgoing = jnp.broadcast_to(
-        output_part.reshape(guide_count, 1, half_rows, -1),
-        (guide_count, tp_count, half_rows, output_part.shape[1]),
-    ).reshape(guide_count * tp_count, half_rows, -1)
+    spread_rows = jnp.broadcast_to(
+        attended.reshape(guide_count, 1, half_rows, -1),
+        (guide_count, tp_count, half_rows, attended.shape[1]),
+    )
+    spread_hidden = jnp.broadcast_to(
+        token_rows.reshape(guide_count, 1, half_rows, -1),
+        (guide_count, tp_count, half_rows, token_rows.shape[1]),
+    )
+    outgoing = jnp.einsum(
+        "gtrk,kc->gtrc", spread_rows, output_weight, preferred_element_type=jnp.float32
+    ) + jnp.where(lax.axis_index("tp") == 0, spread_hidden, 0.0)
+    outgoing = outgoing.reshape(guide_count * tp_count, half_rows, -1)
     incoming = lax.all_to_all(outgoing, ("guide", "tp"), 0, 0, tiled=True)
     residual = jnp.sum(incoming.reshape(guide_count, tp_count, half_rows, -1), axis=1)
     final_rows = norm_rows(residual, final_gain)

time: 211 us -> 211 us (level)
  no operation moved by 1% of the time
where the time goes in v13:
time: 211 us; the launch traced here: 210 us
  blocking collectives  75.3 us (36%)
  waiting for transfers between devices  62.8 us (30%)
  starting transfers between devices  42.7 us (20%)
  local copies, waits for them, and re-layouts  16 us (8%)
  other arithmetic  8.08 us (4%)
  matrix products  4.64 us (2%)
    all_to_all x1, blocking collectives, all_reduce(): parts = lax.all_to_all(flat.reshape(count, chunk), axis, 0, 0, tiled=True)  38.1 us
    all_to_all x1, blocking collectives, all_reduce(): lax.all_to_all(jnp.broadcast_to(total, (count, chunk)), axis, 0, 0, tiled...  37.2 us
    all_to_all x1, starting transfers between devices, shards(): summed = jnp.sum(lax.all_to_all(outgoing, 'seq', 0, 0, tiled=True), axis=0)  18.8 us
    all_to_all x1, waiting for transfers between devices, shards(): incoming = lax.all_to_all(outgoing, ('guide', 'tp'), 0, 0, tiled=True)  14.5 us
    all_to_all x1, waiting for transfers between devices, merge_attention(): lax.all_to_all(jnp.broadcast_to(fraction.reshape(1, -1), (count, fraction...  12.9 us
    all_to_all x1, waiting for transfers between devices, shards(): lax.all_to_all(jnp.broadcast_to(query_chunk[None], (seq_count,) + query_c...  12.5 us
    all_to_all x1, waiting for transfers between devices, merge_attention(): parts = lax.all_to_all(spread, axis, 0, 0, tiled=True)  12 us
    all_to_all x1, waiting for transfers between devices, shards(): summed = jnp.sum(lax.all_to_all(outgoing, 'seq', 0, 0, tiled=True), axis=0)  10.9 us
  transfers between devices with their start and end apart: 5, of which 5 were waited for; matrix products, arithmetic and copies ran while one was open for 4% of the time, Pallas kernels for 0%

profile of v13, /device:TPU:6, one launch (start us, length us, event | category | flops | bytes accessed | tf_op | source)
XLA Modules:
  0.0 210.1 jit_solution(11903705475425016351)
XLA Ops:
  0.0 1.0 convert_bitcast_fusion
  1.0 1.0 multiply_reduce_fusion.1
  2.1 0.8 dynamic-slice.2
  2.9 1.0 fusion.73
  4.1 1.8 gather_fusion.1
  6.5 0.8 copy.171
  7.3 18.8 %all-to-all-start = ((f32[64,1,544]{2,1,0:T(1,128)}), f32[64,1,544]{2,1,0:T(1,128)S(1)}, u32[]{:S(2)}, u32[]{:S(2)}) async-start(f32[64,1,544]{2,1,0:T(1,128)} %copy.171), calls=%async_computation | async-start | bytes 327680 | tf_op jit(solution)/shard_map/all_to_all | solution.py:148
  26.2 0.6 compare_reduce_fusion
  27.2 1.7 dynamic-slice_bitcast_fusion.1
  30.3 0.7 gather_fusion
  31.0 0.6 gather_fusion.3
  31.9 10.9 %all-to-all-done = f32[64,1,544]{2,1,0:T(1,128)S(1)} async-done(((f32[64,1,544]{2,1,0:T(1,128)}), f32[64,1,544]{2,1,0:T(1,128)S(1)}, u32[]{:S(2)}, u32[]{:S(2)}) %all-to-all-start) | async-done | bytes 139296 | tf_op jit(solution)/shard_map/all_to_all | solution.py:148
  43.1 0.7 broadcast_in_dim.207
  43.7 6.6 %all-to-all-start.1 = ((f32[64,1,160]{2,1,0:T(1,128)}), f32[64,1,160]{2,1,0:T(1,128)S(1)}, u32[]{:S(2)}, u32[]{:S(2)}) async-start(f32[64,1,160]{2,1,0:T(1,128)} %broadcast_in_dim.207), calls=%async_computation.1 | async-start | bytes 131072 | tf_op jit(solution)/shard_map/all_to_all | solution.py:151
  50.7 12.5 %all-to-all-done.1 = f32[64,1,160]{2,1,0:T(1,128)S(1)} async-done(((f32[64,1,160]{2,1,0:T(1,128)}), f32[64,1,160]{2,1,0:T(1,128)S(1)}, u32[]{:S(2)}, u32[]{:S(2)}) %all-to-all-start.1) | async-done | bytes 40992 | tf_op jit(solution)/shard_map/all_to_all | solution.py:151
  65.1 0.7 fusion.2
  67.1 0.8 reshape.626
  67.9 6.5 %all-to-all-start.2 = ((f32[64,1,198]{2,1,0:T(1,128)}), f32[64,1,198]{2,1,0:T(1,128)S(1)}, u32[]{:S(2)}, u32[]{:S(2)}) async-start(f32[64,1,198]{2,1,0:T(1,128)} %reshape.626), calls=%async_computation.2 | async-start | bytes 131072 | tf_op jit(solution)/shard_map/all_to_all | solution.py:84
  74.5 0.6 gather_fusion.2
  75.3 12.0 %all-to-all-done.2 = f32[64,1,198]{2,1,0:T(1,128)S(1)} async-done(((f32[64,1,198]{2,1,0:T(1,128)}), f32[64,1,198]{2,1,0:T(1,128)S(1)}, u32[]{:S(2)}, u32[]{:S(2)}) %all-to-all-start.2) | async-done | bytes 50720 | tf_op jit(solution)/shard_map/all_to_all | solution.py:84
  87.3 0.5 broadcast.611
  87.8 0.8 reduce.13
  90.4 0.7 broadcast_in_dim.221
  91.0 6.4 %all-to-all-start.3 = ((f32[64,1,195]{2,1,0:T(1,128)}), f32[64,1,195]{2,1,0:T(1,128)S(1)}, u32[]{:S(2)}, u32[]{:S(2)}) async-start(f32[64,1,195]{2,1,0:T(1,128)} %broadcast_in_dim.221), calls=%async_computation.3 | async-start | bytes 131072 | tf_op jit(solution)/shard_map/all_to_all | solution.py:96
  97.5 12.9 %all-to-all-done.3 = f32[64,1,195]{2,1,0:T(1,128)S(1)} async-done(((f32[64,1,195]{2,1,0:T(1,128)}), f32[64,1,195]{2,1,0:T(1,128)S(1)}, u32[]{:S(2)}, u32[]{:S(2)}) %all-to-all-start.3) | async-done | bytes 49952 | tf_op jit(solution)/shard_map/all_to_all | solution.py:96
  111.0 1.4 convolution_add_fusion
  112.5 4.5 %all-to-all-start.4 = ((f32[8,16,2048]{2,1,0:T(8,128)}), f32[8,16,2048]{2,1,0:T(8,128)S(1)}, u32[]{:S(2)}, u32[]{:S(2)}) async-start(f32[8,16,2048]{2,1,0:T(8,128)} %bitcast.24), calls=%async_computation.4 | async-start | bytes 2097152 | tf_op jit(solution)/shard_map/all_to_all | solution.py:234
  116.9 0.8 dynamic-slice.3
  117.8 14.5 %all-to-all-done.4 = f32[8,16,2048]{2,1,0:T(8,128)S(1)} async-done(((f32[8,16,2048]{2,1,0:T(8,128)}), f32[8,16,2048]{2,1,0:T(8,128)S(1)}, u32[]{:S(2)}, u32[]{:S(2)}) %all-to-all-start.4) | async-done | bytes 1048608 | tf_op jit(solution)/shard_map/all_to_all | solution.py:234
  133.2 38.1 %all_to_all.46 = f32[64,1,2048]{2,1,0:T(1,128)S(1)} all-to-all(f32[64,1,2048]{2,1,0:T(1,128)S(1)} %bitcast.88), channel_id=1, replica_groups=mesh['guide'=2,'seq'=64,'tp'=4] {'seq'}, dimensions={0} | all-to-all | bytes 1048576 | tf_op jit(solution)/shard_map/all_to_all | solution.py:49
  171.8 37.2 %all_to_all.47 = f32[64,1,2048]{2,1,0:T(1,128)S(1)} all-to-all(f32[64,1,2048]{2,1,0:T(1,128)S(1)} %broadcast_in_dim.226), channel_id=1, replica_groups=mesh['guide'=2,'seq'=64,'tp'=4] {'seq'}, dimensions={0} | all-to-all | bytes 1048576 | tf_op jit(solution)/shard_map/all_to_all | solution.py:51
  209.1 1.0 reshape.573
  (120 shorter events, 10.7 us)
Async XLA Ops:
  0.0 111.0 %copy-start = (bf16[320,2048]{1,0:T(8,128)(2,1)S(1)}, bf16[320,2048]{1,0:T(8,128)(2,1)}, u32[]{:S(2)}) copy-start(bf16[320,2048]{1,0:T(8,128)(2,1)} %param.19) | copy-start | bytes 3932164
  0.0 6.1 %copy-start.5 = (bf16[32,320]{1,0:T(8,128)(2,1)S(1)}, bf16[32,320]{1,0:T(8,128)(2,1)}, u32[]{:S(2)}) copy-start(bf16[32,320]{1,0:T(8,128)(2,1)} %param.17) | copy-start | bytes 61444
  3.8 22.4 %copy-start.4 = (s32[1,32,128]{2,1,0:T(8,128)S(1)}, s32[1,32,128]{2,1,0:T(8,128)}, u32[]{:S(2)}) copy-start(s32[1,32,128]{2,1,0:T(8,128)} %param.23) | copy-start | bytes 49156
  3.9 23.2 %copy-start.1 = (s32[1,32]{1,0:T(1,128)S(1)}, s32[1,32]{1,0:T(1,128)}, u32[]{:S(2)}) copy-start(s32[1,32]{1,0:T(1,128)} %param.22) | copy-start | bytes 388
  7.3 35.5 %all-to-all-start = ((f32[64,1,544]{2,1,0:T(1,128)}), f32[64,1,544]{2,1,0:T(1,128)S(1)}, u32[]{:S(2)}, u32[]{:S(2)}) async-start(f32[64,1,544]{2,1,0:T(1,128)} %copy.171), calls=%async_computation | async-start | bytes 327680 | tf_op jit(solution)/shard_map/all_to_all | solution.py:148
  29.8 20.6 %copy-start.7 = (f32[64]{0:T(128)S(1)}, f32[64]{0:T(128)}, u32[]{:S(2)}) copy-start(f32[64]{0:T(128)} %param.16) | copy-start | bytes 772
  30.1 33.6 %copy-start.6 = (f32[64]{0:T(128)S(1)}, f32[64]{0:T(128)}, u32[]{:S(2)}) copy-start(f32[64]{0:T(128)} %param.15) | copy-start | bytes 772
  43.7 19.5 %all-to-all-start.1 = ((f32[64,1,160]{2,1,0:T(1,128)}), f32[64,1,160]{2,1,0:T(1,128)S(1)}, u32[]{:S(2)}, u32[]{:S(2)}) async-start(f32[64,1,160]{2,1,0:T(1,128)} %broadcast_in_dim.207), calls=%async_computation.1 | async-start | bytes 131072 | tf_op jit(solution)/shard_map/all_to_all | solution.py:151
  66.9 30.5 %copy-start.2 = (bf16[1,32,2048]{2,1,0:T(8,128)(2,1)S(1)}, bf16[1,32,2048]{2,1,0:T(8,128)(2,1)}, u32[]{:S(2)}) copy-start(bf16[1,32,2048]{2,1,0:T(8,128)(2,1)} %param.12) | copy-start | bytes 393220
  67.9 19.4 %all-to-all-start.2 = ((f32[64,1,198]{2,1,0:T(1,128)}), f32[64,1,198]{2,1,0:T(1,128)S(1)}, u32[]{:S(2)}, u32[]{:S(2)}) async-start(f32[64,1,198]{2,1,0:T(1,128)} %reshape.626), calls=%async_computation.2 | async-start | bytes 131072 | tf_op jit(solution)/shard_map/all_to_all | solution.py:84
  91.0 19.3 %all-to-all-start.3 = ((f32[64,1,195]{2,1,0:T(1,128)}), f32[64,1,195]{2,1,0:T(1,128)S(1)}, u32[]{:S(2)}, u32[]{:S(2)}) async-start(f32[64,1,195]{2,1,0:T(1,128)} %broadcast_in_dim.221), calls=%async_computation.3 | async-start | bytes 131072 | tf_op jit(solution)/shard_map/all_to_all | solution.py:96
  112.5 19.8 %all-to-all-start.4 = ((f32[8,16,2048]{2,1,0:T(8,128)}), f32[8,16,2048]{2,1,0:T(8,128)S(1)}, u32[]{:S(2)}, u32[]{:S(2)}) async-start(f32[8,16,2048]{2,1,0:T(8,128)} %bitcast.24), calls=%async_computation.4 | async-start | bytes 2097152 | tf_op jit(solution)/shard_map/all_to_all | solution.py:234
  116.9 15.6 %copy-start.3 = (bf16[32,8000]{1,0:T(8,128)(2,1)S(1)}, bf16[32,8000]{1,0:T(8,128)(2,1)}, u32[]{:S(2)}) copy-start(bf16[32,8000]{1,0:T(8,128)(2,1)} %param.20) | copy-start | bytes 1536004

commit v14 on v12

--- a/solution.py
+++ b/solution.py
@@ -145,11 +145,20 @@
         ],
         axis=1,
     )
-    summed = jnp.sum(lax.all_to_all(outgoing, "seq", 0, 0, tiled=True), axis=0)
-    query_chunk = summed[: query_width * request_number // seq_count]
-    own_key_value = summed[query_chunk.shape[0] :].reshape(unit_per, 2, HEAD_SIZE)
+    received = lax.all_to_all(outgoing, "seq", 0, 0, tiled=True)
+    chunk_width = query_width * request_number // seq_count
+    own_key_value = jnp.sum(received[:, chunk_width:], axis=0).reshape(unit_per, 2, HEAD_SIZE)
     query_sum = lax.all_to_all(
-        jnp.broadcast_to(query_chunk[None], (seq_count,) + query_chunk.shape), "seq", 0, 0, tiled=True
+        jnp.dot(
+            jnp.ones((seq_count, seq_count), jnp.float32),
+            received[:, :chunk_width],
+            precision=lax.Precision.HIGHEST,
+            preferred_element_type=jnp.float32,
+        ),
+        "seq",
+        0,
+        0,
+        tiled=True,
     ).reshape(request_number, query_width)
     query_normed = per_head_norm(
         query_sum.reshape(request_number, nearby_heads, HEAD_SIZE), query_gain

time: 211 us -> 211 us (level)
  no operation moved by 1% of the time
where the time goes in v14:
time: 211 us; the launch traced here: 210 us
  blocking collectives  75.3 us (36%)
  waiting for transfers between devices  62.8 us (30%)
  starting transfers between devices  42.7 us (20%)
  local copies, waits for them, and re-layouts  17.1 us (8%)
  other arithmetic  8.02 us (4%)
  matrix products  3.72 us (2%)
    all_to_all x1, blocking collectives, all_reduce(): parts = lax.all_to_all(flat.reshape(count, chunk), axis, 0, 0, tiled=True)  38 us
    all_to_all x1, blocking collectives, all_reduce(): lax.all_to_all(jnp.broadcast_to(total, (count, chunk)), axis, 0, 0, tiled...  37.2 us
    all_to_all x1, starting transfers between devices, shards(): received = lax.all_to_all(outgoing, 'seq', 0, 0, tiled=True)  18.8 us
    all_to_all x1, waiting for transfers between devices, shards(): incoming = lax.all_to_all(outgoing, ('guide', 'tp'), 0, 0, tiled=True)  14.5 us
    all_to_all x1, waiting for transfers between devices, merge_attention(): lax.all_to_all(jnp.broadcast_to(fraction.reshape(1, -1), (count, fraction...  12.9 us
    all_to_all x1, waiting for transfers between devices, shards(): lax.all_to_all(jnp.dot(jnp.ones((seq_count, seq_count), jnp.float32), rec...  12.5 us
    all_to_all x1, waiting for transfers between devices, merge_attention(): parts = lax.all_to_all(spread, axis, 0, 0, tiled=True)  12 us
    all_to_all x1, waiting for transfers between devices, shards(): received = lax.all_to_all(outgoing, 'seq', 0, 0, tiled=True)  10.9 us
  transfers between devices with their start and end apart: 5, of which 5 were waited for; matrix products, arithmetic and copies ran while one was open for 4% of the time, Pallas kernels for 0%

profile of v14, /device:TPU:6, one launch (start us, length us, event | category | flops | bytes accessed | tf_op | source)
XLA Modules:
  0.0 210.2 jit_solution(30146993462113323)
XLA Ops:
  0.0 1.0 bitcast_convert_fusion
  1.0 1.0 multiply_reduce_fusion.1
  2.1 0.8 dynamic-slice.2
  2.9 1.0 fusion.74
  4.1 1.8 gather_fusion.1
  6.4 0.8 copy.176
  7.3 18.8 %all-to-all-start = ((f32[64,1,544]{2,1,0:T(1,128)}), f32[64,1,544]{2,1,0:T(1,128)S(1)}, u32[]{:S(2)}, u32[]{:S(2)}) async-start(f32[64,1,544]{2,1,0:T(1,128)} %copy.176), calls=%async_computation | async-start | bytes 327680 | tf_op jit(solution)/shard_map/all_to_all | solution.py:148
  26.2 0.6 compare_reduce_fusion
  27.2 1.7 dynamic-slice_bitcast_fusion.1
  30.3 0.7 gather_fusion
  31.0 0.6 gather_fusion.3
  31.9 10.9 %all-to-all-done = f32[64,1,544]{2,1,0:T(1,128)S(1)} async-done(((f32[64,1,544]{2,1,0:T(1,128)}), f32[64,1,544]{2,1,0:T(1,128)S(1)}, u32[]{:S(2)}, u32[]{:S(2)}) %all-to-all-start) | async-done | bytes 139296 | tf_op jit(solution)/shard_map/all_to_all | solution.py:148
  43.1 0.7 copy.177
  43.9 6.6 %all-to-all-start.1 = ((f32[64,1,160]{2,1,0:T(1,128)}), f32[64,1,160]{2,1,0:T(1,128)S(1)}, u32[]{:S(2)}, u32[]{:S(2)}) async-start(f32[64,1,160]{2,1,0:T(1,128)} %copy.177), calls=%async_computation.1 | async-start | bytes 131072 | tf_op jit(solution)/shard_map/all_to_all | solution.py:151
  50.8 12.5 %all-to-all-done.1 = f32[64,1,160]{2,1,0:T(1,128)S(1)} async-done(((f32[64,1,160]{2,1,0:T(1,128)}), f32[64,1,160]{2,1,0:T(1,128)S(1)}, u32[]{:S(2)}, u32[]{:S(2)}) %all-to-all-start.1) | async-done | bytes 40992 | tf_op jit(solution)/shard_map/all_to_all | solution.py:151
  65.2 0.7 fusion.1
  67.2 0.8 reshape.616
  68.0 6.5 %all-to-all-start.2 = ((f32[64,1,198]{2,1,0:T(1,128)}), f32[64,1,198]{2,1,0:T(1,128)S(1)}, u32[]{:S(2)}, u32[]{:S(2)}) async-start(f32[64,1,198]{2,1,0:T(1,128)} %reshape.616), calls=%async_computation.2 | async-start | bytes 131072 | tf_op jit(solution)/shard_map/all_to_all | solution.py:84
  74.6 0.6 gather_fusion.2
  75.4 12.0 %all-to-all-done.2 = f32[64,1,198]{2,1,0:T(1,128)S(1)} async-done(((f32[64,1,198]{2,1,0:T(1,128)}), f32[64,1,198]{2,1,0:T(1,128)S(1)}, u32[]{:S(2)}, u32[]{:S(2)}) %all-to-all-start.2) | async-done | bytes 50720 | tf_op jit(solution)/shard_map/all_to_all | solution.py:84
  87.4 0.5 broadcast.601
  87.9 0.8 reduce.12
  90.5 0.7 broadcast_in_dim.213
  91.2 6.4 %all-to-all-start.3 = ((f32[64,1,195]{2,1,0:T(1,128)}), f32[64,1,195]{2,1,0:T(1,128)S(1)}, u32[]{:S(2)}, u32[]{:S(2)}) async-start(f32[64,1,195]{2,1,0:T(1,128)} %broadcast_in_dim.213), calls=%async_computation.3 | async-start | bytes 131072 | tf_op jit(solution)/shard_map/all_to_all | solution.py:96
  97.6 12.9 %all-to-all-done.3 = f32[64,1,195]{2,1,0:T(1,128)S(1)} async-done(((f32[64,1,195]{2,1,0:T(1,128)}), f32[64,1,195]{2,1,0:T(1,128)S(1)}, u32[]{:S(2)}, u32[]{:S(2)}) %all-to-all-start.3) | async-done | bytes 49952 | tf_op jit(solution)/shard_map/all_to_all | solution.py:96
  111.5 1.1 broadcast_in_dim.216
  112.6 4.5 %all-to-all-start.4 = ((f32[8,16,2048]{2,1,0:T(8,128)}), f32[8,16,2048]{2,1,0:T(8,128)S(1)}, u32[]{:S(2)}, u32[]{:S(2)}) async-start(f32[8,16,2048]{2,1,0:T(8,128)} %bitcast.24), calls=%async_computation.4 | async-start | bytes 2097152 | tf_op jit(solution)/shard_map/all_to_all | solution.py:237
  117.1 0.8 dynamic-slice.3
  117.9 14.5 %all-to-all-done.4 = f32[8,16,2048]{2,1,0:T(8,128)S(1)} async-done(((f32[8,16,2048]{2,1,0:T(8,128)}), f32[8,16,2048]{2,1,0:T(8,128)S(1)}, u32[]{:S(2)}, u32[]{:S(2)}) %all-to-all-start.4) | async-done | bytes 1048608 | tf_op jit(solution)/shard_map/all_to_all | solution.py:237
  133.3 38.0 %all_to_all.52 = f32[64,1,2048]{2,1,0:T(1,128)S(1)} all-to-all(f32[64,1,2048]{2,1,0:T(1,128)S(1)} %bitcast.91), channel_id=1, replica_groups=mesh['guide'=2,'seq'=64,'tp'=4] {'seq'}, dimensions={0} | all-to-all | bytes 1048576 | tf_op jit(solution)/shard_map/all_to_all | solution.py:49
  171.9 37.2 %all_to_all.53 = f32[64,1,2048]{2,1,0:T(1,128)S(1)} all-to-all(f32[64,1,2048]{2,1,0:T(1,128)S(1)} %broadcast_in_dim.217), channel_id=1, replica_groups=mesh['guide'=2,'seq'=64,'tp'=4] {'seq'}, dimensions={0} | all-to-all | bytes 1048576 | tf_op jit(solution)/shard_map/all_to_all | solution.py:51
  209.2 1.0 reshape.564
  (120 shorter events, 11.2 us)
Async XLA Ops:
  0.0 111.1 %copy-start = (bf16[320,2048]{1,0:T(8,128)(2,1)S(1)}, bf16[320,2048]{1,0:T(8,128)(2,1)}, u32[]{:S(2)}) copy-start(bf16[320,2048]{1,0:T(8,128)(2,1)} %param.19) | copy-start | bytes 3932164
  0.0 6.1 %copy-start.5 = (bf16[32,320]{1,0:T(8,128)(2,1)S(1)}, bf16[32,320]{1,0:T(8,128)(2,1)}, u32[]{:S(2)}) copy-start(bf16[32,320]{1,0:T(8,128)(2,1)} %param.17) | copy-start | bytes 61444
  3.8 22.4 %copy-start.4 = (s32[1,32,128]{2,1,0:T(8,128)S(1)}, s32[1,32,128]{2,1,0:T(8,128)}, u32[]{:S(2)}) copy-start(s32[1,32,128]{2,1,0:T(8,128)} %param.23) | copy-start | bytes 49156
  7.3 35.5 %all-to-all-start = ((f32[64,1,544]{2,1,0:T(1,128)}), f32[64,1,544]{2,1,0:T(1,128)S(1)}, u32[]{:S(2)}, u32[]{:S(2)}) async-start(f32[64,1,544]{2,1,0:T(1,128)} %copy.176), calls=%async_computation | async-start | bytes 327680 | tf_op jit(solution)/shard_map/all_to_all | solution.py:148
  29.3 0.8 copy-start.1
  29.9 20.8 %copy-start.7 = (f32[64]{0:T(128)S(1)}, f32[64]{0:T(128)}, u32[]{:S(2)}) copy-start(f32[64]{0:T(128)} %param.16) | copy-start | bytes 772
  30.1 33.7 %copy-start.6 = (f32[64]{0:T(128)S(1)}, f32[64]{0:T(128)}, u32[]{:S(2)}) copy-start(f32[64]{0:T(128)} %param.15) | copy-start | bytes 772
  43.9 19.5 %all-to-all-start.1 = ((f32[64,1,160]{2,1,0:T(1,128)}), f32[64,1,160]{2,1,0:T(1,128)S(1)}, u32[]{:S(2)}, u32[]{:S(2)}) async-start(f32[64,1,160]{2,1,0:T(1,128)} %copy.177), calls=%async_computation.1 | async-start | bytes 131072 | tf_op jit(solution)/shard_map/all_to_all | solution.py:151
  68.0 19.4 %all-to-all-start.2 = ((f32[64,1,198]{2,1,0:T(1,128)}), f32[64,1,198]{2,1,0:T(1,128)S(1)}, u32[]{:S(2)}, u32[]{:S(2)}) async-start(f32[64,1,198]{2,1,0:T(1,128)} %reshape.616), calls=%async_computation.2 | async-start | bytes 131072 | tf_op jit(solution)/shard_map/all_to_all | solution.py:84
  74.5 36.7 %copy-start.2 = (bf16[1,32,2048]{2,1,0:T(8,128)(2,1)S(1)}, bf16[1,32,2048]{2,1,0:T(8,128)(2,1)}, u32[]{:S(2)}) copy-start(bf16[1,32,2048]{2,1,0:T(8,128)(2,1)} %param.12) | copy-start | bytes 393220
  91.2 19.3 %all-to-all-start.3 = ((f32[64,1,195]{2,1,0:T(1,128)}), f32[64,1,195]{2,1,0:T(1,128)S(1)}, u32[]{:S(2)}, u32[]{:S(2)}) async-start(f32[64,1,195]{2,1,0:T(1,128)} %broadcast_in_dim.213), calls=%async_computation.3 | async-start | bytes 131072 | tf_op jit(solution)/shard_map/all_to_all | solution.py:96
  112.6 19.8 %all-to-all-start.4 = ((f32[8,16,2048]{2,1,0:T(8,128)}), f32[8,16,2048]{2,1,0:T(8,128)S(1)}, u32[]{:S(2)}, u32[]{:S(2)}) async-start(f32[8,16,2048]{2,1,0:T(8,128)} %bitcast.24), calls=%async_computation.4 | async-start | bytes 2097152 | tf_op jit(solution)/shard_map/all_to_all | solution.py:237
  117.1 15.6 %copy-start.3 = (bf16[32,8000]{1,0:T(8,128)(2,1)S(1)}, bf16[32,8000]{1,0:T(8,128)(2,1)}, u32[]{:S(2)}) copy-start(bf16[32,8000]{1,0:T(8,128)(2,1)} %param.20) | copy-start | bytes 1536004

commit v15 on v12

--- a/solution.py
+++ b/solution.py
@@ -230,11 +230,15 @@
     final_rows = norm_rows(residual, final_gain)
     final_part = lax.dynamic_slice_in_dim(final_rows, shard_index * part_width, part_width, 2)
     both = final_part.reshape(guide_count * half_rows, part_width)
-    logit_part = jnp.dot(both, head_weight, preferred_element_type=jnp.float32)
+    seq_count = lax.axis_size("seq")
+    vocab = head_weight.shape[1]
+    vocab_padded = -(-vocab * half_rows // (seq_count * 128)) * seq_count * 128 // half_rows
+    padded_weight = jnp.pad(head_weight, ((0, 0), (0, vocab_padded - vocab)))
+    logit_part = jnp.dot(both, padded_weight, preferred_element_type=jnp.float32)
     conditional_part = logit_part[:half_rows]
     unconditional_part = logit_part[half_rows:]
     guided_part = unconditional_part + GUIDE_WEIGHT * (conditional_part - unconditional_part)
-    return all_reduce(guided_part, "seq")
+    return all_reduce(guided_part, "seq")[:, :vocab]
 
 
 def solution(mesh):

time: 211 us -> 212 us (level)
  no operation moved by 1% of the time
where the time goes in v15:
time: 212 us
  blocking collectives  75.3 us (36%)
  waiting for transfers between devices  62.8 us (30%)
  starting transfers between devices  42.7 us (20%)
  local copies, waits for them, and re-layouts  17.5 us (8%)
  other arithmetic  9.3 us (4%)
  matrix products  3.52 us (2%)
    all_to_all x1, blocking collectives, all_reduce(): parts = lax.all_to_all(flat.reshape(count, chunk), axis, 0, 0, tiled=True)  38 us
    all_to_all x1, blocking collectives, all_reduce(): lax.all_to_all(jnp.broadcast_to(total, (count, chunk)), axis, 0, 0, tiled...  37.2 us
    all_to_all x1, starting transfers between devices, shards(): summed = jnp.sum(lax.all_to_all(outgoing, 'seq', 0, 0, tiled=True), axis=0)  18.8 us
    all_to_all x1, waiting for transfers between devices, shards(): incoming = lax.all_to_all(outgoing, ('guide', 'tp'), 0, 0, tiled=True)  14.5 us
    all_to_all x1, waiting for transfers between devices, merge_attention(): lax.all_to_all(jnp.broadcast_to(fraction.reshape(1, -1), (count, fraction...  12.9 us
    all_to_all x1, waiting for transfers between devices, shards(): lax.all_to_all(jnp.broadcast_to(query_chunk[None], (seq_count,) + query_c...  12.5 us
    all_to_all x1, waiting for transfers between devices, merge_attention(): parts = lax.all_to_all(spread, axis, 0, 0, tiled=True)  12 us
    all_to_all x1, waiting for transfers between devices, shards(): summed = jnp.sum(lax.all_to_all(outgoing, 'seq', 0, 0, tiled=True), axis=0)  10.9 us
  transfers between devices with their start and end apart: 5, of which 5 were waited for; matrix products, arithmetic and copies ran while one was open for 4% of the time, Pallas kernels for 0%

profile of v15, /device:TPU:6, one launch (start us, length us, event | category | flops | bytes accessed | tf_op | source)
XLA Modules:
  0.0 211.7 jit_solution(11409809843419307101)
XLA Ops:
  0.0 1.0 bitcast_convert_fusion
  1.0 1.0 multiply_reduce_fusion.1
  2.1 0.8 dynamic-slice.2
  2.9 1.0 fusion.74
  4.1 1.8 gather_fusion.1
  6.4 0.8 copy.148
  7.3 18.8 %all-to-all-start = ((f32[64,1,544]{2,1,0:T(1,128)}), f32[64,1,544]{2,1,0:T(1,128)S(1)}, u32[]{:S(2)}, u32[]{:S(2)}) async-start(f32[64,1,544]{2,1,0:T(1,128)} %copy.148), calls=%async_computation | async-start | bytes 327680 | tf_op jit(solution)/shard_map/all_to_all | solution.py:148
  26.2 0.6 compare_reduce_fusion
  27.2 1.7 dynamic-slice_bitcast_fusion.1
  30.3 0.7 gather_fusion
  31.0 0.6 gather_fusion.3
  31.9 10.9 %all-to-all-done = f32[64,1,544]{2,1,0:T(1,128)S(1)} async-done(((f32[64,1,544]{2,1,0:T(1,128)}), f32[64,1,544]{2,1,0:T(1,128)S(1)}, u32[]{:S(2)}, u32[]{:S(2)}) %all-to-all-start) | async-done | bytes 139296 | tf_op jit(solution)/shard_map/all_to_all | solution.py:148
  43.0 0.7 broadcast_in_dim.202
  43.7 6.6 %all-to-all-start.1 = ((f32[64,1,160]{2,1,0:T(1,128)}), f32[64,1,160]{2,1,0:T(1,128)S(1)}, u32[]{:S(2)}, u32[]{:S(2)}) async-start(f32[64,1,160]{2,1,0:T(1,128)} %broadcast_in_dim.202), calls=%async_computation.1 | async-start | bytes 131072 | tf_op jit(solution)/shard_map/all_to_all | solution.py:151
  50.7 12.5 %all-to-all-done.1 = f32[64,1,160]{2,1,0:T(1,128)S(1)} async-done(((f32[64,1,160]{2,1,0:T(1,128)}), f32[64,1,160]{2,1,0:T(1,128)S(1)}, u32[]{:S(2)}, u32[]{:S(2)}) %all-to-all-start.1) | async-done | bytes 40992 | tf_op jit(solution)/shard_map/all_to_all | solution.py:151
  65.0 0.7 fusion.1
  67.0 0.8 reshape.611
  67.8 6.5 %all-to-all-start.2 = ((f32[64,1,198]{2,1,0:T(1,128)}), f32[64,1,198]{2,1,0:T(1,128)S(1)}, u32[]{:S(2)}, u32[]{:S(2)}) async-start(f32[64,1,198]{2,1,0:T(1,128)} %reshape.611), calls=%async_computation.2 | async-start | bytes 131072 | tf_op jit(solution)/shard_map/all_to_all | solution.py:84
  75.2 12.0 %all-to-all-done.2 = f32[64,1,198]{2,1,0:T(1,128)S(1)} async-done(((f32[64,1,198]{2,1,0:T(1,128)}), f32[64,1,198]{2,1,0:T(1,128)S(1)}, u32[]{:S(2)}, u32[]{:S(2)}) %all-to-all-start.2) | async-done | bytes 50720 | tf_op jit(solution)/shard_map/all_to_all | solution.py:84
  87.7 0.8 reduce.14
  90.3 0.7 broadcast_in_dim.216
  91.0 6.4 %all-to-all-start.3 = ((f32[64,1,195]{2,1,0:T(1,128)}), f32[64,1,195]{2,1,0:T(1,128)S(1)}, u32[]{:S(2)}, u32[]{:S(2)}) async-start(f32[64,1,195]{2,1,0:T(1,128)} %broadcast_in_dim.216), calls=%async_computation.3 | async-start | bytes 131072 | tf_op jit(solution)/shard_map/all_to_all | solution.py:96
  97.4 12.9 %all-to-all-done.3 = f32[64,1,195]{2,1,0:T(1,128)S(1)} async-done(((f32[64,1,195]{2,1,0:T(1,128)}), f32[64,1,195]{2,1,0:T(1,128)S(1)}, u32[]{:S(2)}, u32[]{:S(2)}) %all-to-all-start.3) | async-done | bytes 49952 | tf_op jit(solution)/shard_map/all_to_all | solution.py:96
  111.3 1.1 broadcast_in_dim.219
  112.4 4.5 %all-to-all-start.4 = ((f32[8,16,2048]{2,1,0:T(8,128)}), f32[8,16,2048]{2,1,0:T(8,128)S(1)}, u32[]{:S(2)}, u32[]{:S(2)}) async-start(f32[8,16,2048]{2,1,0:T(8,128)} %bitcast.23), calls=%async_computation.4 | async-start | bytes 2097152 | tf_op jit(solution)/shard_map/all_to_all | solution.py:228
  116.9 0.8 dynamic-slice.3
  117.7 14.5 %all-to-all-done.4 = f32[8,16,2048]{2,1,0:T(8,128)S(1)} async-done(((f32[8,16,2048]{2,1,0:T(8,128)}), f32[8,16,2048]{2,1,0:T(8,128)S(1)}, u32[]{:S(2)}, u32[]{:S(2)}) %all-to-all-start.4) | async-done | bytes 1048608 | tf_op jit(solution)/shard_map/all_to_all | solution.py:228
  132.9 0.6 all_to_all.39
  133.5 38.0 %all_to_all.47 = f32[64,1,2048]{2,1,0:T(1,128)S(1)} all-to-all(f32[64,1,2048]{2,1,0:T(1,128)S(1)} %all_to_all.39), channel_id=1, replica_groups=mesh['guide'=2,'seq'=64,'tp'=4] {'seq'}, dimensions={0} | all-to-all | bytes 1048576 | tf_op jit(solution)/shard_map/all_to_all | solution.py:49
  172.1 37.2 %all_to_all.48 = f32[64,1,2048]{2,1,0:T(1,128)S(1)} all-to-all(f32[64,1,2048]{2,1,0:T(1,128)S(1)} %broadcast_in_dim.220), channel_id=1, replica_groups=mesh['guide'=2,'seq'=64,'tp'=4] {'seq'}, dimensions={0} | all-to-all | bytes 1048576 | tf_op jit(solution)/shard_map/all_to_all | solution.py:51
  209.4 1.2 reduce.9
  210.9 0.8 slice.111
  (120 shorter events, 12.1 us)
Async XLA Ops:
  0.0 111.0 %copy-start = (bf16[320,2048]{1,0:T(8,128)(2,1)S(1)}, bf16[320,2048]{1,0:T(8,128)(2,1)}, u32[]{:S(2)}) copy-start(bf16[320,2048]{1,0:T(8,128)(2,1)} %param.19) | copy-start | bytes 3932164
  0.0 6.1 %copy-start.5 = (bf16[32,320]{1,0:T(8,128)(2,1)S(1)}, bf16[32,320]{1,0:T(8,128)(2,1)}, u32[]{:S(2)}) copy-start(bf16[32,320]{1,0:T(8,128)(2,1)} %param.17) | copy-start | bytes 61444
  3.8 22.4 %copy-start.4 = (s32[1,32,128]{2,1,0:T(8,128)S(1)}, s32[1,32,128]{2,1,0:T(8,128)}, u32[]{:S(2)}) copy-start(s32[1,32,128]{2,1,0:T(8,128)} %param.23) | copy-start | bytes 49156
  7.3 35.5 %all-to-all-start = ((f32[64,1,544]{2,1,0:T(1,128)}), f32[64,1,544]{2,1,0:T(1,128)S(1)}, u32[]{:S(2)}, u32[]{:S(2)}) async-start(f32[64,1,544]{2,1,0:T(1,128)} %copy.148), calls=%async_computation | async-start | bytes 327680 | tf_op jit(solution)/shard_map/all_to_all | solution.py:148
  29.3 0.8 copy-start.1
  29.7 20.8 %copy-start.7 = (f32[64]{0:T(128)S(1)}, f32[64]{0:T(128)}, u32[]{:S(2)}) copy-start(f32[64]{0:T(128)} %param.16) | copy-start | bytes 772
  29.9 33.7 %copy-start.6 = (f32[64]{0:T(128)S(1)}, f32[64]{0:T(128)}, u32[]{:S(2)}) copy-start(f32[64]{0:T(128)} %param.15) | copy-start | bytes 772
  43.7 19.5 %all-to-all-start.1 = ((f32[64,1,160]{2,1,0:T(1,128)}), f32[64,1,160]{2,1,0:T(1,128)S(1)}, u32[]{:S(2)}, u32[]{:S(2)}) async-start(f32[64,1,160]{2,1,0:T(1,128)} %broadcast_in_dim.202), calls=%async_computation.1 | async-start | bytes 131072 | tf_op jit(solution)/shard_map/all_to_all | solution.py:151
  67.8 19.4 %all-to-all-start.2 = ((f32[64,1,198]{2,1,0:T(1,128)}), f32[64,1,198]{2,1,0:T(1,128)S(1)}, u32[]{:S(2)}, u32[]{:S(2)}) async-start(f32[64,1,198]{2,1,0:T(1,128)} %reshape.611), calls=%async_computation.2 | async-start | bytes 131072 | tf_op jit(solution)/shard_map/all_to_all | solution.py:84
  74.3 36.7 %copy-start.2 = (bf16[1,32,2048]{2,1,0:T(8,128)(2,1)S(1)}, bf16[1,32,2048]{2,1,0:T(8,128)(2,1)}, u32[]{:S(2)}) copy-start(bf16[1,32,2048]{2,1,0:T(8,128)(2,1)} %param.12) | copy-start | bytes 393220
  91.0 19.3 %all-to-all-start.3 = ((f32[64,1,195]{2,1,0:T(1,128)}), f32[64,1,195]{2,1,0:T(1,128)S(1)}, u32[]{:S(2)}, u32[]{:S(2)}) async-start(f32[64,1,195]{2,1,0:T(1,128)} %broadcast_in_dim.216), calls=%async_computation.3 | async-start | bytes 131072 | tf_op jit(solution)/shard_map/all_to_all | solution.py:96
  112.4 19.8 %all-to-all-start.4 = ((f32[8,16,2048]{2,1,0:T(8,128)}), f32[8,16,2048]{2,1,0:T(8,128)S(1)}, u32[]{:S(2)}, u32[]{:S(2)}) async-start(f32[8,16,2048]{2,1,0:T(8,128)} %bitcast.23), calls=%async_computation.4 | async-start | bytes 2097152 | tf_op jit(solution)/shard_map/all_to_all | solution.py:228
  116.9 15.6 %copy-start.3 = (bf16[32,8000]{1,0:T(8,128)(2,1)S(1)}, bf16[32,8000]{1,0:T(8,128)(2,1)}, u32[]{:S(2)}) copy-start(bf16[32,8000]{1,0:T(8,128)(2,1)} %param.20) | copy-start | bytes 1536004

commit v16 on v12

--- a/solution.py
+++ b/solution.py
@@ -44,7 +44,6 @@
     count = lax.axis_size(axis)
     flat = value.reshape(-1)
     chunk = -(-flat.size // count)
-    chunk = -(-chunk // 128) * 128
     flat = jnp.pad(flat, (0, count * chunk - flat.size))
     parts = lax.all_to_all(flat.reshape(count, chunk), axis, 0, 0, tiled=True)
     total = jnp.sum(parts, axis=0, keepdims=True)

time: 211 us -> 212 us (level)
  no operation moved by 1% of the time
where the time goes in v16:
time: 212 us
  blocking collectives  75.3 us (36%)
  waiting for transfers between devices  62.8 us (30%)
  starting transfers between devices  42.7 us (20%)
  local copies, waits for them, and re-layouts  17.7 us (8%)
  other arithmetic  9.34 us (4%)
  matrix products  3.52 us (2%)
    all_to_all x1, blocking collectives, all_reduce(): parts = lax.all_to_all(flat.reshape(count, chunk), axis, 0, 0, tiled=True)  38 us
    all_to_all x1, blocking collectives, all_reduce(): lax.all_to_all(jnp.broadcast_to(total, (count, chunk)), axis, 0, 0, tiled...  37.2 us
    all_to_all x1, starting transfers between devices, shards(): summed = jnp.sum(lax.all_to_all(outgoing, 'seq', 0, 0, tiled=True), axis=0)  18.8 us
    all_to_all x1, waiting for transfers between devices, shards(): incoming = lax.all_to_all(outgoing, ('guide', 'tp'), 0, 0, tiled=True)  14.5 us
    all_to_all x1, waiting for transfers between devices, merge_attention(): lax.all_to_all(jnp.broadcast_to(fraction.reshape(1, -1), (count, fraction...  12.9 us
    all_to_all x1, waiting for transfers between devices, shards(): lax.all_to_all(jnp.broadcast_to(query_chunk[None], (seq_count,) + query_c...  12.5 us
    all_to_all x1, waiting for transfers between devices, merge_attention(): parts = lax.all_to_all(spread, axis, 0, 0, tiled=True)  12 us
    all_to_all x1, waiting for transfers between devices, shards(): summed = jnp.sum(lax.all_to_all(outgoing, 'seq', 0, 0, tiled=True), axis=0)  10.9 us
  transfers between devices with their start and end apart: 5, of which 5 were waited for; matrix products, arithmetic and copies ran while one was open for 4% of the time, Pallas kernels for 0%

profile of v16, /device:TPU:6, one launch (start us, length us, event | category | flops | bytes accessed | tf_op | source)
XLA Modules:
  0.0 211.9 jit_solution(7625206014307760055)
XLA Ops:
  0.0 1.0 bitcast_convert_fusion
  1.0 1.0 multiply_reduce_fusion.1
  2.1 0.8 dynamic-slice.2
  2.9 1.0 fusion.71
  4.1 1.8 gather_fusion.1
  6.4 0.8 copy.148
  7.3 18.8 %all-to-all-start = ((f32[64,1,544]{2,1,0:T(1,128)}), f32[64,1,544]{2,1,0:T(1,128)S(1)}, u32[]{:S(2)}, u32[]{:S(2)}) async-start(f32[64,1,544]{2,1,0:T(1,128)} %copy.148), calls=%async_computation | async-start | bytes 327680 | tf_op jit(solution)/shard_map/all_to_all | solution.py:147
  26.2 0.6 compare_reduce_fusion
  27.2 1.7 dynamic-slice_bitcast_fusion.1
  30.3 0.7 gather_fusion
  31.0 0.6 gather_fusion.3
  31.9 10.9 %all-to-all-done = f32[64,1,544]{2,1,0:T(1,128)S(1)} async-done(((f32[64,1,544]{2,1,0:T(1,128)}), f32[64,1,544]{2,1,0:T(1,128)S(1)}, u32[]{:S(2)}, u32[]{:S(2)}) %all-to-all-start) | async-done | bytes 139296 | tf_op jit(solution)/shard_map/all_to_all | solution.py:147
  43.0 0.7 broadcast_in_dim.202
  43.7 6.6 %all-to-all-start.1 = ((f32[64,1,160]{2,1,0:T(1,128)}), f32[64,1,160]{2,1,0:T(1,128)S(1)}, u32[]{:S(2)}, u32[]{:S(2)}) async-start(f32[64,1,160]{2,1,0:T(1,128)} %broadcast_in_dim.202), calls=%async_computation.1 | async-start | bytes 131072 | tf_op jit(solution)/shard_map/all_to_all | solution.py:150
  50.7 12.5 %all-to-all-done.1 = f32[64,1,160]{2,1,0:T(1,128)S(1)} async-done(((f32[64,1,160]{2,1,0:T(1,128)}), f32[64,1,160]{2,1,0:T(1,128)S(1)}, u32[]{:S(2)}, u32[]{:S(2)}) %all-to-all-start.1) | async-done | bytes 40992 | tf_op jit(solution)/shard_map/all_to_all | solution.py:150
  65.0 0.7 fusion.1
  67.0 0.8 reshape.611
  67.8 6.5 %all-to-all-start.2 = ((f32[64,1,198]{2,1,0:T(1,128)}), f32[64,1,198]{2,1,0:T(1,128)S(1)}, u32[]{:S(2)}, u32[]{:S(2)}) async-start(f32[64,1,198]{2,1,0:T(1,128)} %reshape.611), calls=%async_computation.2 | async-start | bytes 131072 | tf_op jit(solution)/shard_map/all_to_all | solution.py:83
  75.2 12.0 %all-to-all-done.2 = f32[64,1,198]{2,1,0:T(1,128)S(1)} async-done(((f32[64,1,198]{2,1,0:T(1,128)}), f32[64,1,198]{2,1,0:T(1,128)S(1)}, u32[]{:S(2)}, u32[]{:S(2)}) %all-to-all-start.2) | async-done | bytes 50720 | tf_op jit(solution)/shard_map/all_to_all | solution.py:83
  87.7 0.8 reduce.14
  90.3 0.7 broadcast_in_dim.216
  91.0 6.4 %all-to-all-start.3 = ((f32[64,1,195]{2,1,0:T(1,128)}), f32[64,1,195]{2,1,0:T(1,128)S(1)}, u32[]{:S(2)}, u32[]{:S(2)}) async-start(f32[64,1,195]{2,1,0:T(1,128)} %broadcast_in_dim.216), calls=%async_computation.3 | async-start | bytes 131072 | tf_op jit(solution)/shard_map/all_to_all | solution.py:95
  97.4 12.9 %all-to-all-done.3 = f32[64,1,195]{2,1,0:T(1,128)S(1)} async-done(((f32[64,1,195]{2,1,0:T(1,128)}), f32[64,1,195]{2,1,0:T(1,128)S(1)}, u32[]{:S(2)}, u32[]{:S(2)}) %all-to-all-start.3) | async-done | bytes 49952 | tf_op jit(solution)/shard_map/all_to_all | solution.py:95
  111.3 1.1 broadcast_in_dim.219
  112.4 4.5 %all-to-all-start.4 = ((f32[8,16,2048]{2,1,0:T(8,128)}), f32[8,16,2048]{2,1,0:T(8,128)S(1)}, u32[]{:S(2)}, u32[]{:S(2)}) async-start(f32[8,16,2048]{2,1,0:T(8,128)} %bitcast.23), calls=%async_computation.4 | async-start | bytes 2097152 | tf_op jit(solution)/shard_map/all_to_all | solution.py:227
  116.9 0.8 dynamic-slice.3
  117.7 14.5 %all-to-all-done.4 = f32[8,16,2048]{2,1,0:T(8,128)S(1)} async-done(((f32[8,16,2048]{2,1,0:T(8,128)}), f32[8,16,2048]{2,1,0:T(8,128)S(1)}, u32[]{:S(2)}, u32[]{:S(2)}) %all-to-all-start.4) | async-done | bytes 1048608 | tf_op jit(solution)/shard_map/all_to_all | solution.py:227
  132.9 0.7 all_to_all.39
  133.6 38.0 %all_to_all.47 = f32[64,1,2000]{2,1,0:T(1,128)S(1)} all-to-all(f32[64,1,2000]{2,1,0:T(1,128)S(1)} %all_to_all.39), channel_id=1, replica_groups=mesh['guide'=2,'seq'=64,'tp'=4] {'seq'}, dimensions={0} | all-to-all | bytes 1024000 | tf_op jit(solution)/shard_map/all_to_all | solution.py:48
  172.3 37.2 %all_to_all.48 = f32[64,1,2000]{2,1,0:T(1,128)S(1)} all-to-all(f32[64,1,2000]{2,1,0:T(1,128)S(1)} %broadcast_in_dim.220), channel_id=1, replica_groups=mesh['guide'=2,'seq'=64,'tp'=4] {'seq'}, dimensions={0} | all-to-all | bytes 1024000 | tf_op jit(solution)/shard_map/all_to_all | solution.py:50
  209.5 1.2 reduce.9
  210.8 1.1 reshape_reshape.7
  (119 shorter events, 11.9 us)
Async XLA Ops:
  0.0 111.0 %copy-start = (bf16[320,2048]{1,0:T(8,128)(2,1)S(1)}, bf16[320,2048]{1,0:T(8,128)(2,1)}, u32[]{:S(2)}) copy-start(bf16[320,2048]{1,0:T(8,128)(2,1)} %param.19) | copy-start | bytes 3932164
  0.0 6.1 %copy-start.5 = (bf16[32,320]{1,0:T(8,128)(2,1)S(1)}, bf16[32,320]{1,0:T(8,128)(2,1)}, u32[]{:S(2)}) copy-start(bf16[32,320]{1,0:T(8,128)(2,1)} %param.17) | copy-start | bytes 61444
  3.8 22.4 %copy-start.4 = (s32[1,32,128]{2,1,0:T(8,128)S(1)}, s32[1,32,128]{2,1,0:T(8,128)}, u32[]{:S(2)}) copy-start(s32[1,32,128]{2,1,0:T(8,128)} %param.23) | copy-start | bytes 49156
  7.3 35.5 %all-to-all-start = ((f32[64,1,544]{2,1,0:T(1,128)}), f32[64,1,544]{2,1,0:T(1,128)S(1)}, u32[]{:S(2)}, u32[]{:S(2)}) async-start(f32[64,1,544]{2,1,0:T(1,128)} %copy.148), calls=%async_computation | async-start | bytes 327680 | tf_op jit(solution)/shard_map/all_to_all | solution.py:147
  29.3 0.8 copy-start.1
  29.7 20.8 %copy-start.7 = (f32[64]{0:T(128)S(1)}, f32[64]{0:T(128)}, u32[]{:S(2)}) copy-start(f32[64]{0:T(128)} %param.16) | copy-start | bytes 772
  29.9 33.7 %copy-start.6 = (f32[64]{0:T(128)S(1)}, f32[64]{0:T(128)}, u32[]{:S(2)}) copy-start(f32[64]{0:T(128)} %param.15) | copy-start | bytes 772
  43.7 19.5 %all-to-all-start.1 = ((f32[64,1,160]{2,1,0:T(1,128)}), f32[64,1,160]{2,1,0:T(1,128)S(1)}, u32[]{:S(2)}, u32[]{:S(2)}) async-start(f32[64,1,160]{2,1,0:T(1,128)} %broadcast_in_dim.202), calls=%async_computation.1 | async-start | bytes 131072 | tf_op jit(solution)/shard_map/all_to_all | solution.py:150
  67.8 19.4 %all-to-all-start.2 = ((f32[64,1,198]{2,1,0:T(1,128)}), f32[64,1,198]{2,1,0:T(1,128)S(1)}, u32[]{:S(2)}, u32[]{:S(2)}) async-start(f32[64,1,198]{2,1,0:T(1,128)} %reshape.611), calls=%async_computation.2 | async-start | bytes 131072 | tf_op jit(solution)/shard_map/all_to_all | solution.py:83
  74.3 36.7 %copy-start.2 = (bf16[1,32,2048]{2,1,0:T(8,128)(2,1)S(1)}, bf16[1,32,2048]{2,1,0:T(8,128)(2,1)}, u32[]{:S(2)}) copy-start(bf16[1,32,2048]{2,1,0:T(8,128)(2,1)} %param.12) | copy-start | bytes 393220
  91.0 19.3 %all-to-all-start.3 = ((f32[64,1,195]{2,1,0:T(1,128)}), f32[64,1,195]{2,1,0:T(1,128)S(1)}, u32[]{:S(2)}, u32[]{:S(2)}) async-start(f32[64,1,195]{2,1,0:T(1,128)} %broadcast_in_dim.216), calls=%async_computation.3 | async-start | bytes 131072 | tf_op jit(solution)/shard_map/all_to_all | solution.py:95
  112.4 19.8 %all-to-all-start.4 = ((f32[8,16,2048]{2,1,0:T(8,128)}), f32[8,16,2048]{2,1,0:T(8,128)S(1)}, u32[]{:S(2)}, u32[]{:S(2)}) async-start(f32[8,16,2048]{2,1,0:T(8,128)} %bitcast.23), calls=%async_computation.4 | async-start | bytes 2097152 | tf_op jit(solution)/shard_map/all_to_all | solution.py:227
  116.9 15.6 %copy-start.3 = (bf16[32,8000]{1,0:T(8,128)(2,1)S(1)}, bf16[32,8000]{1,0:T(8,128)(2,1)}, u32[]{:S(2)}) copy-start(bf16[32,8000]{1,0:T(8,128)(2,1)} %param.20) | copy-start | bytes 1536004
